TPU v7x, 256 devices: a whole 4x4x8 slice. The times are simulated.
256 devices in a mesh: kv: 2 (over core), pg: 128 (over x, z, y).
Axes of the slice: x: 4, y: 4, z: 8, core: 2. Of those that a mesh axis runs over, the one named last changes fastest.
Arguments:
- layer_hidden_input: bfloat16 [16384, 2560], P('pg'), may hold values from -6 to 6
- norm_scale_vector: float32 [2560], replicated, may hold values from 0.1 to 1.9
- expert_choice_index: int32 [16384, 6], P('pg'), may hold values from 0 to 63, all different within a row; in each aligned block of 128 rows (0 to 127, 128 to 255, ...) at most 16 rows name the same one
- expert_choice_weight: float32 [16384, 6], P('pg'), may hold values from 0.05 to 0.35
- request_of_token: int32 [16384], P('pg'), may hold values from 0 to 255, never falling along the last dimension, each value on 1 to 512 neighbouring positions
- adapter_of_request: int32 [256], replicated, may hold values from 0 to 63
- adapter_of_slot: int32 [128], replicated, may hold values from 0 to 63, as said below
- expert_gate_up_weight: bfloat16 [128, 2560, 2, 768], P('pg', None, None, 'kv'), may hold values from -0.125 to 0.125
- expert_down_weight: bfloat16 [128, 768, 2560], P('pg', 'kv'), may hold values from -0.15625 to 0.15625
- adapter_down_weight: bfloat16 [128, 2560, 8], P('pg'), may hold values from -0.125 to 0.125
- adapter_up_weight: bfloat16 [128, 8, 2560], P('pg', None, 'kv'), may hold values from -0.75 to 0.75
Outputs:
- mixed: bfloat16 [16384, 2560], P('pg', 'kv')
Inputs may be any that keep to these rules, and one draw needn't show every extreme that they name: `expert_choice_index`: each row names 6 different experts. The 128 rows of one index of pg name one expert at most 16 times; some expert is named exactly 16 times by the rows of some index. `adapter_of_slot`: every adapter is held by exactly two slots. `request_of_token`: tokens of one request stand in a row; request numbers never fall along the tokens.
All inputs are finite; a program needn't handle non-finite values.
Results may differ from a plain program's by a relative error of at most 0.013.
Values may be sent and summed in bfloat16 or wider, within the bound.
No kernel may reach another device: no remote copies, remote signals or barrier semaphores. Data moves between devices by JAX's collectives and lax.ppermute only.
A program may use at most 128 MiB of HBM per device.

v0:
```python
import jax
import jax.numpy as jnp
from jax import lax
from jax.sharding import PartitionSpec as P


def normalize(states, gain_vector):
    values = states.astype(jnp.float32)
    inverse_rms = lax.rsqrt(jnp.mean(values * values, axis=-1, keepdims=True) + 1e-06)
    return (values * inverse_rms * gain_vector).astype(jnp.bfloat16)


def expert_half(expert_rows, expert_gate_up_weight, expert_down_weight):
    gate_up = jnp.einsum(
        "rd,dgf->rgf", expert_rows, expert_gate_up_weight[0], preferred_element_type=jnp.float32
    )
    hidden = (jax.nn.silu(gate_up[:, 0]) * gate_up[:, 1]).astype(jnp.bfloat16)
    local_units = hidden.shape[1]
    piece_count = 2 // lax.axis_size("kv")
    piece_units = local_units // piece_count
    quarter = jnp.dot(
        hidden, expert_down_weight[0, 0:piece_units], preferred_element_type=jnp.float32
    )
    summed = quarter.astype(jnp.bfloat16).astype(jnp.float32)
    return lax.psum_scatter(summed.astype(jnp.bfloat16), "kv", scatter_dimension=1, tiled=True)


def rank_in_expert(flat_ids, expert_count):
    onehot = (flat_ids[:, None] == jnp.arange(expert_count, dtype=jnp.int32)[None, :]).astype(
        jnp.bfloat16
    )
    entries = flat_ids.shape[0]
    lower = (
        jnp.arange(entries, dtype=jnp.int32)[:, None]
        >= jnp.arange(entries, dtype=jnp.int32)[None, :]
    ).astype(jnp.bfloat16)
    running = jnp.dot(lower, onehot, preferred_element_type=jnp.float32)
    return (jnp.sum(running * onehot.astype(jnp.float32), axis=1) - 1.0).astype(jnp.int32)


def place_rows(slot_table, slot_total, normalized_input):
    slot_ids = jnp.arange(slot_total, dtype=jnp.int32)
    hits = jnp.zeros((slot_total, slot_table[0].shape[0]), jnp.float32)
    for table in slot_table:
        hits = hits + jnp.sum(
            (table[None, :, :] == slot_ids[:, None, None]).astype(jnp.float32), axis=2
        )
    placed = jnp.dot(
        hits.astype(jnp.bfloat16), normalized_input, preferred_element_type=jnp.float32
    )
    return placed.astype(jnp.bfloat16)


def collect_rows(slot_table, slot_total, weights, gathered):
    slot_ids = jnp.arange(slot_total, dtype=jnp.int32)
    combine = jnp.zeros((weights.shape[0], slot_total), jnp.float32)
    for table in slot_table:
        combine = combine + jnp.sum(
            jnp.where(table[:, :, None] == slot_ids[None, None, :], weights[:, :, None], 0.0),
            axis=1,
        )
    upper_part = combine.astype(jnp.bfloat16)
    lower_part = (combine - upper_part.astype(jnp.float32)).astype(jnp.bfloat16)
    return jnp.dot(upper_part, gathered, preferred_element_type=jnp.float32) + jnp.dot(
        lower_part, gathered, preferred_element_type=jnp.float32
    )


def on_device(
    layer_hidden_input,
    norm_scale_vector,
    expert_choice_index,
    expert_choice_weight,
    request_of_token,
    adapter_of_request,
    adapter_of_slot,
    expert_gate_up_weight,
    expert_down_weight,
    adapter_down_weight,
    adapter_up_weight,
):
    tok_rows, model_width = layer_hidden_input.shape
    top_count = expert_choice_index.shape[1]
    pg_size = lax.axis_size("pg")
    expert_count = pg_size // 2
    slot_cap = 4 * tok_rows * top_count // (3 * expert_count)
    half_width = model_width // lax.axis_size("kv")
    normalized_input = normalize(layer_hidden_input, norm_scale_vector)
    flat_ids = expert_choice_index.reshape(-1)
    slot_rank = rank_in_expert(flat_ids, expert_count)
    rank_table = slot_rank.reshape(tok_rows, top_count)
    first_slot = 2 * expert_choice_index * slot_cap + rank_table
    second_slot = first_slot + slot_cap
    slot_total = pg_size * slot_cap
    outbox = place_rows((first_slot, second_slot), slot_total, normalized_input).reshape(
        pg_size, slot_cap, model_width
    )
    inbox_rows = lax.all_to_all(outbox, "pg", split_axis=0, concat_axis=0, tiled=True)
    half_out = expert_half(
        inbox_rows.reshape(pg_size * slot_cap, model_width),
        expert_gate_up_weight,
        expert_down_weight,
    )
    results = lax.all_to_all(
        half_out.reshape(pg_size, slot_cap, half_width),
        "pg",
        split_axis=0,
        concat_axis=0,
        tiled=True,
    )
    moe_sum = collect_rows(
        (first_slot, second_slot),
        slot_total,
        expert_choice_weight,
        results.reshape(slot_total, half_width),
    )
    request_count = adapter_of_request.shape[0]
    owner_table = request_of_token[:, None] == jnp.arange(request_count, dtype=jnp.int32)[None, :]
    token_adapter = jnp.sum(jnp.where(owner_table, adapter_of_request[None, :], 0), axis=1)
    down_projected = lax.all_gather(adapter_down_weight, "pg", axis=0, tiled=True)
    up_projected = lax.all_gather(adapter_up_weight, "pg", axis=0, tiled=True)
    slot_count = down_projected.shape[0]
    rank_projected = jnp.einsum(
        "ic,ycz->iyz", normalized_input, down_projected, preferred_element_type=jnp.float32
    )
    matched = adapter_of_slot[None, :, None] == token_adapter[:, None, None]
    rank_projected = jnp.where(matched, rank_projected, 0.0).astype(jnp.bfloat16)
    flat_low = rank_projected.reshape(tok_rows, slot_count * down_projected.shape[2])
    flat_up = up_projected.reshape(slot_count * up_projected.shape[1], up_projected.shape[2])
    adapter_total_output = jnp.dot(flat_low, flat_up, preferred_element_type=jnp.float32)
    return (moe_sum + adapter_total_output).astype(jnp.bfloat16)


def solution(mesh):
    placed = (
        P("pg", None),
        P(),
        P("pg", None),
        P("pg", None),
        P("pg"),
        P(),
        P(),
        P("pg", None, None, "kv"),
        P("pg", "kv", None),
        P("pg", None, None),
        P("pg", None, "kv"),
    )
    return jax.shard_map(
        on_device, mesh=mesh, in_specs=placed, out_specs=P("pg", "kv"), check_vma=False
    )
```

profile of v0, /device:TPU:2, one launch (start us, length us, event | category | flops | bytes accessed | tf_op | source)
XLA Modules:
  0.0 561.2 jit_solution(11370878380709900751)
XLA Ops:
  7.4 0.0 copy-start
  7.4 0.0 copy-start.2
  7.4 0.0 copy-start.4
  7.4 0.0 reduce-scatter.2.cloned.1.call-start
  7.4 0.9 copy.42
  8.3 0.1 eq.98
  8.5 0.4 fusion.26
  8.9 0.1 convert_element_type.61
  9.0 0.1 copy.43
  9.1 0.7 broadcast_add_fusion
  9.8 1.3 fusion.16
  11.1 1.7 convert_reduce_fusion
  12.8 0.0 copy-done.2
  12.8 0.0 copy-done.4
  12.8 3.3 convolution_convert_fusion.1
  16.1 0.0 copy-start.9
  16.1 247.3 %all_to_all.10 = bf16[128,16,2560]{2,1,0:T(8,128)(2,1)} all-to-all(bf16[128,16,2560]{2,1,0:T(8,128)(2,1)S(1)} %bitcast.23), channel_id=1, replica_groups=mesh['kv'=2,'pg'=128] {'pg'}, dimensions={0} | all-to-all | bytes 20971520 | tf_op jit(solution)/shard_map/all_to_all | solution.py:98
  263.4 0.0 copy-done.9
  263.4 11.0 %fusion.2 = f32[2048,2,384]{2,0,1:T(8,128)S(1)} fusion(bf16[2048,2560,1]{1,0,2:T(8,128)(2,1)} %bitcast.24, bf16[2560,2,384]{2,1,0:T(2,128)(2,1)S(1)} %bitcast.26), kind=kOutput, calls=%fused_computation.12 | convolution fusion | flops 8053063680 | bytes 20709376 | tf_op jit(solution)/shard_map/rd,dgf->rgf/dot_general | solution.py:14
  274.3 0.0 copy-done
  274.4 8.2 %convolution_convert_fusion = bf16[2048,2560]{1,0:T(8,128)(2,1)} fusion(bf16[1,384,2560]{2,1,0:T(8,128)(2,1)S(1)} %copy-done, f32[2048,2,384]{2,0,1:T(8,128)S(1)} %fusion.2), kind=kOutput, calls=%fused_computation | convolution fusion | flops 4036493312 | bytes 18743296 | tf_op jit(solution)/shard_map/dot_general | solution.py:21
  282.6 0.0 reduce-scatter.2.cloned.1.call-update
  282.6 0.0 all-gather.5.cloned.1.call-start
  282.6 0.5 all-gather.5.cloned.1.call-update
  283.2 0.0 all-gather.3.cloned.1.call-start
  283.2 0.5 all-gather.3.cloned.1.call-update
  283.8 18.6 %reduce-scatter.2.cloned.1.call-done = bf16[2048,1280]{1,0:T(8,128)(2,1)} async-done(((bf16[2048,2560]{1,0:T(8,128)(2,1)}), bf16[2048,1280]{1,0:T(8,128)(2,1)}) %reduce-scatter.2.cloned.1.call-update) | async-done | bytes 5242896 | tf_op jit(solution)/shard_map/reduce_scatter | solution.py:25
  302.4 0.0 copy-start.6
  302.4 0.0 copy-start.8
  302.4 0.0 copy-start.7
  302.4 0.0 copy-start.5
  302.4 14.4 %all-to-all-start.1 = ((bf16[128,16,1280]{2,1,0:T(8,128)(2,1)}), bf16[128,16,1280]{2,1,0:T(8,128)(2,1)}, u32[]{:S(2)}, u32[]{:S(2)}) async-start(bf16[128,16,1280]{2,1,0:T(8,128)(2,1)} %bitcast.25), calls=%async_computation.2 | async-start | bytes 10485760 | tf_op jit(solution)/shard_map/all_to_all | solution.py:104
  316.8 0.0 copy-done.6
  316.8 0.0 copy-done.8
  316.8 0.2 select_reduce_fusion.2
  317.0 0.0 copy-done.7
  317.0 0.1 broadcast_compare_fusion
  317.1 0.0 copy-done.5
  317.1 3.5 select_reduce_fusion
  320.6 94.0 %all-gather.5.cloned.1.call-done = bf16[128,8,1280]{2,1,0:T(8,128)(2,1)} async-done(((bf16[1,8,1280]{2,1,0:T(8,128)(2,1)}), bf16[128,8,1280]{2,1,0:T(8,128)(2,1)}) %all-gather.5.cloned.1.call-update) | async-done | bytes 2621456 | tf_op jit(solution)/shard_map/all_gather | solution.py:121
  414.6 122.8 %all-gather.3.cloned.1.call-done = bf16[128,2560,8]{1,2,0:T(8,128)(2,1)} async-done(((bf16[1,2560,8]{1,2,0:T(8,128)(2,1)}), bf16[128,2560,8]{1,2,0:T(8,128)(2,1)}) %all-gather.3.cloned.1.call-update) | async-done | bytes 5242896 | tf_op jit(solution)/shard_map/all_gather | solution.py:120
  537.5 8.2 %fusion.8 = f32[128,1280]{1,0:T(8,128)} fusion(bf16[128,8,1280]{2,1,0:T(8,128)(2,1)} %all-gather.5.cloned.1.call-done, bf16[128,2560,8]{1,2,0:T(8,128)(2,1)} %all-gather.3.cloned.1.call-done, pred[128,128]{1,0:T(8,128)(4,1)S(1)} %broadcast_compare_fusion, bf16[128,2560]{1,0:T(8,128)(2,1)} %param.11, f32[2560]{0:T(1024)S(1)} %copy-done.4, ...), kind=kOutput, calls=%fused_computation.20 | convolution fusion | flops 1008205824 | bytes 9202176 | tf_op jit(solution)/shard_map/dot_general | solution.py:130
  545.7 0.0 all-to-all-done.1
  545.7 0.0 copy-start.1
  545.7 3.8 fusion.33
  549.5 0.0 copy-done.1
  549.5 0.0 copy-done.3
  549.5 4.2 fusion.11
  (3 shorter events, 0.0 us)
Async XLA Ops:
  7.4 267.0 %copy-start = (bf16[1,384,2560]{2,1,0:T(8,128)(2,1)S(1)}, bf16[1,384,2560]{2,1,0:T(8,128)(2,1)}, u32[]{:S(2)}) copy-start(bf16[1,384,2560]{2,1,0:T(8,128)(2,1)} %param.19) | copy-start | bytes 5898244
  7.4 5.4 copy-start.2
  7.4 5.4 copy-start.4
  7.4 295.0 %reduce-scatter.2.cloned.1.call-start = ((), (), s32[]{:S(2)}) async-start(), calls=%async_computation.3 | async-start | bytes 15728640 | tf_op jit(solution)/shard_map/reduce_scatter | solution.py:25
  16.1 247.3 %copy-start.9 = (bf16[1,2560,2,384]{3,2,1,0:T(2,128)(2,1)S(1)}, bf16[1,2560,2,384]{3,2,1,0:T(2,128)(2,1)}, u32[]{:S(2)}) copy-start(bf16[1,2560,2,384]{3,2,1,0:T(2,128)(2,1)} %param.18) | copy-start | bytes 11796484
  282.6 132.0 %all-gather.5.cloned.1.call-start = ((), (), s32[]{:S(2)}) async-start(), calls=%async_computation.5 | async-start | bytes 2641920 | tf_op jit(solution)/shard_map/all_gather | solution.py:121
  283.2 254.3 %all-gather.3.cloned.1.call-start = ((), (), s32[]{:S(2)}) async-start(), calls=%async_computation.4 | async-start | bytes 5283840 | tf_op jit(solution)/shard_map/all_gather | solution.py:120
  302.4 14.4 %copy-start.6 = (s32[256]{0:T(256)S(1)}, s32[256]{0:T(256)}, u32[]{:S(2)}) copy-start(s32[256]{0:T(256)} %param.16) | copy-start | bytes 3076
  302.4 14.4 %copy-start.8 = (s32[128]{0:T(128)S(1)}, s32[128]{0:T(128)}, u32[]{:S(2)}) copy-start(s32[128]{0:T(128)} %param.15) | copy-start | bytes 1540
  302.4 14.6 %copy-start.7 = (s32[128]{0:T(128)S(1)}, s32[128]{0:T(128)}, u32[]{:S(2)}) copy-start(s32[128]{0:T(128)} %param.17) | copy-start | bytes 1540
  302.4 14.7 %copy-start.5 = (f32[128,6]{0,1:T(8,128)S(1)}, f32[128,6]{0,1:T(8,128)}, u32[]{:S(2)}) copy-start(f32[128,6]{0,1:T(8,128)} %param.14) | copy-start | bytes 9220
  302.4 243.3 %all-to-all-start.1 = ((bf16[128,16,1280]{2,1,0:T(8,128)(2,1)}), bf16[128,16,1280]{2,1,0:T(8,128)(2,1)}, u32[]{:S(2)}, u32[]{:S(2)}) async-start(bf16[128,16,1280]{2,1,0:T(8,128)(2,1)} %bitcast.25), calls=%async_computation.2 | async-start | bytes 10485760 | tf_op jit(solution)/shard_map/all_to_all | solution.py:104
  545.7 3.8 copy-start.1
  545.7 3.8 copy-start.3
Sparse Core Ops, SparseCore 0:
  282.7 19.6 reduce-scatter.1
Sparse Core Ops, SparseCore 1:
  286.7 127.9 all-gather.4
  418.0 119.4 all-gather.2
where the time goes:
time: 561 us
  blocking collectives  247 us (44%)
  waiting for transfers between devices  237 us (42%)
  matrix products  39 us (7%)
  between operations  15 us (3%)
  starting transfers between devices  14.5 us (3%)
  other arithmetic  7.46 us (1%)
    all_to_all x1, blocking collectives, on_device(): lax.all_to_all(outbox, 'pg', split_axis=0, concat_axis=0, tiled=True)  247 us
    all_gather x1, waiting for transfers between devices, on_device(): lax.all_gather(adapter_down_weight, 'pg', axis=0, tiled=True)  123 us
    all_gather x1, waiting for transfers between devices, on_device(): up_projected = lax.all_gather(adapter_up_weight, 'pg', axis=0, tiled=True)  94 us
    reduce_scatter x1, waiting for transfers between devices, expert_half(): lax.psum_scatter(summed.astype(jnp.bfloat16), 'kv', scatter_dimension=1,...  18.6 us
    all_to_all x1, starting transfers between devices, on_device(): lax.all_to_all(half_out.reshape(pg_size, slot_cap, half_width), 'pg', spl...  14.4 us
  transfers between devices with their start and end apart: 4, of which 3 were waited for; matrix products, arithmetic and copies ran while one was open for 2% of the time, Pallas kernels for 0%

commit v1 on v0

--- a/solution.py
+++ b/solution.py
@@ -85,22 +85,27 @@
     expert_count = pg_size // 2
     slot_cap = 4 * tok_rows * top_count // (3 * expert_count)
     half_width = model_width // lax.axis_size("kv")
+    kv_index = lax.axis_index("kv")
     normalized_input = normalize(layer_hidden_input, norm_scale_vector)
+    own_features = lax.dynamic_slice_in_dim(normalized_input, kv_index * half_width, half_width, axis=1)
+    down_own = lax.dynamic_slice_in_dim(adapter_down_weight[0], kv_index * half_width, half_width, axis=0)
+    rank_half = down_own.shape[1]
+    packed = jnp.concatenate([down_own.T, adapter_up_weight[0]], axis=0)
+    packed_all = lax.all_gather(packed, "pg", axis=0, tiled=False)
     flat_ids = expert_choice_index.reshape(-1)
     slot_rank = rank_in_expert(flat_ids, expert_count)
     rank_table = slot_rank.reshape(tok_rows, top_count)
     first_slot = 2 * expert_choice_index * slot_cap + rank_table
     second_slot = first_slot + slot_cap
     slot_total = pg_size * slot_cap
-    outbox = place_rows((first_slot, second_slot), slot_total, normalized_input).reshape(
-        pg_size, slot_cap, model_width
+    outbox = place_rows((first_slot, second_slot), slot_total, own_features).reshape(
+        pg_size, slot_cap, half_width
     )
-    inbox_rows = lax.all_to_all(outbox, "pg", split_axis=0, concat_axis=0, tiled=True)
-    half_out = expert_half(
-        inbox_rows.reshape(pg_size * slot_cap, model_width),
-        expert_gate_up_weight,
-        expert_down_weight,
+    inbox_half = lax.all_to_all(outbox, "pg", split_axis=0, concat_axis=0, tiled=True)
+    inbox_rows = lax.all_gather(
+        inbox_half.reshape(pg_size * slot_cap, half_width), "kv", axis=1, tiled=True
     )
+    half_out = expert_half(inbox_rows, expert_gate_up_weight, expert_down_weight)
     results = lax.all_to_all(
         half_out.reshape(pg_size, slot_cap, half_width),
         "pg",
@@ -117,17 +122,17 @@
     request_count = adapter_of_request.shape[0]
     owner_table = request_of_token[:, None] == jnp.arange(request_count, dtype=jnp.int32)[None, :]
     token_adapter = jnp.sum(jnp.where(owner_table, adapter_of_request[None, :], 0), axis=1)
-    down_projected = lax.all_gather(adapter_down_weight, "pg", axis=0, tiled=True)
-    up_projected = lax.all_gather(adapter_up_weight, "pg", axis=0, tiled=True)
-    slot_count = down_projected.shape[0]
-    rank_projected = jnp.einsum(
-        "ic,ycz->iyz", normalized_input, down_projected, preferred_element_type=jnp.float32
+    slot_count = packed_all.shape[0]
+    down_all = packed_all[:, 0:rank_half, :].reshape(slot_count * rank_half, half_width)
+    up_all = packed_all[:, rank_half:, :].reshape(slot_count * rank_half, half_width)
+    partial_rank = lax.dot_general(
+        own_features, down_all, (((1,), (1,)), ((), ())), preferred_element_type=jnp.float32
     )
+    rank_projected = lax.psum(partial_rank, "kv").reshape(tok_rows, slot_count, rank_half)
     matched = adapter_of_slot[None, :, None] == token_adapter[:, None, None]
     rank_projected = jnp.where(matched, rank_projected, 0.0).astype(jnp.bfloat16)
-    flat_low = rank_projected.reshape(tok_rows, slot_count * down_projected.shape[2])
-    flat_up = up_projected.reshape(slot_count * up_projected.shape[1], up_projected.shape[2])
-    adapter_total_output = jnp.dot(flat_low, flat_up, preferred_element_type=jnp.float32)
+    flat_low = rank_projected.reshape(tok_rows, slot_count * rank_half)
+    adapter_total_output = jnp.dot(flat_low, up_all, preferred_element_type=jnp.float32)
     return (moe_sum + adapter_total_output).astype(jnp.bfloat16)
 
 

time: 561 us -> 393 us (0.70)
  blocking collectives: 247 us -> 140 us
  waiting for transfers between devices: 237 us -> 173 us
    all_to_all x1, blocking collectives: 247 us -> 135 us  [on_device(): lax.all_to_all(outbox, 'pg', split_axis=0, concat_axis=0, tiled=True)]
    all_gather x2, waiting for transfers between devices: 217 us -> 145 us  [the longest x1 122 us: on_device(): packed_all = lax.all_gather(packed, 'pg', axis=0, tiled=False)]
    reduce_scatter x1, waiting for transfers between devices: 18.6 us -> 24.4 us  [expert_half(): lax.psum_scatter(summed.astype(jnp.bfloat16), 'kv', scatter_dimension=1,...]
  transfers between devices with their start and end apart: 4 -> 4, of which waited for: 3 -> 4; matrix products, arithmetic and copies ran while one was open for 2% -> 3% of each run, Pallas kernels for 0% -> 0%
where the time goes in v1:
time: 393 us
  waiting for transfers between devices  173 us (44%)
  blocking collectives  140 us (36%)
  matrix products  36.5 us (9%)
  between operations  15 us (4%)
  starting transfers between devices  14.5 us (4%)
  other arithmetic  10.5 us (3%)
    all_to_all x1, blocking collectives, on_device(): lax.all_to_all(outbox, 'pg', split_axis=0, concat_axis=0, tiled=True)  135 us
    all_gather x1, waiting for transfers between devices, on_device(): packed_all = lax.all_gather(packed, 'pg', axis=0, tiled=False)  122 us
    reduce_scatter x1, waiting for transfers between devices, expert_half(): lax.psum_scatter(summed.astype(jnp.bfloat16), 'kv', scatter_dimension=1,...  24.4 us
    all_gather x1, waiting for transfers between devices, on_device(): lax.all_gather(inbox_half.reshape(pg_size * slot_cap, half_width), 'kv',...  23.4 us
    all_to_all x1, starting transfers between devices, on_device(): lax.all_to_all(half_out.reshape(pg_size, slot_cap, half_width), 'pg', spl...  14.4 us
    dot_general x1, matrix products, expert_half(): jnp.einsum('rd,dgf->rgf', expert_rows, expert_gate_up_weight[0], preferre...  12.2 us
    dot_general x1, matrix products, expert_half(): jnp.dot(hidden, expert_down_weight[0, 0:piece_units], preferred_element_t...  8.23 us
  transfers between devices with their start and end apart: 4, of which 4 were waited for; matrix products, arithmetic and copies ran while one was open for 3% of the time, Pallas kernels for 0%

profile of v1, /device:TPU:2, one launch (start us, length us, event | category | flops | bytes accessed | tf_op | source)
XLA Modules:
  0.0 392.5 jit_solution(7069685487450936111)
XLA Ops:
  7.4 0.0 copy-start
  7.4 0.0 all-gather.4.cloned.1.call-start
  7.4 1.4 convert_element_type.66
  8.7 0.0 copy-start.2
  8.7 1.8 multiply_reduce_fusion
  10.5 0.8 copy.36
  11.3 0.1 eq.98
  11.5 0.4 fusion.18
  11.9 0.1 convert_element_type.61
  12.0 0.1 copy.37
  12.1 0.7 broadcast_add_fusion
  12.8 0.8 dynamic-slice.1
  13.6 1.7 convert_reduce_fusion
  15.2 1.6 convolution_convert_fusion.1
  16.8 0.0 copy-done.2
  16.9 134.8 %all_to_all.10 = bf16[128,16,1280]{2,1,0:T(8,128)(2,1)} all-to-all(bf16[128,16,1280]{2,1,0:T(8,128)(2,1)S(1)} %bitcast.31), channel_id=1, replica_groups=mesh['kv'=2,'pg'=128] {'pg'}, dimensions={0} | all-to-all | bytes 10485760 | tf_op jit(solution)/shard_map/all_to_all | solution.py:104
  151.6 0.0 all-gather.4.cloned.1.call-update
  151.6 0.0 reduce-scatter.2.cloned.1.call-start
  151.7 23.4 %all-gather.4.cloned.1.call-done = bf16[2048,2560]{1,0:T(8,128)(2,1)} async-done(((bf16[2048,1280]{1,0:T(8,128)(2,1)}), bf16[2048,2560]{1,0:T(8,128)(2,1)}) %all-gather.4.cloned.1.call-update) | async-done | bytes 10485776 | tf_op jit(solution)/shard_map/all_gather | solution.py:105
  175.1 12.2 %fusion = f32[2048,2,384]{2,0,1:T(8,128)S(1)} fusion(bf16[2048,2560]{1,0:T(8,128)(2,1)} %all-gather.4.cloned.1.call-done, bf16[2560,2,384]{2,1,0:T(2,128)(2,1)} %bitcast.37), kind=kOutput, calls=%fused_computation.1 | convolution fusion | flops 8053063680 | bytes 20709376 | tf_op jit(solution)/shard_map/rd,dgf->rgf/dot_general | solution.py:14
  187.2 0.0 copy-done
  187.3 8.2 %convolution_convert_fusion = bf16[2048,2560]{1,0:T(8,128)(2,1)} fusion(bf16[1,384,2560]{2,1,0:T(8,128)(2,1)S(1)} %copy-done, f32[2048,2,384]{2,0,1:T(8,128)S(1)} %fusion), kind=kOutput, calls=%fused_computation | convolution fusion | flops 4036493312 | bytes 18743296 | tf_op jit(solution)/shard_map/dot_general | solution.py:21
  195.5 0.0 copy-start.5
  195.5 0.0 copy-start.4
  195.5 0.0 reduce-scatter.2.cloned.1.call-update
  195.5 0.0 all-gather.6.cloned.1.call-start
  195.6 0.7 copy-done.5
  196.3 0.0 copy-done.4
  196.3 0.6 pad_maximum_fusion
  196.9 0.0 all-gather.6.cloned.1.call-update
  196.9 24.4 %reduce-scatter.2.cloned.1.call-done = bf16[2048,1280]{1,0:T(8,128)(2,1)} async-done(((bf16[2048,2560]{1,0:T(8,128)(2,1)}), bf16[2048,1280]{1,0:T(8,128)(2,1)}) %reduce-scatter.2.cloned.1.call-update) | async-done | bytes 5242896 | tf_op jit(solution)/shard_map/reduce_scatter | solution.py:25
  221.4 14.4 %all-to-all-start.1 = ((bf16[128,16,1280]{2,1,0:T(8,128)(2,1)}), bf16[128,16,1280]{2,1,0:T(8,128)(2,1)}, u32[]{:S(2)}, u32[]{:S(2)}) async-start(bf16[128,16,1280]{2,1,0:T(8,128)(2,1)} %bitcast.33), calls=%async_computation.2 | async-start | bytes 10485760 | tf_op jit(solution)/shard_map/all_to_all | solution.py:109
  235.8 0.0 copy-done.7
  235.8 0.0 copy-done.9
  235.8 0.2 select_reduce_fusion.2
  236.0 0.0 copy-done.8
  236.0 0.7 broadcast_compare_fusion
  236.7 0.0 copy-done.6
  236.7 3.5 select_reduce_fusion
  240.1 121.8 %all-gather.6.cloned.1.call-done = bf16[2048,1280]{1,0:T(8,128)(2,1)} async-done(((bf16[16,1280]{1,0:T(8,128)(2,1)}), bf16[2048,1280]{1,0:T(8,128)(2,1)}) %all-gather.6.cloned.1.call-update) | async-done | bytes 5242896 | tf_op jit(solution)/shard_map/all_gather | solution.py:94
  361.9 2.9 fusion.16
  364.8 5.3 %all-reduce.1 = bf16[128,128,8]{0,2,1:T(8,128)(2,1)} all-reduce(f32[128,128,8]{0,2,1:T(8,128)S(1)} %fusion.16), channel_id=1, replica_groups=mesh['kv'=2,'pg'=128] {'kv'}, use_global_device_ids=true, to_apply=%region_8.9 | all-reduce | flops 131072 | bytes 786432 | tf_op jit(solution)/shard_map/psum | solution.py:131
  370.1 3.3 fusion.8
  373.4 3.7 all-to-all-done.1
  377.1 3.8 fusion.22
  380.9 0.0 copy-done.1
  380.9 0.0 copy-done.3
  380.9 4.2 %fusion.11 = bf16[128,1280]{1,0:T(8,128)(2,1)} fusion(f32[128,1280]{1,0:T(8,128)S(1)} %copy-done.3, f32[128,1280]{1,0:T(8,128)S(1)} %fusion.22, bf16[2048,1280]{1,0:T(8,128)(2,1)} %bitcast.7, f32[128,2048]{1,0:T(8,128)S(1)} %copy-done.1, f32[128,2048]{1,0:T(8,128)S(1)} %get-tuple-element.5), kind=kOutput, calls=%fused_computation.22 | convolution fusion | flops 672890880 | bytes 8978432 | tf_op jit(solution)/shard_map/dot_general | solution.py:64
  (9 shorter events, 0.0 us)
Async XLA Ops:
  7.4 179.9 %copy-start = (bf16[1,384,2560]{2,1,0:T(8,128)(2,1)S(1)}, bf16[1,384,2560]{2,1,0:T(8,128)(2,1)}, u32[]{:S(2)}) copy-start(bf16[1,384,2560]{2,1,0:T(8,128)(2,1)} %param.19) | copy-start | bytes 5898244
  7.4 167.7 %all-gather.4.cloned.1.call-start = ((), (), s32[]{:S(2)}) async-start(), calls=%async_computation.3 | async-start | bytes 15728640 | tf_op jit(solution)/shard_map/all_gather | solution.py:105
  8.7 8.1 %copy-start.2 = (f32[128,2560]{1,0:T(8,128)}, f32[128,2560]{1,0:T(8,128)S(1)}, u32[]{:S(2)}) copy-start(f32[128,2560]{1,0:T(8,128)S(1)} %convert_element_type.66) | copy-start | bytes 3932164
  151.6 69.7 %reduce-scatter.2.cloned.1.call-start = ((), (), s32[]{:S(2)}) async-start(), calls=%async_computation.4 | async-start | bytes 15728640 | tf_op jit(solution)/shard_map/reduce_scatter | solution.py:25
  195.5 0.8 copy-start.5
  195.5 0.8 copy-start.4
  195.5 166.4 %all-gather.6.cloned.1.call-start = ((), (), s32[]{:S(2)}) async-start(), calls=%async_computation.5 | async-start | bytes 5283840 | tf_op jit(solution)/shard_map/all_gather | solution.py:94
  221.3 14.4 %copy-start.7 = (s32[256]{0:T(256)S(1)}, s32[256]{0:T(256)}, u32[]{:S(2)}) copy-start(s32[256]{0:T(256)} %param.16) | copy-start | bytes 3076
  221.3 14.4 %copy-start.9 = (s32[128]{0:T(128)S(1)}, s32[128]{0:T(128)}, u32[]{:S(2)}) copy-start(s32[128]{0:T(128)} %param.15) | copy-start | bytes 1540
  221.4 14.6 %copy-start.8 = (s32[128]{0:T(128)S(1)}, s32[128]{0:T(128)}, u32[]{:S(2)}) copy-start(s32[128]{0:T(128)} %param.17) | copy-start | bytes 1540
  221.4 15.3 %copy-start.6 = (f32[128,6]{0,1:T(8,128)S(1)}, f32[128,6]{0,1:T(8,128)}, u32[]{:S(2)}) copy-start(f32[128,6]{0,1:T(8,128)} %param.14) | copy-start | bytes 9220
  221.4 155.7 %all-to-all-start.1 = ((bf16[128,16,1280]{2,1,0:T(8,128)(2,1)}), bf16[128,16,1280]{2,1,0:T(8,128)(2,1)}, u32[]{:S(2)}, u32[]{:S(2)}) async-start(bf16[128,16,1280]{2,1,0:T(8,128)(2,1)} %bitcast.33), calls=%async_computation.2 | async-start | bytes 10485760 | tf_op jit(solution)/shard_map/all_to_all | solution.py:109
  377.1 3.8 copy-start.1
  377.1 3.8 copy-start.3
Sparse Core Ops, SparseCore 0:
  151.8 23.2 all-gather.3
  195.6 25.6 reduce-scatter.1
Sparse Core Ops, SparseCore 1:
  199.5 162.4 all-gather.5

commit v2 on v1

--- a/solution.py
+++ b/solution.py
@@ -2,6 +2,9 @@
 import jax.numpy as jnp
 from jax import lax
 from jax.sharding import PartitionSpec as P
+
+
+PG_AXES = ("px", "pz", "py")
 
 
 def normalize(states, gain_vector):
@@ -81,7 +84,7 @@
 ):
     tok_rows, model_width = layer_hidden_input.shape
     top_count = expert_choice_index.shape[1]
-    pg_size = lax.axis_size("pg")
+    pg_size = lax.axis_size(PG_AXES)
     expert_count = pg_size // 2
     slot_cap = 4 * tok_rows * top_count // (3 * expert_count)
     half_width = model_width // lax.axis_size("kv")
@@ -91,7 +94,6 @@
     down_own = lax.dynamic_slice_in_dim(adapter_down_weight[0], kv_index * half_width, half_width, axis=0)
     rank_half = down_own.shape[1]
     packed = jnp.concatenate([down_own.T, adapter_up_weight[0]], axis=0)
-    packed_all = lax.all_gather(packed, "pg", axis=0, tiled=False)
     flat_ids = expert_choice_index.reshape(-1)
     slot_rank = rank_in_expert(flat_ids, expert_count)
     rank_table = slot_rank.reshape(tok_rows, top_count)
@@ -101,14 +103,20 @@
     outbox = place_rows((first_slot, second_slot), slot_total, own_features).reshape(
         pg_size, slot_cap, half_width
     )
-    inbox_half = lax.all_to_all(outbox, "pg", split_axis=0, concat_axis=0, tiled=True)
+    inbox_half = lax.all_to_all(outbox, PG_AXES, split_axis=0, concat_axis=0, tiled=True)
+    inbox_half, packed = lax.optimization_barrier((inbox_half, packed))
+    packed_all = packed
+    for axis_name in reversed(PG_AXES):
+        packed_all = lax.all_gather(packed_all, axis_name, axis=0, tiled=False)
+    packed_all = packed_all.reshape((pg_size,) + packed.shape)
     inbox_rows = lax.all_gather(
         inbox_half.reshape(pg_size * slot_cap, half_width), "kv", axis=1, tiled=True
     )
     half_out = expert_half(inbox_rows, expert_gate_up_weight, expert_down_weight)
+    half_out, packed_all = lax.optimization_barrier((half_out, packed_all))
     results = lax.all_to_all(
         half_out.reshape(pg_size, slot_cap, half_width),
-        "pg",
+        PG_AXES,
         split_axis=0,
         concat_axis=0,
         tiled=True,
@@ -137,19 +145,29 @@
 
 
 def solution(mesh):
+    kv_count = mesh.shape["kv"]
+    pg_count = mesh.shape["pg"]
+    y_count = 4 if pg_count % 4 == 0 else 1
+    rest = pg_count // y_count
+    z_count = 8 if rest % 8 == 0 else rest
+    x_count = rest // z_count
+    split_mesh = jax.sharding.Mesh(
+        mesh.devices.reshape(kv_count, x_count, z_count, y_count), ("kv",) + PG_AXES
+    )
+    pg = PG_AXES
     placed = (
-        P("pg", None),
+        P(pg, None),
         P(),
-        P("pg", None),
-        P("pg", None),
-        P("pg"),
+        P(pg, None),
+        P(pg, None),
+        P(pg),
         P(),
         P(),
-        P("pg", None, None, "kv"),
-        P("pg", "kv", None),
-        P("pg", None, None),
-        P("pg", None, "kv"),
+        P(pg, None, None, "kv"),
+        P(pg, "kv", None),
+        P(pg, None, None),
+        P(pg, None, "kv"),
     )
     return jax.shard_map(
-        on_device, mesh=mesh, in_specs=placed, out_specs=P("pg", "kv"), check_vma=False
+        on_device, mesh=split_mesh, in_specs=placed, out_specs=P(pg, "kv"), check_vma=False
     )

time: 393 us -> 469 us (1.19)
  waiting for transfers between devices: 173 us -> 356 us
  blocking collectives: 140 us -> 18.3 us
  starting transfers between devices: 14.5 us -> 30.6 us
    all_to_all x1 -> x2, waiting for transfers between devices: 3.7 us -> 223 us  [the longest x1 119 us: on_device(): lax.all_to_all(outbox, PG_AXES, split_axis=0, concat_axis=0, tiled=True)]
    all_to_all x1 -> x0, blocking collectives: 135 us -> none  [on_device(): lax.all_to_all(outbox, 'pg', split_axis=0, concat_axis=0, tiled=True)]
    all_gather x1 -> x2, waiting for transfers between devices: 122 us -> 75 us  [on_device(): packed_all = lax.all_gather(packed_all, axis_name, axis=0, tiled=False)]
    all_to_all x1 -> x2, starting transfers between devices: 14.4 us -> 30.5 us  [the longest x1 16.1 us: on_device(): lax.all_to_all(outbox, PG_AXES, split_axis=0, concat_axis=0, tiled=True)]
    all_gather x0 -> x1, blocking collectives: none -> 13 us  [on_device(): packed_all = lax.all_gather(packed_all, axis_name, axis=0, tiled=False)]
    all_gather x1, waiting for transfers between devices: 23.4 us -> 28.5 us  [on_device(): lax.all_gather(inbox_half.reshape(pg_size * slot_cap, half_width), 'kv',...]
  transfers between devices with their start and end apart: 4 -> 6, of which waited for: 4 -> 6; matrix products, arithmetic and copies ran while one was open for 3% -> 7% of each run, Pallas kernels for 0% -> 0%
where the time goes in v2:
time: 469 us; the launch traced here: 468 us
  waiting for transfers between devices  356 us (76%)
  matrix products  38.7 us (8%)
  starting transfers between devices  30.6 us (7%)
  blocking collectives  18.3 us (4%)
  between operations  13.3 us (3%)
  other arithmetic  9.88 us (2%)
    all_to_all x1, waiting for transfers between devices, on_device(): lax.all_to_all(outbox, PG_AXES, split_axis=0, concat_axis=0, tiled=True)  119 us
    all_to_all x1, waiting for transfers between devices, on_device(): lax.all_to_all(half_out.reshape(pg_size, slot_cap, half_width), PG_AXES,...  104 us
    all_gather x2, waiting for transfers between devices, on_device(): packed_all = lax.all_gather(packed_all, axis_name, axis=0, tiled=False)  75 us
    all_gather x1, waiting for transfers between devices, on_device(): lax.all_gather(inbox_half.reshape(pg_size * slot_cap, half_width), 'kv',...  28.5 us
    reduce_scatter x1, waiting for transfers between devices, expert_half(): lax.psum_scatter(summed.astype(jnp.bfloat16), 'kv', scatter_dimension=1,...  27.9 us
    all_to_all x1, starting transfers between devices, on_device(): lax.all_to_all(outbox, PG_AXES, split_axis=0, concat_axis=0, tiled=True)  16.1 us
    all_to_all x1, starting transfers between devices, on_device(): lax.all_to_all(half_out.reshape(pg_size, slot_cap, half_width), PG_AXES,...  14.4 us
    all_gather x1, blocking collectives, on_device(): packed_all = lax.all_gather(packed_all, axis_name, axis=0, tiled=False)  13 us
  transfers between devices with their start and end apart: 6, of which 6 were waited for; matrix products, arithmetic and copies ran while one was open for 7% of the time, Pallas kernels for 0%

profile of v2, /device:TPU:2, one launch (start us, length us, event | category | flops | bytes accessed | tf_op | source)
XLA Modules:
  0.0 468.3 jit_solution(15037000671731903780)
XLA Ops:
  6.5 0.0 copy-start
  6.5 1.4 convert_element_type.66
  7.9 0.0 copy-start.2
  7.9 1.8 multiply_reduce_fusion
  9.7 0.8 copy.50
  10.5 0.1 eq.98
  10.6 0.4 fusion.22
  11.0 0.1 convert_element_type.61
  11.1 0.1 copy.51
  11.2 0.7 broadcast_add_fusion
  11.9 0.8 dynamic-slice.1
  12.7 1.7 convert_reduce_fusion
  14.4 3.9 convolution_convert_fusion.1
  18.3 0.0 copy-done.2
  18.3 16.1 %all-to-all-start = ((bf16[128,16,1280]{2,1,0:T(8,128)(2,1)}), bf16[128,16,1280]{2,1,0:T(8,128)(2,1)}, u32[]{:S(2)}, u32[]{:S(2)}) async-start(bf16[128,16,1280]{2,1,0:T(8,128)(2,1)} %bitcast.33), calls=%async_computation | async-start | bytes 10485760 | tf_op jit(solution)/shard_map/all_to_all | solution.py:106
  34.4 0.0 all-gather.9.cloned.1.call-start
  34.4 0.0 copy-done.5
  34.5 0.0 copy-done.4
  34.5 119.2 %all-to-all-done = bf16[128,16,1280]{2,1,0:T(8,128)(2,1)} async-done(((bf16[128,16,1280]{2,1,0:T(8,128)(2,1)}), bf16[128,16,1280]{2,1,0:T(8,128)(2,1)}, u32[]{:S(2)}, u32[]{:S(2)}) %all-to-all-start) | async-done | bytes 5242912 | tf_op jit(solution)/shard_map/all_to_all | solution.py:106
  153.7 13.0 %all-gather = bf16[64,1280]{1,0:T(8,128)(2,1)} all-gather(bf16[16,1280]{1,0:T(8,128)(2,1)S(1)} %pad_maximum_fusion), channel_id=2, replica_groups=mesh['kv'=2,'px'=4,'pz'=8,'py'=4] {'py'}, dimensions={0}, use_global_device_ids=true | all-gather | bytes 204800 | tf_op jit(solution)/shard_map/all_gather | solution.py:110
  166.6 0.0 all-gather.9.cloned.1.call-update
  166.6 0.0 all-gather.7.cloned.1.call-start
  166.7 0.7 all-gather.7.cloned.1.call-update
  167.4 0.0 all-gather.11.cloned.1.call-start
  167.4 33.2 %all-gather.9.cloned.1.call-done = bf16[32,16,1280]{2,1,0:T(8,128)(2,1)} async-done(((bf16[4,16,1280]{2,1,0:T(8,128)(2,1)}), bf16[32,16,1280]{2,1,0:T(8,128)(2,1)}) %all-gather.9.cloned.1.call-update) | async-done | bytes 1310736 | tf_op jit(solution)/shard_map/all_gather | solution.py:110
  200.6 0.0 all-gather.11.cloned.1.call-update
  200.6 0.0 reduce-scatter.2.cloned.1.call-start
  200.7 28.5 %all-gather.7.cloned.1.call-done = bf16[2048,2560]{1,0:T(8,128)(2,1)} async-done(((bf16[2048,1280]{1,0:T(8,128)(2,1)}), bf16[2048,2560]{1,0:T(8,128)(2,1)}) %all-gather.7.cloned.1.call-update) | async-done | bytes 10485776 | tf_op jit(solution)/shard_map/all_gather | solution.py:112
  229.1 12.2 %fusion = f32[2048,2,384]{2,0,1:T(8,128)S(1)} fusion(bf16[2048,2560]{1,0:T(8,128)(2,1)} %all-gather.7.cloned.1.call-done, bf16[2560,2,384]{2,1,0:T(2,128)(2,1)} %bitcast.40), kind=kOutput, calls=%fused_computation.1 | convolution fusion | flops 8053063680 | bytes 20709376 | tf_op jit(solution)/shard_map/rd,dgf->rgf/dot_general | solution.py:17
  241.3 0.0 copy-done
  241.3 8.2 %convolution_convert_fusion = bf16[2048,2560]{1,0:T(8,128)(2,1)} fusion(bf16[1,384,2560]{2,1,0:T(8,128)(2,1)S(1)} %copy-done, f32[2048,2,384]{2,0,1:T(8,128)S(1)} %fusion), kind=kOutput, calls=%fused_computation | convolution fusion | flops 4036493312 | bytes 18743296 | tf_op jit(solution)/shard_map/dot_general | solution.py:24
  249.5 0.0 reduce-scatter.2.cloned.1.call-update
  249.5 41.8 %all-gather.11.cloned.1.call-done = bf16[32,4,16,1280]{3,2,1,0:T(8,128)(2,1)} async-done(((bf16[8,4,16,1280]{3,2,1,0:T(8,128)(2,1)}), bf16[32,4,16,1280]{3,2,1,0:T(8,128)(2,1)}) %all-gather.11.cloned.1.call-update) | async-done | bytes 5242896 | tf_op jit(solution)/shard_map/all_gather | solution.py:110
  291.3 27.9 %reduce-scatter.2.cloned.1.call-done = bf16[2048,1280]{1,0:T(8,128)(2,1)} async-done(((bf16[2048,2560]{1,0:T(8,128)(2,1)}), bf16[2048,1280]{1,0:T(8,128)(2,1)}) %reduce-scatter.2.cloned.1.call-update) | async-done | bytes 5242896 | tf_op jit(solution)/shard_map/reduce_scatter | solution.py:28
  319.2 14.4 %all-to-all-start.1 = ((bf16[128,16,1280]{2,1,0:T(8,128)(2,1)}), bf16[128,16,1280]{2,1,0:T(8,128)(2,1)}, u32[]{:S(2)}, u32[]{:S(2)}) async-start(bf16[128,16,1280]{2,1,0:T(8,128)(2,1)} %bitcast.34), calls=%async_computation.2 | async-start | bytes 10485760 | tf_op jit(solution)/shard_map/all_to_all | solution.py:117
  333.7 0.0 copy-done.7
  333.7 0.0 copy-done.9
  333.7 0.2 select_reduce_fusion.2
  333.8 0.0 copy-done.8
  333.9 0.7 broadcast_compare_fusion
  334.6 0.0 copy-done.6
  334.6 3.5 select_reduce_fusion
  338.0 2.9 fusion.18
  340.9 5.3 %all-reduce.1 = bf16[128,128,8]{0,2,1:T(8,128)(2,1)} all-reduce(f32[128,128,8]{0,2,1:T(8,128)S(1)} %fusion.18), channel_id=1, replica_groups=mesh['kv'=2,'px'=4,'pz'=8,'py'=4] {'kv'}, use_global_device_ids=true, to_apply=%region_8.9 | all-reduce | flops 131072 | bytes 786432 | tf_op jit(solution)/shard_map/psum | solution.py:139
  346.2 3.3 fusion.10
  349.5 104.3 %all-to-all-done.1 = bf16[128,16,1280]{2,1,0:T(8,128)(2,1)} async-done(((bf16[128,16,1280]{2,1,0:T(8,128)(2,1)}), bf16[128,16,1280]{2,1,0:T(8,128)(2,1)}, u32[]{:S(2)}, u32[]{:S(2)}) %all-to-all-start.1) | async-done | bytes 5242912 | tf_op jit(solution)/shard_map/all_to_all | solution.py:117
  453.8 3.8 fusion.26
  457.6 4.2 fusion.13
  (14 shorter events, 0.0 us)
Async XLA Ops:
  6.5 234.8 %copy-start = (bf16[1,384,2560]{2,1,0:T(8,128)(2,1)S(1)}, bf16[1,384,2560]{2,1,0:T(8,128)(2,1)}, u32[]{:S(2)}) copy-start(bf16[1,384,2560]{2,1,0:T(8,128)(2,1)} %param.19) | copy-start | bytes 5898244
  7.9 10.4 %copy-start.2 = (f32[128,2560]{1,0:T(8,128)}, f32[128,2560]{1,0:T(8,128)S(1)}, u32[]{:S(2)}) copy-start(f32[128,2560]{1,0:T(8,128)S(1)} %convert_element_type.66) | copy-start | bytes 3932164
  18.3 16.1 %copy-start.5 = (bf16[1,2560,8]{1,2,0:T(8,128)(2,1)S(1)}, bf16[1,2560,8]{1,2,0:T(8,128)(2,1)}, u32[]{:S(2)}) copy-start(bf16[1,2560,8]{1,2,0:T(8,128)(2,1)} %param.20) | copy-start | bytes 122884
  18.3 16.2 %copy-start.4 = (bf16[1,8,1280]{2,1,0:T(8,128)(2,1)S(1)}, bf16[1,8,1280]{2,1,0:T(8,128)(2,1)}, u32[]{:S(2)}) copy-start(bf16[1,8,1280]{2,1,0:T(8,128)(2,1)} %param.21) | copy-start | bytes 61444
  18.3 135.3 %all-to-all-start = ((bf16[128,16,1280]{2,1,0:T(8,128)(2,1)}), bf16[128,16,1280]{2,1,0:T(8,128)(2,1)}, u32[]{:S(2)}, u32[]{:S(2)}) async-start(bf16[128,16,1280]{2,1,0:T(8,128)(2,1)} %bitcast.33), calls=%async_computation | async-start | bytes 10485760 | tf_op jit(solution)/shard_map/all_to_all | solution.py:106
  34.4 166.2 %all-gather.9.cloned.1.call-start = ((), (), s32[]{:S(2)}) async-start(), calls=%async_computation.5 | async-start | bytes 1474560 | tf_op jit(solution)/shard_map/all_gather | solution.py:110
  166.6 62.5 %all-gather.7.cloned.1.call-start = ((), (), s32[]{:S(2)}) async-start(), calls=%async_computation.3 | async-start | bytes 15728640 | tf_op jit(solution)/shard_map/all_gather | solution.py:112
  167.4 123.9 %all-gather.11.cloned.1.call-start = ((), (), s32[]{:S(2)}) async-start(), calls=%async_computation.6 | async-start | bytes 6553600 | tf_op jit(solution)/shard_map/all_gather | solution.py:110
  200.6 118.6 %reduce-scatter.2.cloned.1.call-start = ((), (), s32[]{:S(2)}) async-start(), calls=%async_computation.4 | async-start | bytes 15728640 | tf_op jit(solution)/shard_map/reduce_scatter | solution.py:28
  319.2 14.4 %copy-start.7 = (s32[256]{0:T(256)S(1)}, s32[256]{0:T(256)}, u32[]{:S(2)}) copy-start(s32[256]{0:T(256)} %param.16) | copy-start | bytes 3076
  319.2 14.5 %copy-start.9 = (s32[128]{0:T(128)S(1)}, s32[128]{0:T(128)}, u32[]{:S(2)}) copy-start(s32[128]{0:T(128)} %param.15) | copy-start | bytes 1540
  319.2 14.6 %copy-start.8 = (s32[128]{0:T(128)S(1)}, s32[128]{0:T(128)}, u32[]{:S(2)}) copy-start(s32[128]{0:T(128)} %param.17) | copy-start | bytes 1540
  319.2 15.3 %copy-start.6 = (f32[128,6]{0,1:T(8,128)S(1)}, f32[128,6]{0,1:T(8,128)}, u32[]{:S(2)}) copy-start(f32[128,6]{0,1:T(8,128)} %param.14) | copy-start | bytes 9220
  319.2 134.5 %all-to-all-start.1 = ((bf16[128,16,1280]{2,1,0:T(8,128)(2,1)}), bf16[128,16,1280]{2,1,0:T(8,128)(2,1)}, u32[]{:S(2)}, u32[]{:S(2)}) async-start(bf16[128,16,1280]{2,1,0:T(8,128)(2,1)} %bitcast.34), calls=%async_computation.2 | async-start | bytes 10485760 | tf_op jit(solution)/shard_map/all_to_all | solution.py:117
  453.8 3.8 copy-start.1
  453.8 3.8 copy-start.3
Sparse Core Ops, SparseCore 0:
  166.8 33.7 all-gather.8
  202.4 26.7 all-gather.6
  231.0 60.3 all-gather.10
  293.7 25.4 reduce-scatter.1

commit v3 on v2

--- a/solution.py
+++ b/solution.py
@@ -13,19 +13,36 @@
     return (values * inverse_rms * gain_vector).astype(jnp.bfloat16)
 
 
-def expert_half(expert_rows, expert_gate_up_weight, expert_down_weight):
+def swap_kv(values):
+    return lax.ppermute(values, "kv", perm=[(0, 1), (1, 0)])
+
+
+def expert_half(own_rows, expert_gate_up_weight, expert_down_weight):
+    kv_index = lax.axis_index("kv")
+    half_width = own_rows.shape[1]
+    other_rows = swap_kv(own_rows)
+    gate_up_weight = expert_gate_up_weight[0]
+    own_weight = lax.dynamic_slice_in_dim(gate_up_weight, kv_index * half_width, half_width, 0)
+    other_weight = lax.dynamic_slice_in_dim(
+        gate_up_weight, (1 - kv_index) * half_width, half_width, 0
+    )
     gate_up = jnp.einsum(
-        "rd,dgf->rgf", expert_rows, expert_gate_up_weight[0], preferred_element_type=jnp.float32
+        "rd,dgf->rgf", own_rows, own_weight, preferred_element_type=jnp.float32
+    ) + jnp.einsum("rd,dgf->rgf", other_rows, other_weight, preferred_element_type=jnp.float32)
+    hidden = (jax.nn.silu(gate_up[:, 0]) * gate_up[:, 1]).astype(jnp.bfloat16)
+    down_weight = expert_down_weight[0]
+    other_cols = lax.dynamic_slice_in_dim(down_weight, (1 - kv_index) * half_width, half_width, 1)
+    own_cols = lax.dynamic_slice_in_dim(down_weight, kv_index * half_width, half_width, 1)
+    sent_quarter = jnp.dot(hidden, other_cols, preferred_element_type=jnp.float32).astype(
+        jnp.bfloat16
     )
-    hidden = (jax.nn.silu(gate_up[:, 0]) * gate_up[:, 1]).astype(jnp.bfloat16)
-    local_units = hidden.shape[1]
-    piece_count = 2 // lax.axis_size("kv")
-    piece_units = local_units // piece_count
-    quarter = jnp.dot(
-        hidden, expert_down_weight[0, 0:piece_units], preferred_element_type=jnp.float32
+    received_quarter = swap_kv(sent_quarter)
+    own_quarter = jnp.dot(hidden, own_cols, preferred_element_type=jnp.float32).astype(
+        jnp.bfloat16
     )
-    summed = quarter.astype(jnp.bfloat16).astype(jnp.float32)
-    return lax.psum_scatter(summed.astype(jnp.bfloat16), "kv", scatter_dimension=1, tiled=True)
+    return (own_quarter.astype(jnp.float32) + received_quarter.astype(jnp.float32)).astype(
+        jnp.bfloat16
+    )
 
 
 def rank_in_expert(flat_ids, expert_count):
@@ -103,16 +120,13 @@
     outbox = place_rows((first_slot, second_slot), slot_total, own_features).reshape(
         pg_size, slot_cap, half_width
     )
+    outbox, packed = lax.optimization_barrier((outbox, packed))
     inbox_half = lax.all_to_all(outbox, PG_AXES, split_axis=0, concat_axis=0, tiled=True)
-    inbox_half, packed = lax.optimization_barrier((inbox_half, packed))
     packed_all = packed
     for axis_name in reversed(PG_AXES):
         packed_all = lax.all_gather(packed_all, axis_name, axis=0, tiled=False)
     packed_all = packed_all.reshape((pg_size,) + packed.shape)
-    inbox_rows = lax.all_gather(
-        inbox_half.reshape(pg_size * slot_cap, half_width), "kv", axis=1, tiled=True
-    )
-    half_out = expert_half(inbox_rows, expert_gate_up_weight, expert_down_weight)
+    half_out = expert_half(inbox_half.reshape(pg_size * slot_cap, half_width), expert_gate_up_weight, expert_down_weight)
     half_out, packed_all = lax.optimization_barrier((half_out, packed_all))
     results = lax.all_to_all(
         half_out.reshape(pg_size, slot_cap, half_width),

time: 469 us -> 407 us (0.87)
  waiting for transfers between devices: 356 us -> 169 us
  blocking collectives: 18.3 us -> 153 us
  starting transfers between devices: 30.6 us -> 14.4 us
  local copies, waits for them, and re-layouts: 1.95 us -> 8.5 us
    all_to_all x0 -> x1, blocking collectives: none -> 135 us  [on_device(): lax.all_to_all(outbox, PG_AXES, split_axis=0, concat_axis=0, tiled=True)]
    all_to_all x1 -> x0, waiting for transfers between devices: 119 us -> none  [on_device(): lax.all_to_all(outbox, PG_AXES, split_axis=0, concat_axis=0, tiled=True)]
    all_gather x1 -> x0, waiting for transfers between devices: 28.5 us -> none  [on_device(): lax.all_gather(inbox_half.reshape(pg_size * slot_cap, half_width), 'kv',...]
    reduce_scatter x1 -> x0, waiting for transfers between devices: 27.9 us -> none  [expert_half(): lax.psum_scatter(summed.astype(jnp.bfloat16), 'kv', scatter_dimension=1,...]
    all_gather x2, waiting for transfers between devices: 75 us -> 57.4 us  [on_device(): packed_all = lax.all_gather(packed_all, axis_name, axis=0, tiled=False)]
    all_to_all x1 -> x0, starting transfers between devices: 16.1 us -> none  [on_device(): lax.all_to_all(outbox, PG_AXES, split_axis=0, concat_axis=0, tiled=True)]
    ppermute x0 -> x2, waiting for transfers between devices: none -> 8.65 us  [swap_kv(): return lax.ppermute(values, 'kv', perm=[(0, 1), (1, 0)])]
    dynamic_slice x0 -> x1, local copies, waits for them, and re-layouts: none -> 5.83 us  [expert_half(): lax.dynamic_slice_in_dim(gate_up_weight, (1 - kv_index) * half_width, hal...]
  transfers between devices with their start and end apart: 6 -> 5, of which waited for: 6 -> 4; matrix products, arithmetic and copies ran while one was open for 7% -> 9% of each run, Pallas kernels for 0% -> 0%
where the time goes in v3:
time: 407 us
  waiting for transfers between devices  169 us (42%)
  blocking collectives  153 us (38%)
  matrix products  37 us (9%)
  starting transfers between devices  14.4 us (4%)
  between operations  13.6 us (3%)
  other arithmetic  10.8 us (3%)
  local copies, waits for them, and re-layouts  8.5 us (2%)
    all_to_all x1, blocking collectives, on_device(): lax.all_to_all(outbox, PG_AXES, split_axis=0, concat_axis=0, tiled=True)  135 us
    all_to_all x1, waiting for transfers between devices, on_device(): lax.all_to_all(half_out.reshape(pg_size, slot_cap, half_width), PG_AXES,...  103 us
    all_gather x2, waiting for transfers between devices, on_device(): packed_all = lax.all_gather(packed_all, axis_name, axis=0, tiled=False)  57.4 us
    all_to_all x1, starting transfers between devices, on_device(): lax.all_to_all(half_out.reshape(pg_size, slot_cap, half_width), PG_AXES,...  14.1 us
    all_gather x1, blocking collectives, on_device(): packed_all = lax.all_gather(packed_all, axis_name, axis=0, tiled=False)  12.8 us
    ppermute x2, waiting for transfers between devices, swap_kv(): return lax.ppermute(values, 'kv', perm=[(0, 1), (1, 0)])  8.65 us
  transfers between devices with their start and end apart: 5, of which 4 were waited for; matrix products, arithmetic and copies ran while one was open for 9% of the time, Pallas kernels for 0%

profile of v3, /device:TPU:2, one launch (start us, length us, event | category | flops | bytes accessed | tf_op | source)
XLA Modules:
  0.0 406.8 jit_solution(13614306296349522557)
XLA Ops:
  6.5 0.0 copy-start
  6.5 0.0 all-gather.6.cloned.1.call-start
  6.5 1.4 convert_element_type.77
  7.9 0.0 copy-start.2
  7.9 1.8 multiply_reduce_fusion
  9.7 0.8 copy.55
  10.5 0.1 eq.98
  10.6 0.4 fusion.28
  11.0 0.1 convert_element_type.72
  11.2 0.1 copy.56
  11.2 0.7 broadcast_add_fusion
  11.9 0.8 dynamic-slice.5
  12.7 0.7 dynamic-slice_bitcast_fusion
  13.5 1.7 convert_reduce_fusion
  15.2 0.0 copy-done.5
  15.2 1.6 convolution_convert_fusion.2
  16.8 0.0 copy-done.2
  16.8 134.8 %all_to_all.10 = bf16[128,16,1280]{2,1,0:T(8,128)(2,1)} all-to-all(bf16[128,16,1280]{2,1,0:T(8,128)(2,1)S(1)} %bitcast.48), channel_id=1, replica_groups=mesh['kv'=2,'px'=4,'pz'=8,'py'=4] {'px','pz','py'}, dimensions={0} | all-to-all | bytes 10485760 | tf_op jit(solution)/shard_map/all_to_all | solution.py:124
  151.6 0.0 collective-permute-start
  151.6 12.8 %all-gather = bf16[64,1280]{1,0:T(8,128)(2,1)} all-gather(bf16[16,1280]{1,0:T(8,128)(2,1)S(1)} %pad_maximum_fusion), channel_id=2, replica_groups=mesh['kv'=2,'px'=4,'pz'=8,'py'=4] {'py'}, dimensions={0}, use_global_device_ids=true | all-gather | bytes 204800 | tf_op jit(solution)/shard_map/all_gather | solution.py:127
  164.3 0.0 all-gather.6.cloned.1.call-update
  164.4 0.2 all-gather.8.cloned.1.call-start
  164.6 5.8 %constant_dynamic-slice_fusion = (bf16[1,1280,2,384]{3,2,1,0:T(2,128)(2,1)}, bf16[1,1280,2,384]{3,2,1,0:T(2,128)(2,1)}) fusion(bf16[1,2560,2,384]{3,2,1,0:T(2,128)(2,1)} %param.18, s32[]{:T(128)S(6)} %select_n.28, s32[]{:T(128)S(6)} %select_n.27), kind=kLoop, calls=%fused_computation.67 | loop fusion | bytes 7864328 | tf_op jit(solution)/shard_map/dynamic_slice | solution.py:26
  170.4 28.7 %all-gather.6.cloned.1.call-done = bf16[32,16,1280]{2,1,0:T(8,128)(2,1)} async-done(((bf16[4,16,1280]{2,1,0:T(8,128)(2,1)}), bf16[32,16,1280]{2,1,0:T(8,128)(2,1)}) %all-gather.6.cloned.1.call-update) | async-done | bytes 1310736 | tf_op jit(solution)/shard_map/all_gather | solution.py:127
  199.1 0.0 all-gather.8.cloned.1.call-update
  199.1 0.0 copy-start.3
  199.1 7.0 %fusion.18 = f32[2048,2,384]{2,0,1:T(8,128)S(1)} fusion(bf16[2048,1280,1]{1,0,2:T(8,128)(2,1)} %bitcast.5, bf16[1,1280,2,384]{3,2,1,0:T(2,128)(2,1)} %get-tuple-element.18), kind=kOutput, calls=%fused_computation.29 | convolution fusion | flops 4026531840 | bytes 13500416 | tf_op jit(solution)/shard_map/rd,dgf->rgf/dot_general | solution.py:29
  206.1 0.0 collective-permute-done
  206.1 0.0 copy-done.3
  206.1 6.3 %fusion.2 = f32[2048,2,384]{2,0,1:T(8,128)S(1)} fusion(f32[2048,2,384]{2,0,1:T(8,128)S(1)} %fusion.18, bf16[2048,1280]{1,0:T(8,128)(2,1)} %collective-permute-done, bf16[1,1280,2,384]{3,2,1,0:T(2,128)(2,1)S(1)} %copy-done.3), kind=kOutput, calls=%fused_computation.14 | convolution fusion | flops 4028104704 | bytes 19791872 | tf_op jit(solution)/shard_map/rd,dgf->rgf/dot_general | solution.py:31
  212.4 0.9 fusion.5
  213.4 3.1 convolution_convert_fusion
  216.5 0.1 collective-permute-start.1
  216.6 8.6 %collective-permute-done.1 = bf16[2048,1280]{1,0:T(8,128)(2,1)S(1)} collective-permute-done((bf16[2048,1280]{1,0:T(8,128)(2,1)S(1)}, bf16[2048,1280]{1,0:T(8,128)(2,1)S(1)}, u32[]{:S(2)}, u32[]{:S(2)}) %collective-permute-start.1) | collective-permute-done | bytes 5242912 | tf_op jit(solution)/shard_map/ppermute | solution.py:17
  225.2 4.5 %add_convert_fusion = bf16[2048,1280]{1,0:T(8,128)(2,1)} fusion(bf16[2048,1280]{1,0:T(8,128)(2,1)S(1)} %collective-permute-done.1, bf16[2048,1,384]{2,0,1:T(8,128)(2,1)S(1)} %fusion.5, bf16[1,384,2560]{2,1,0:T(8,128)(2,1)S(1)} %copy-done, s32[]{:T(128)S(6)} %select_n.27), kind=kOutput, calls=%fused_computation | convolution fusion | flops 2026373120 | bytes 13041668 | tf_op jit(solution)/shard_map/dot_general | solution.py:40
  229.8 28.8 %all-gather.8.cloned.1.call-done = bf16[32,4,16,1280]{3,2,1,0:T(8,128)(2,1)} async-done(((bf16[8,4,16,1280]{3,2,1,0:T(8,128)(2,1)}), bf16[32,4,16,1280]{3,2,1,0:T(8,128)(2,1)}) %all-gather.8.cloned.1.call-update) | async-done | bytes 5242896 | tf_op jit(solution)/shard_map/all_gather | solution.py:127
  258.5 14.1 %all-to-all-start.1 = ((bf16[128,16,1280]{2,1,0:T(8,128)(2,1)}), bf16[128,16,1280]{2,1,0:T(8,128)(2,1)}, u32[]{:S(2)}, u32[]{:S(2)}) async-start(bf16[128,16,1280]{2,1,0:T(8,128)(2,1)} %bitcast.49), calls=%async_computation.1 | async-start | bytes 10485760 | tf_op jit(solution)/shard_map/all_to_all | solution.py:131
  272.7 0.2 select_reduce_fusion.2
  272.9 0.7 broadcast_compare_fusion
  273.6 3.5 select_reduce_fusion
  277.0 2.9 fusion.24
  279.9 5.5 %all-reduce.1 = bf16[128,128,8]{0,2,1:T(8,128)(2,1)} all-reduce(f32[128,128,8]{0,2,1:T(8,128)S(1)} %fusion.24), channel_id=1, replica_groups=mesh['kv'=2,'px'=4,'pz'=8,'py'=4] {'kv'}, use_global_device_ids=true, to_apply=%region_7.8 | all-reduce | flops 131072 | bytes 786432 | tf_op jit(solution)/shard_map/psum | solution.py:153
  285.4 3.3 fusion.12
  288.7 103.2 %all-to-all-done.1 = bf16[128,16,1280]{2,1,0:T(8,128)(2,1)} async-done(((bf16[128,16,1280]{2,1,0:T(8,128)(2,1)}), bf16[128,16,1280]{2,1,0:T(8,128)(2,1)}, u32[]{:S(2)}, u32[]{:S(2)}) %all-to-all-start.1) | async-done | bytes 5242912 | tf_op jit(solution)/shard_map/all_to_all | solution.py:131
  391.9 3.8 fusion.36
  395.7 0.0 copy-done.1
  395.7 0.0 copy-done.4
  395.7 4.2 %fusion.15 = bf16[128,1280]{1,0:T(8,128)(2,1)} fusion(f32[128,1280]{1,0:T(8,128)S(1)} %copy-done.4, f32[128,1280]{1,0:T(8,128)S(1)} %fusion.36, bf16[2048,1280]{1,0:T(8,128)(2,1)} %bitcast.16, f32[128,2048]{1,0:T(8,128)S(1)} %copy-done.1, f32[128,2048]{1,0:T(8,128)S(1)} %get-tuple-element.13), kind=kOutput, calls=%fused_computation.25 | convolution fusion | flops 672890880 | bytes 8978432 | tf_op jit(solution)/shard_map/dot_general | solution.py:84
  (15 shorter events, 0.0 us)
Async XLA Ops:
  6.5 206.8 %copy-start = (bf16[1,384,2560]{2,1,0:T(8,128)(2,1)S(1)}, bf16[1,384,2560]{2,1,0:T(8,128)(2,1)}, u32[]{:S(2)}) copy-start(bf16[1,384,2560]{2,1,0:T(8,128)(2,1)} %param.19) | copy-start | bytes 5898244
  6.5 8.6 %copy-start.5 = (bf16[1,8,1280]{2,1,0:T(8,128)(2,1)S(1)}, bf16[1,8,1280]{2,1,0:T(8,128)(2,1)}, u32[]{:S(2)}) copy-start(bf16[1,8,1280]{2,1,0:T(8,128)(2,1)} %param.21) | copy-start | bytes 61444
  6.5 192.6 %all-gather.6.cloned.1.call-start = ((), (), s32[]{:S(2)}) async-start(), calls=%async_computation.2 | async-start | bytes 1474560 | tf_op jit(solution)/shard_map/all_gather | solution.py:127
  7.9 8.9 %copy-start.2 = (f32[128,2560]{1,0:T(8,128)}, f32[128,2560]{1,0:T(8,128)S(1)}, u32[]{:S(2)}) copy-start(f32[128,2560]{1,0:T(8,128)S(1)} %convert_element_type.77) | copy-start | bytes 3932164
  151.6 54.6 %collective-permute-start = (bf16[2048,1280]{1,0:T(8,128)(2,1)}, bf16[2048,1280]{1,0:T(8,128)(2,1)}, u32[]{:S(2)}, u32[]{:S(2)}) collective-permute-start(bf16[2048,1280]{1,0:T(8,128)(2,1)} %bitcast.4), channel_id=1, source_target_pairs={{0,128},{128,0},{1,129},{129,1},{2,130},{130,2},{3,131},{131,3},{4... | collective-permute-start | bytes 15728648 | tf_op jit(solution)/shard_map/ppermute | solution.py:17
  164.4 94.2 %all-gather.8.cloned.1.call-start = ((), (), s32[]{:S(2)}) async-start(), calls=%async_computation.3 | async-start | bytes 6553600 | tf_op jit(solution)/shard_map/all_gather | solution.py:127
  199.1 7.0 %copy-start.3 = (bf16[1,1280,2,384]{3,2,1,0:T(2,128)(2,1)S(1)}, bf16[1,1280,2,384]{3,2,1,0:T(2,128)(2,1)}, u32[]{:S(2)}) copy-start(bf16[1,1280,2,384]{3,2,1,0:T(2,128)(2,1)} %get-tuple-element.17) | copy-start | bytes 5898244
  216.5 8.7 %collective-permute-start.1 = (bf16[2048,1280]{1,0:T(8,128)(2,1)S(1)}, bf16[2048,1280]{1,0:T(8,128)(2,1)S(1)}, u32[]{:S(2)}, u32[]{:S(2)}) collective-permute-start(bf16[2048,1280]{1,0:T(8,128)(2,1)S(1)} %convolution_convert_fusion), channel_id=1, source_target_pairs={{0,128},{128,0},{1,129},{129,1},{2,130},{130,2},{3,131},{131,3},{4... | collective-permute-start | bytes 15728648 | tf_op jit(solution)/shard_map/ppermute | solution.py:17
  258.5 14.1 %copy-start.7 = (s32[256]{0:T(256)S(1)}, s32[256]{0:T(256)}, u32[]{:S(2)}) copy-start(s32[256]{0:T(256)} %param.16) | copy-start | bytes 3076
  258.5 14.1 %copy-start.9 = (s32[128]{0:T(128)S(1)}, s32[128]{0:T(128)}, u32[]{:S(2)}) copy-start(s32[128]{0:T(128)} %param.15) | copy-start | bytes 1540
  258.5 14.3 %copy-start.8 = (s32[128]{0:T(128)S(1)}, s32[128]{0:T(128)}, u32[]{:S(2)}) copy-start(s32[128]{0:T(128)} %param.17) | copy-start | bytes 1540
  258.5 15.0 %copy-start.6 = (f32[128,6]{0,1:T(8,128)S(1)}, f32[128,6]{0,1:T(8,128)}, u32[]{:S(2)}) copy-start(f32[128,6]{0,1:T(8,128)} %param.14) | copy-start | bytes 9220
  258.5 133.3 %all-to-all-start.1 = ((bf16[128,16,1280]{2,1,0:T(8,128)(2,1)}), bf16[128,16,1280]{2,1,0:T(8,128)(2,1)}, u32[]{:S(2)}, u32[]{:S(2)}) async-start(bf16[128,16,1280]{2,1,0:T(8,128)(2,1)} %bitcast.49), calls=%async_computation.1 | async-start | bytes 10485760 | tf_op jit(solution)/shard_map/all_to_all | solution.py:131
  391.9 3.8 copy-start.1
  391.9 3.8 copy-start.4
Sparse Core Ops, SparseCore 0:
  164.5 34.5 all-gather.5
  200.9 57.5 all-gather.7

commit v4 on v3

--- a/solution.py
+++ b/solution.py
@@ -120,14 +120,9 @@
     outbox = place_rows((first_slot, second_slot), slot_total, own_features).reshape(
         pg_size, slot_cap, half_width
     )
-    outbox, packed = lax.optimization_barrier((outbox, packed))
     inbox_half = lax.all_to_all(outbox, PG_AXES, split_axis=0, concat_axis=0, tiled=True)
-    packed_all = packed
-    for axis_name in reversed(PG_AXES):
-        packed_all = lax.all_gather(packed_all, axis_name, axis=0, tiled=False)
-    packed_all = packed_all.reshape((pg_size,) + packed.shape)
+    packed_all = lax.all_gather(packed, PG_AXES, axis=0, tiled=False)
     half_out = expert_half(inbox_half.reshape(pg_size * slot_cap, half_width), expert_gate_up_weight, expert_down_weight)
-    half_out, packed_all = lax.optimization_barrier((half_out, packed_all))
     results = lax.all_to_all(
         half_out.reshape(pg_size, slot_cap, half_width),
         PG_AXES,

time: 407 us -> 362 us (0.89)
  waiting for transfers between devices: 169 us -> 140 us
  blocking collectives: 153 us -> 140 us
  starting transfers between devices: 14.4 us -> 8.71 us
    all_to_all x1, waiting for transfers between devices: 103 us -> 0.01 us  [on_device(): lax.all_to_all(half_out.reshape(pg_size, slot_cap, half_width), PG_AXES,...]
    all_gather x2 -> x1, waiting for transfers between devices: 57.4 us -> 132 us  [on_device(): packed_all = lax.all_gather(packed, PG_AXES, axis=0, tiled=False)]
    all_gather x1 -> x0, blocking collectives: 12.8 us -> none  [on_device(): packed_all = lax.all_gather(packed_all, axis_name, axis=0, tiled=False)]
    all_to_all x1, starting transfers between devices: 14.1 us -> 8.21 us  [on_device(): lax.all_to_all(half_out.reshape(pg_size, slot_cap, half_width), PG_AXES,...]
  transfers between devices with their start and end apart: 5 -> 4, of which waited for: 4 -> 2; matrix products, arithmetic and copies ran while one was open for 9% -> 8% of each run, Pallas kernels for 0% -> 0%
where the time goes in v4:
time: 362 us; the launch traced here: 359 us
  blocking collectives  140 us (39%)
  waiting for transfers between devices  140 us (39%)
  matrix products  39.4 us (11%)
  between operations  13.6 us (4%)
  other arithmetic  11.4 us (3%)
  starting transfers between devices  8.71 us (2%)
  local copies, waits for them, and re-layouts  6.44 us (2%)
    all_to_all x1, blocking collectives, on_device(): lax.all_to_all(outbox, PG_AXES, split_axis=0, concat_axis=0, tiled=True)  135 us
    all_gather x1, waiting for transfers between devices, on_device(): packed_all = lax.all_gather(packed, PG_AXES, axis=0, tiled=False)  132 us
    all_to_all x1, starting transfers between devices, on_device(): lax.all_to_all(half_out.reshape(pg_size, slot_cap, half_width), PG_AXES,...  8.21 us
    ppermute x2, waiting for transfers between devices, swap_kv(): return lax.ppermute(values, 'kv', perm=[(0, 1), (1, 0)])  7.97 us
  transfers between devices with their start and end apart: 4, of which 2 were waited for; matrix products, arithmetic and copies ran while one was open for 8% of the time, Pallas kernels for 0%

profile of v4, /device:TPU:2, one launch (start us, length us, event | category | flops | bytes accessed | tf_op | source)
XLA Modules:
  0.0 359.5 jit_solution(15841248711372504677)
XLA Ops:
  6.5 0.0 copy-start
  6.5 0.0 all-gather.3.cloned.1.call-start
  6.5 1.4 convert_element_type.77
  7.9 0.0 copy-start.2
  7.9 1.8 multiply_reduce_fusion
  9.7 0.0 copy-start.8
  9.7 0.8 copy.39
  10.5 0.1 eq.98
  10.6 0.4 fusion.24
  11.0 0.1 convert_element_type.72
  11.2 0.1 copy.40
  11.2 0.7 broadcast_add_fusion
  11.9 0.8 dynamic-slice.5
  12.7 1.7 convert_reduce_fusion
  14.4 1.6 convolution_convert_fusion.2
  16.0 0.0 copy-done.2
  16.0 0.0 copy-done.8
  16.0 134.8 %all_to_all.10 = bf16[128,16,1280]{2,1,0:T(8,128)(2,1)} all-to-all(bf16[128,16,1280]{2,1,0:T(8,128)(2,1)S(1)} %bitcast.46), channel_id=1, replica_groups=mesh['kv'=2,'px'=4,'pz'=8,'py'=4] {'px','pz','py'}, dimensions={0} | all-to-all | bytes 10485760 | tf_op jit(solution)/shard_map/all_to_all | solution.py:123
  150.8 0.0 collective-permute-start
  150.8 4.5 %constant_dynamic-slice_fusion = (bf16[1,1280,2,384]{3,2,1,0:T(2,128)(2,1)S(1)}, bf16[1,1280,2,384]{3,2,1,0:T(2,128)(2,1)S(1)}) fusion(bf16[1,2560,2,384]{3,2,1,0:T(2,128)(2,1)} %param.18, s32[]{:T(128)S(6)} %select_n.28, s32[]{:T(128)S(6)} %select_n.27), kind=kLoop, calls=%fused_computation.66 | loop fusion | bytes 7864328 | tf_op jit(solution)/shard_map/dynamic_slice | solution.py:26
  155.3 6.2 %fusion.16 = f32[2048,2,384]{2,0,1:T(8,128)S(1)} fusion(bf16[2048,1280,1]{1,0,2:T(8,128)(2,1)} %bitcast.2, bf16[1,1280,2,384]{3,2,1,0:T(2,128)(2,1)S(1)} %get-tuple-element.10), kind=kOutput, calls=%fused_computation.28 | convolution fusion | flops 4026531840 | bytes 13500416 | tf_op jit(solution)/shard_map/rd,dgf->rgf/dot_general | solution.py:29
  161.6 0.0 collective-permute-done
  161.6 6.3 %fusion.2 = f32[2048,2,384]{2,0,1:T(8,128)S(1)} fusion(f32[2048,2,384]{2,0,1:T(8,128)S(1)} %fusion.16, bf16[2048,1280]{1,0:T(8,128)(2,1)} %collective-permute-done, bf16[1,1280,2,384]{3,2,1,0:T(2,128)(2,1)S(1)} %get-tuple-element.9), kind=kOutput, calls=%fused_computation.14 | convolution fusion | flops 4028104704 | bytes 19791872 | tf_op jit(solution)/shard_map/rd,dgf->rgf/dot_general | solution.py:31
  167.9 0.9 fusion.5
  168.8 0.0 copy-done
  168.8 0.0 copy-start.5
  168.8 0.0 copy-start.4
  168.8 4.6 %convolution_convert_fusion = bf16[2048,1280]{1,0:T(8,128)(2,1)} fusion(bf16[2048,1,384]{2,0,1:T(8,128)(2,1)S(1)} %fusion.5, bf16[1,384,2560]{2,1,0:T(8,128)(2,1)S(1)} %copy-done, s32[]{:T(128)S(6)} %select_n.28), kind=kOutput, calls=%fused_computation.1 | convolution fusion | flops 2015887360 | bytes 7798788 | tf_op jit(solution)/shard_map/dot_general | solution.py:36
  173.4 0.5 collective-permute-start.1
  173.9 0.0 copy-done.5
  173.9 0.0 copy-done.4
  173.9 0.6 pad_maximum_fusion
  174.5 0.0 all-gather.3.cloned.1.call-update
  174.5 8.0 %collective-permute-done.1 = bf16[2048,1280]{1,0:T(8,128)(2,1)} collective-permute-done((bf16[2048,1280]{1,0:T(8,128)(2,1)}, bf16[2048,1280]{1,0:T(8,128)(2,1)}, u32[]{:S(2)}, u32[]{:S(2)}) %collective-permute-start.1) | collective-permute-done | bytes 5242912 | tf_op jit(solution)/shard_map/ppermute | solution.py:17
  182.5 6.3 %add_convert_fusion = bf16[2048,1280]{1,0:T(8,128)(2,1)} fusion(bf16[2048,1280]{1,0:T(8,128)(2,1)} %collective-permute-done.1, bf16[2048,1,384]{2,0,1:T(8,128)(2,1)S(1)} %fusion.5, bf16[1,384,2560]{2,1,0:T(8,128)(2,1)S(1)} %copy-done, s32[]{:T(128)S(6)} %select_n.27), kind=kOutput, calls=%fused_computation | convolution fusion | flops 2026373120 | bytes 13041668 | tf_op jit(solution)/shard_map/dot_general | solution.py:40
  188.8 8.2 %all-to-all-start.1 = ((bf16[128,16,1280]{2,1,0:T(8,128)(2,1)}), bf16[128,16,1280]{2,1,0:T(8,128)(2,1)}, u32[]{:S(2)}, u32[]{:S(2)}) async-start(bf16[128,16,1280]{2,1,0:T(8,128)(2,1)} %bitcast.47), calls=%async_computation.1 | async-start | bytes 10485760 | tf_op jit(solution)/shard_map/all_to_all | solution.py:126
  197.0 0.0 copy-done.7
  197.0 0.0 copy-done.10
  197.1 0.2 select_reduce_fusion.2
  197.2 0.7 broadcast_compare_fusion
  197.9 3.4 select_reduce_fusion
  201.4 131.6 %all-gather.3.cloned.1.call-done = bf16[2048,1280]{1,0:T(8,128)(2,1)} async-done(((bf16[16,1280]{1,0:T(8,128)(2,1)}), bf16[2048,1280]{1,0:T(8,128)(2,1)}) %all-gather.3.cloned.1.call-update) | async-done | bytes 5242896 | tf_op jit(solution)/shard_map/all_gather | solution.py:124
  333.0 2.9 fusion.22
  335.8 5.5 %all-reduce.1 = bf16[128,128,8]{0,2,1:T(8,128)(2,1)} all-reduce(f32[128,128,8]{0,2,1:T(8,128)S(1)} %fusion.22), channel_id=1, replica_groups=mesh['kv'=2,'px'=4,'pz'=8,'py'=4] {'kv'}, use_global_device_ids=true, to_apply=%region_7.8 | all-reduce | flops 131072 | bytes 786432 | tf_op jit(solution)/shard_map/psum | solution.py:148
  341.4 3.3 fusion.10
  344.6 0.0 all-to-all-done.1
  344.6 3.8 %fusion.32 = f32[128,1280]{1,0:T(8,128)S(1)} fusion(bf16[2048,1280]{1,0:T(8,128)(2,1)} %bitcast.10, f32[128,2048]{1,0:T(8,128)} %get-tuple-element.6, f32[128,2048]{1,0:T(8,128)S(1)} %get-tuple-element.5), kind=kOutput, calls=%fused_computation.50 | convolution fusion | flops 671612928 | bytes 7995392 | tf_op jit(solution)/shard_map/dot_general | solution.py:84
  348.5 4.2 %fusion.13 = bf16[128,1280]{1,0:T(8,128)(2,1)} fusion(f32[128,1280]{1,0:T(8,128)S(1)} %copy-done.3, f32[128,1280]{1,0:T(8,128)S(1)} %fusion.32, bf16[2048,1280]{1,0:T(8,128)(2,1)} %bitcast.10, f32[128,2048]{1,0:T(8,128)S(1)} %copy-done.1, f32[128,2048]{1,0:T(8,128)S(1)} %get-tuple-element.5), kind=kOutput, calls=%fused_computation.24 | convolution fusion | flops 672890880 | bytes 8978432 | tf_op jit(solution)/shard_map/dot_general | solution.py:84
  (13 shorter events, 0.0 us)
Async XLA Ops:
  6.5 162.3 %copy-start = (bf16[1,384,2560]{2,1,0:T(8,128)(2,1)S(1)}, bf16[1,384,2560]{2,1,0:T(8,128)(2,1)}, u32[]{:S(2)}) copy-start(bf16[1,384,2560]{2,1,0:T(8,128)(2,1)} %param.19) | copy-start | bytes 5898244
  6.5 326.4 %all-gather.3.cloned.1.call-start = ((), (), s32[]{:S(2)}) async-start(), calls=%async_computation.2 | async-start | bytes 5283840 | tf_op jit(solution)/shard_map/all_gather | solution.py:124
  7.9 8.1 %copy-start.2 = (f32[128,2560]{1,0:T(8,128)}, f32[128,2560]{1,0:T(8,128)S(1)}, u32[]{:S(2)}) copy-start(f32[128,2560]{1,0:T(8,128)S(1)} %convert_element_type.77) | copy-start | bytes 3932164
  9.7 6.3 %copy-start.8 = (f32[128]{0:T(128)}, f32[128]{0:T(128)S(1)}, u32[]{:S(2)}) copy-start(f32[128]{0:T(128)S(1)} %add_rsqrt_fusion) | copy-start | bytes 1540
  150.8 10.7 %collective-permute-start = (bf16[2048,1280]{1,0:T(8,128)(2,1)}, bf16[2048,1280]{1,0:T(8,128)(2,1)}, u32[]{:S(2)}, u32[]{:S(2)}) collective-permute-start(bf16[2048,1280]{1,0:T(8,128)(2,1)} %bitcast.1), channel_id=1, source_target_pairs={{0,128},{128,0},{1,129},{129,1},{2,130},{130,2},{3,131},{131,3},{4... | collective-permute-start | bytes 15728648 | tf_op jit(solution)/shard_map/ppermute | solution.py:17
  168.8 5.1 %copy-start.5 = (bf16[1,2560,8]{1,2,0:T(8,128)(2,1)S(1)}, bf16[1,2560,8]{1,2,0:T(8,128)(2,1)}, u32[]{:S(2)}) copy-start(bf16[1,2560,8]{1,2,0:T(8,128)(2,1)} %param.20) | copy-start | bytes 122884
  168.8 5.1 %copy-start.4 = (bf16[1,8,1280]{2,1,0:T(8,128)(2,1)S(1)}, bf16[1,8,1280]{2,1,0:T(8,128)(2,1)}, u32[]{:S(2)}) copy-start(bf16[1,8,1280]{2,1,0:T(8,128)(2,1)} %param.21) | copy-start | bytes 61444
  173.4 9.1 %collective-permute-start.1 = (bf16[2048,1280]{1,0:T(8,128)(2,1)}, bf16[2048,1280]{1,0:T(8,128)(2,1)}, u32[]{:S(2)}, u32[]{:S(2)}) collective-permute-start(bf16[2048,1280]{1,0:T(8,128)(2,1)} %convolution_convert_fusion), channel_id=1, source_target_pairs={{0,128},{128,0},{1,129},{129,1},{2,130},{130,2},{3,131},{131,3},{4... | collective-permute-start | bytes 15728648 | tf_op jit(solution)/shard_map/ppermute | solution.py:17
  188.8 8.2 %copy-start.7 = (s32[256]{0:T(256)S(1)}, s32[256]{0:T(256)}, u32[]{:S(2)}) copy-start(s32[256]{0:T(256)} %param.16) | copy-start | bytes 3076
  188.8 8.2 %copy-start.10 = (s32[128]{0:T(128)S(1)}, s32[128]{0:T(128)}, u32[]{:S(2)}) copy-start(s32[128]{0:T(128)} %param.15) | copy-start | bytes 1540
  188.8 8.4 %copy-start.9 = (s32[128]{0:T(128)S(1)}, s32[128]{0:T(128)}, u32[]{:S(2)}) copy-start(s32[128]{0:T(128)} %param.17) | copy-start | bytes 1540
  188.8 9.1 %copy-start.6 = (f32[128,6]{0,1:T(8,128)S(1)}, f32[128,6]{0,1:T(8,128)}, u32[]{:S(2)}) copy-start(f32[128,6]{0,1:T(8,128)} %param.14) | copy-start | bytes 9220
  188.8 155.8 %all-to-all-start.1 = ((bf16[128,16,1280]{2,1,0:T(8,128)(2,1)}), bf16[128,16,1280]{2,1,0:T(8,128)(2,1)}, u32[]{:S(2)}, u32[]{:S(2)}) async-start(bf16[128,16,1280]{2,1,0:T(8,128)(2,1)} %bitcast.47), calls=%async_computation.1 | async-start | bytes 10485760 | tf_op jit(solution)/shard_map/all_to_all | solution.py:126
  344.6 3.8 %copy-start.1 = (f32[128,2048]{1,0:T(8,128)S(1)}, f32[128,2048]{1,0:T(8,128)}, u32[]{:S(2)}) copy-start(f32[128,2048]{1,0:T(8,128)} %get-tuple-element.6) | copy-start | bytes 3145732
  344.6 3.8 %copy-start.3 = (f32[128,1280]{1,0:T(8,128)S(1)}, f32[128,1280]{1,0:T(8,128)}, u32[]{:S(2)}) copy-start(f32[128,1280]{1,0:T(8,128)} %fusion.10) | copy-start | bytes 1966084
Sparse Core Ops, SparseCore 0:
  174.7 158.2 all-gather.2

commit v5 on v4

--- a/solution.py
+++ b/solution.py
@@ -122,6 +122,7 @@
     )
     inbox_half = lax.all_to_all(outbox, PG_AXES, split_axis=0, concat_axis=0, tiled=True)
     packed_all = lax.all_gather(packed, PG_AXES, axis=0, tiled=False)
+    inbox_half, packed_all = lax.optimization_barrier((inbox_half, packed_all))
     half_out = expert_half(inbox_half.reshape(pg_size * slot_cap, half_width), expert_gate_up_weight, expert_down_weight)
     results = lax.all_to_all(
         half_out.reshape(pg_size, slot_cap, half_width),

time: 362 us -> 357 us (0.986)
  blocking collectives: 140 us -> 5.54 us
  waiting for transfers between devices: 140 us -> 250 us
  starting transfers between devices: 8.71 us -> 28.8 us
    all_to_all x1 -> x0, blocking collectives: 135 us -> none  [on_device(): lax.all_to_all(outbox, PG_AXES, split_axis=0, concat_axis=0, tiled=True)]
    all_to_all x1, waiting for transfers between devices: 0.01 us -> 104 us  [on_device(): lax.all_to_all(half_out.reshape(pg_size, slot_cap, half_width), PG_AXES,...]
    all_to_all x0 -> x1, starting transfers between devices: none -> 15.9 us  [on_device(): lax.all_to_all(outbox, PG_AXES, split_axis=0, concat_axis=0, tiled=True)]
    all_gather x1, waiting for transfers between devices: 132 us -> 137 us  [on_device(): packed_all = lax.all_gather(packed, PG_AXES, axis=0, tiled=False)]
    all_to_all x1, starting transfers between devices: 8.21 us -> 12.3 us  [on_device(): lax.all_to_all(half_out.reshape(pg_size, slot_cap, half_width), PG_AXES,...]
  transfers between devices with their start and end apart: 4 -> 5, of which waited for: 2 -> 4; matrix products, arithmetic and copies ran while one was open for 8% -> 9% of each run, Pallas kernels for 0% -> 0%
where the time goes in v5:
time: 357 us; the launch traced here: 356 us
  waiting for transfers between devices  250 us (70%)
  matrix products  38.6 us (11%)
  starting transfers between devices  28.8 us (8%)
  between operations  13.6 us (4%)
  other arithmetic  12 us (3%)
  local copies, waits for them, and re-layouts  7.29 us (2%)
  blocking collectives  5.54 us (2%)
    all_gather x1, waiting for transfers between devices, on_device(): packed_all = lax.all_gather(packed, PG_AXES, axis=0, tiled=False)  137 us
    all_to_all x1, waiting for transfers between devices, on_device(): lax.all_to_all(half_out.reshape(pg_size, slot_cap, half_width), PG_AXES,...  104 us
    all_to_all x1, starting transfers between devices, on_device(): lax.all_to_all(outbox, PG_AXES, split_axis=0, concat_axis=0, tiled=True)  15.9 us
    all_to_all x1, starting transfers between devices, on_device(): lax.all_to_all(half_out.reshape(pg_size, slot_cap, half_width), PG_AXES,...  12.3 us
    ppermute x2, waiting for transfers between devices, swap_kv(): return lax.ppermute(values, 'kv', perm=[(0, 1), (1, 0)])  8.29 us
  transfers between devices with their start and end apart: 5, of which 4 were waited for; matrix products, arithmetic and copies ran while one was open for 9% of the time, Pallas kernels for 0%

profile of v5, /device:TPU:2, one launch (start us, length us, event | category | flops | bytes accessed | tf_op | source)
XLA Modules:
  0.0 356.2 jit_solution(14973037867539011406)
XLA Ops:
  6.5 0.0 copy-start
  6.5 0.0 all-gather.3.cloned.1.call-start
  6.5 0.9 dynamic-slice_bitcast_fusion
  7.4 1.3 pad_maximum_fusion
  8.8 0.0 all-gather.3.cloned.1.call-update
  8.8 1.2 convert_element_type.77
  10.0 0.0 copy-start.2
  10.0 1.8 multiply_reduce_fusion
  11.8 0.8 copy.39
  12.6 0.1 eq.98
  12.7 0.4 fusion.28
  13.1 0.1 convert_element_type.72
  13.3 0.1 copy.40
  13.3 0.7 broadcast_add_fusion
  14.0 0.8 dynamic-slice.5
  14.8 1.7 convert_reduce_fusion
  16.5 4.0 %convolution_convert_fusion.2 = bf16[2048,1280]{1,0:T(8,128)(2,1)} fusion(f32[2048,128]{1,0:T(8,128)S(1)} %get-tuple-element.16, f32[2048,128]{1,0:T(8,128)S(1)} %get-tuple-element.15, f32[128,2560]{1,0:T(8,128)S(1)} %convert_element_type.77, s32[]{:T(128)S(6)} %select_n.27, f32[1280]{0:T(1024)S(1)} %dynamic-slice.5, f32[128]{0:T(128)S(1)} %add_rsqrt_fusion), kind=kOutput, calls=%fused_computation.3 | convolution fusion | flops 674725888 | bytes 8004100 | tf_op jit(solution)/shard_map/dot_general | solution.py:68
  20.5 0.0 copy-done.2
  20.5 15.9 %all-to-all-start = ((bf16[128,16,1280]{2,1,0:T(8,128)(2,1)}), bf16[128,16,1280]{2,1,0:T(8,128)(2,1)}, u32[]{:S(2)}, u32[]{:S(2)}) async-start(bf16[128,16,1280]{2,1,0:T(8,128)(2,1)} %bitcast.46), calls=%async_computation | async-start | bytes 10485760 | tf_op jit(solution)/shard_map/all_to_all | solution.py:123
  36.4 137.1 %all-gather.3.cloned.1.call-done = bf16[2048,1280]{1,0:T(8,128)(2,1)} async-done(((bf16[16,1280]{1,0:T(8,128)(2,1)}), bf16[2048,1280]{1,0:T(8,128)(2,1)}) %all-gather.3.cloned.1.call-update) | async-done | bytes 5242896 | tf_op jit(solution)/shard_map/all_gather | solution.py:124
  173.5 0.7 all-to-all-done
  174.2 0.0 collective-permute-start
  174.2 4.5 %constant_dynamic-slice_fusion = (bf16[1,1280,2,384]{3,2,1,0:T(2,128)(2,1)S(1)}, bf16[1,1280,2,384]{3,2,1,0:T(2,128)(2,1)S(1)}) fusion(bf16[1,2560,2,384]{3,2,1,0:T(2,128)(2,1)} %param.18, s32[]{:T(128)S(6)} %select_n.28, s32[]{:T(128)S(6)} %select_n.27), kind=kLoop, calls=%fused_computation.67 | loop fusion | bytes 7864328 | tf_op jit(solution)/shard_map/dynamic_slice | solution.py:26
  178.7 6.2 %fusion.18 = f32[2048,2,384]{2,0,1:T(8,128)S(1)} fusion(bf16[2048,1280,1]{1,0,2:T(8,128)(2,1)} %bitcast.6, bf16[1,1280,2,384]{3,2,1,0:T(2,128)(2,1)S(1)} %get-tuple-element.14), kind=kOutput, calls=%fused_computation.29 | convolution fusion | flops 4026531840 | bytes 13500416 | tf_op jit(solution)/shard_map/rd,dgf->rgf/dot_general | solution.py:29
  184.9 0.0 collective-permute-done
  184.9 6.3 %fusion.2 = f32[2048,2,384]{2,0,1:T(8,128)S(1)} fusion(f32[2048,2,384]{2,0,1:T(8,128)S(1)} %fusion.18, bf16[2048,1280]{1,0:T(8,128)(2,1)} %collective-permute-done, bf16[1,1280,2,384]{3,2,1,0:T(2,128)(2,1)S(1)} %get-tuple-element.13), kind=kOutput, calls=%fused_computation.14 | convolution fusion | flops 4028104704 | bytes 19791872 | tf_op jit(solution)/shard_map/rd,dgf->rgf/dot_general | solution.py:31
  191.2 0.9 fusion.5
  192.2 0.0 copy-done
  192.2 3.1 convolution_convert_fusion
  195.3 0.6 collective-permute-start.1
  195.9 8.3 %collective-permute-done.1 = bf16[2048,1280]{1,0:T(8,128)(2,1)S(1)} collective-permute-done((bf16[2048,1280]{1,0:T(8,128)(2,1)S(1)}, bf16[2048,1280]{1,0:T(8,128)(2,1)S(1)}, u32[]{:S(2)}, u32[]{:S(2)}) %collective-permute-start.1) | collective-permute-done | bytes 5242912 | tf_op jit(solution)/shard_map/ppermute | solution.py:17
  204.1 4.5 %add_convert_fusion = bf16[2048,1280]{1,0:T(8,128)(2,1)} fusion(bf16[2048,1280]{1,0:T(8,128)(2,1)S(1)} %collective-permute-done.1, bf16[2048,1,384]{2,0,1:T(8,128)(2,1)S(1)} %fusion.5, bf16[1,384,2560]{2,1,0:T(8,128)(2,1)S(1)} %copy-done, s32[]{:T(128)S(6)} %select_n.27), kind=kOutput, calls=%fused_computation | convolution fusion | flops 2026373120 | bytes 13041668 | tf_op jit(solution)/shard_map/dot_general | solution.py:40
  208.7 12.3 %all-to-all-start.1 = ((bf16[128,16,1280]{2,1,0:T(8,128)(2,1)}), bf16[128,16,1280]{2,1,0:T(8,128)(2,1)}, u32[]{:S(2)}, u32[]{:S(2)}) async-start(bf16[128,16,1280]{2,1,0:T(8,128)(2,1)} %bitcast.47), calls=%async_computation.1 | async-start | bytes 10485760 | tf_op jit(solution)/shard_map/all_to_all | solution.py:127
  221.0 0.0 copy-done.5
  221.0 0.0 copy-done.7
  221.0 0.2 select_reduce_fusion.2
  221.2 0.0 copy-done.6
  221.2 0.7 broadcast_compare_fusion
  221.9 0.0 copy-done.4
  221.9 3.4 select_reduce_fusion
  225.3 2.9 fusion.24
  228.2 5.5 %all-reduce.1 = bf16[128,128,8]{0,2,1:T(8,128)(2,1)} all-reduce(f32[128,128,8]{0,2,1:T(8,128)S(1)} %fusion.24), channel_id=1, replica_groups=mesh['kv'=2,'px'=4,'pz'=8,'py'=4] {'kv'}, use_global_device_ids=true, to_apply=%region_7.8 | all-reduce | flops 131072 | bytes 786432 | tf_op jit(solution)/shard_map/psum | solution.py:149
  233.7 3.2 fusion.12
  237.0 104.4 %all-to-all-done.1 = bf16[128,16,1280]{2,1,0:T(8,128)(2,1)} async-done(((bf16[128,16,1280]{2,1,0:T(8,128)(2,1)}), bf16[128,16,1280]{2,1,0:T(8,128)(2,1)}, u32[]{:S(2)}, u32[]{:S(2)}) %all-to-all-start.1) | async-done | bytes 5242912 | tf_op jit(solution)/shard_map/all_to_all | solution.py:127
  341.4 3.8 %fusion.36 = f32[128,1280]{1,0:T(8,128)S(1)} fusion(bf16[2048,1280]{1,0:T(8,128)(2,1)} %bitcast.14, f32[128,2048]{1,0:T(8,128)} %get-tuple-element.10, f32[128,2048]{1,0:T(8,128)S(1)} %get-tuple-element.9), kind=kOutput, calls=%fused_computation.51 | convolution fusion | flops 671612928 | bytes 7995392 | tf_op jit(solution)/shard_map/dot_general | solution.py:84
  345.2 0.0 copy-done.1
  345.2 0.0 copy-done.3
  345.2 4.2 %fusion.15 = bf16[128,1280]{1,0:T(8,128)(2,1)} fusion(f32[128,1280]{1,0:T(8,128)S(1)} %copy-done.3, f32[128,1280]{1,0:T(8,128)S(1)} %fusion.36, bf16[2048,1280]{1,0:T(8,128)(2,1)} %bitcast.14, f32[128,2048]{1,0:T(8,128)S(1)} %copy-done.1, f32[128,2048]{1,0:T(8,128)S(1)} %get-tuple-element.9), kind=kOutput, calls=%fused_computation.25 | convolution fusion | flops 672890880 | bytes 8978432 | tf_op jit(solution)/shard_map/dot_general | solution.py:84
  (8 shorter events, 0.0 us)
Async XLA Ops:
  6.5 185.6 %copy-start = (bf16[1,384,2560]{2,1,0:T(8,128)(2,1)S(1)}, bf16[1,384,2560]{2,1,0:T(8,128)(2,1)}, u32[]{:S(2)}) copy-start(bf16[1,384,2560]{2,1,0:T(8,128)(2,1)} %param.19) | copy-start | bytes 5898244
  6.5 167.0 %all-gather.3.cloned.1.call-start = ((), (), s32[]{:S(2)}) async-start(), calls=%async_computation.2 | async-start | bytes 5283840 | tf_op jit(solution)/shard_map/all_gather | solution.py:124
  10.0 10.5 %copy-start.2 = (f32[128,2560]{1,0:T(8,128)}, f32[128,2560]{1,0:T(8,128)S(1)}, u32[]{:S(2)}) copy-start(f32[128,2560]{1,0:T(8,128)S(1)} %convert_element_type.77) | copy-start | bytes 3932164
  20.5 153.7 %all-to-all-start = ((bf16[128,16,1280]{2,1,0:T(8,128)(2,1)}), bf16[128,16,1280]{2,1,0:T(8,128)(2,1)}, u32[]{:S(2)}, u32[]{:S(2)}) async-start(bf16[128,16,1280]{2,1,0:T(8,128)(2,1)} %bitcast.46), calls=%async_computation | async-start | bytes 10485760 | tf_op jit(solution)/shard_map/all_to_all | solution.py:123
  174.2 10.7 %collective-permute-start = (bf16[2048,1280]{1,0:T(8,128)(2,1)}, bf16[2048,1280]{1,0:T(8,128)(2,1)}, u32[]{:S(2)}, u32[]{:S(2)}) collective-permute-start(bf16[2048,1280]{1,0:T(8,128)(2,1)} %bitcast.5), channel_id=1, source_target_pairs={{0,128},{128,0},{1,129},{129,1},{2,130},{130,2},{3,131},{131,3},{4... | collective-permute-start | bytes 15728648 | tf_op jit(solution)/shard_map/ppermute | solution.py:17
  195.3 8.9 %collective-permute-start.1 = (bf16[2048,1280]{1,0:T(8,128)(2,1)S(1)}, bf16[2048,1280]{1,0:T(8,128)(2,1)S(1)}, u32[]{:S(2)}, u32[]{:S(2)}) collective-permute-start(bf16[2048,1280]{1,0:T(8,128)(2,1)S(1)} %convolution_convert_fusion), channel_id=1, source_target_pairs={{0,128},{128,0},{1,129},{129,1},{2,130},{130,2},{3,131},{131,3},{4... | collective-permute-start | bytes 15728648 | tf_op jit(solution)/shard_map/ppermute | solution.py:17
  208.7 12.3 %copy-start.5 = (s32[256]{0:T(256)S(1)}, s32[256]{0:T(256)}, u32[]{:S(2)}) copy-start(s32[256]{0:T(256)} %param.16) | copy-start | bytes 3076
  208.7 12.3 %copy-start.7 = (s32[128]{0:T(128)S(1)}, s32[128]{0:T(128)}, u32[]{:S(2)}) copy-start(s32[128]{0:T(128)} %param.15) | copy-start | bytes 1540
  208.7 12.5 %copy-start.6 = (s32[128]{0:T(128)S(1)}, s32[128]{0:T(128)}, u32[]{:S(2)}) copy-start(s32[128]{0:T(128)} %param.17) | copy-start | bytes 1540
  208.7 13.2 %copy-start.4 = (f32[128,6]{0,1:T(8,128)S(1)}, f32[128,6]{0,1:T(8,128)}, u32[]{:S(2)}) copy-start(f32[128,6]{0,1:T(8,128)} %param.14) | copy-start | bytes 9220
  208.7 132.7 %all-to-all-start.1 = ((bf16[128,16,1280]{2,1,0:T(8,128)(2,1)}), bf16[128,16,1280]{2,1,0:T(8,128)(2,1)}, u32[]{:S(2)}, u32[]{:S(2)}) async-start(bf16[128,16,1280]{2,1,0:T(8,128)(2,1)} %bitcast.47), calls=%async_computation.1 | async-start | bytes 10485760 | tf_op jit(solution)/shard_map/all_to_all | solution.py:127
  341.4 3.8 %copy-start.1 = (f32[128,2048]{1,0:T(8,128)S(1)}, f32[128,2048]{1,0:T(8,128)}, u32[]{:S(2)}) copy-start(f32[128,2048]{1,0:T(8,128)} %get-tuple-element.10) | copy-start | bytes 3145732
  341.4 3.8 %copy-start.3 = (f32[128,1280]{1,0:T(8,128)S(1)}, f32[128,1280]{1,0:T(8,128)}, u32[]{:S(2)}) copy-start(f32[128,1280]{1,0:T(8,128)} %fusion.12) | copy-start | bytes 1966084
Sparse Core Ops, SparseCore 0:
  10.8 162.6 all-gather.2

commit v6 on v5

--- a/solution.py
+++ b/solution.py
@@ -11,6 +11,34 @@
     values = states.astype(jnp.float32)
     inverse_rms = lax.rsqrt(jnp.mean(values * values, axis=-1, keepdims=True) + 1e-06)
     return (values * inverse_rms * gain_vector).astype(jnp.bfloat16)
+
+
+def shift_gather(block, axis_name):
+    count = lax.axis_size(axis_name)
+    pieces = [block]
+    for shift in range(1, count):
+        pieces.append(
+            lax.ppermute(
+                block, axis_name, perm=[(j, (j + shift) % count) for j in range(count)]
+            )
+        )
+    return jnp.stack(pieces)
+
+
+def gathered_slot_order(axis_order):
+    sizes = {name: lax.axis_size(name) for name in PG_AXES}
+    grids = jnp.meshgrid(
+        *[jnp.arange(sizes[name], dtype=jnp.int32) for name in reversed(axis_order)],
+        indexing="ij",
+    )
+    source = {}
+    for name, offsets in zip(reversed(axis_order), grids):
+        own = lax.axis_index(name).astype(jnp.int32)
+        source[name] = (own - offsets) % sizes[name]
+    slot = jnp.zeros_like(grids[0])
+    for name in PG_AXES:
+        slot = slot * sizes[name] + source[name]
+    return slot.reshape(-1)
 
 
 def swap_kv(values):
@@ -121,7 +149,12 @@
         pg_size, slot_cap, half_width
     )
     inbox_half = lax.all_to_all(outbox, PG_AXES, split_axis=0, concat_axis=0, tiled=True)
-    packed_all = lax.all_gather(packed, PG_AXES, axis=0, tiled=False)
+    gather_order = ("pz", "py", "px")
+    packed_all = packed
+    for axis_name in gather_order:
+        packed_all = shift_gather(packed_all, axis_name)
+    packed_all = packed_all.reshape((pg_size,) + packed.shape)
+    adapter_of_position = adapter_of_slot[gathered_slot_order(gather_order)]
     inbox_half, packed_all = lax.optimization_barrier((inbox_half, packed_all))
     half_out = expert_half(inbox_half.reshape(pg_size * slot_cap, half_width), expert_gate_up_weight, expert_down_weight)
     results = lax.all_to_all(
@@ -147,7 +180,7 @@
         own_features, down_all, (((1,), (1,)), ((), ())), preferred_element_type=jnp.float32
     )
     rank_projected = lax.psum(partial_rank, "kv").reshape(tok_rows, slot_count, rank_half)
-    matched = adapter_of_slot[None, :, None] == token_adapter[:, None, None]
+    matched = adapter_of_position[None, :, None] == token_adapter[:, None, None]
     rank_projected = jnp.where(matched, rank_projected, 0.0).astype(jnp.bfloat16)
     flat_low = rank_projected.reshape(tok_rows, slot_count * rank_half)
     adapter_total_output = jnp.dot(flat_low, up_all, preferred_element_type=jnp.float32)

time: 357 us -> 409 us (1.15)
  waiting for transfers between devices: 250 us -> 289 us
  starting transfers between devices: 28.8 us -> 51.5 us
  between operations: 13.6 us -> 0.36 us
    ppermute x0 -> x13, waiting for transfers between devices: none -> 178 us  [shift_gather(): lax.ppermute(block, axis_name, perm=[(j, (j + shift) % count) for j in ra...]
    all_gather x1 -> x0, waiting for transfers between devices: 137 us -> none  [on_device(): packed_all = lax.all_gather(packed, PG_AXES, axis=0, tiled=False)]
    ppermute x0 -> x13, starting transfers between devices: none -> 23.7 us  [shift_gather(): lax.ppermute(block, axis_name, perm=[(j, (j + shift) % count) for j in ra...]
  transfers between devices with their start and end apart: 5 -> 17, of which waited for: 4 -> 11; matrix products, arithmetic and copies ran while one was open for 9% -> 6% of each run, Pallas kernels for 0% -> 0%
where the time goes in v6:
time: 409 us; the launch traced here: 408 us
  waiting for transfers between devices  289 us (71%)
  starting transfers between devices  51.5 us (13%)
  matrix products  40 us (10%)
  other arithmetic  14.5 us (4%)
  local copies, waits for them, and re-layouts  7.42 us (2%)
  blocking collectives  5.32 us (1%)
    ppermute x13, waiting for transfers between devices, shift_gather(): lax.ppermute(block, axis_name, perm=[(j, (j + shift) % count) for j in ra...  178 us
    all_to_all x1, waiting for transfers between devices, on_device(): lax.all_to_all(half_out.reshape(pg_size, slot_cap, half_width), PG_AXES,...  103 us
    ppermute x13, starting transfers between devices, shift_gather(): lax.ppermute(block, axis_name, perm=[(j, (j + shift) % count) for j in ra...  23.7 us
    all_to_all x1, starting transfers between devices, on_device(): lax.all_to_all(outbox, PG_AXES, split_axis=0, concat_axis=0, tiled=True)  16.1 us
    all_to_all x1, starting transfers between devices, on_device(): lax.all_to_all(half_out.reshape(pg_size, slot_cap, half_width), PG_AXES,...  11.1 us
    ppermute x2, waiting for transfers between devices, swap_kv(): return lax.ppermute(values, 'kv', perm=[(0, 1), (1, 0)])  8.29 us
  transfers between devices with their start and end apart: 17, of which 11 were waited for; matrix products, arithmetic and copies ran while one was open for 6% of the time, Pallas kernels for 0%

profile of v6, /device:TPU:2, one launch (start us, length us, event | category | flops | bytes accessed | tf_op | source)
XLA Modules:
  0.0 407.9 jit_solution(4808004316504737649)
XLA Ops:
  0.0 2.4 convert_element_type.77
  2.4 1.3 multiply_reduce_fusion
  3.7 0.8 copy.41
  4.7 0.4 fusion.28
  5.3 2.7 convert_reduce_fusion
  8.0 5.4 %convolution_convert_fusion.2 = bf16[2048,1280]{1,0:T(8,128)(2,1)} fusion(f32[2048,128]{1,0:T(8,128)} %get-tuple-element.18, f32[2048,128]{1,0:T(8,128)S(1)} %get-tuple-element.17, f32[128,2560]{1,0:T(8,128)} %convert_element_type.77, s32[]{:T(128)S(6)} %select_n.76, f32[1280]{0:T(1024)S(1)} %dynamic-slice.5, f32[128]{0:T(128)S(1)} %add_rsqrt_fusion), kind=kOutput, calls=%fused_computation.4 | convolution fusion | flops 674725888 | bytes 8001028 | tf_op jit(solution)/shard_map/dot_general | solution.py:96
  13.4 16.1 %all-to-all-start = ((bf16[128,16,1280]{2,1,0:T(8,128)(2,1)}), bf16[128,16,1280]{2,1,0:T(8,128)(2,1)}, u32[]{:S(2)}, u32[]{:S(2)}) async-start(bf16[128,16,1280]{2,1,0:T(8,128)(2,1)} %bitcast.73), calls=%async_computation | async-start | bytes 10485760 | tf_op jit(solution)/shard_map/all_to_all | solution.py:151
  29.5 1.6 collective-permute-start
  31.1 2.4 collective-permute-start.1
  33.5 2.8 collective-permute-start.2
  36.3 2.3 collective-permute-start.3
  38.5 2.8 collective-permute-start.4
  41.3 104.8 %collective-permute-done = bf16[16,1280]{1,0:T(8,128)(2,1)S(1)} collective-permute-done((bf16[16,1280]{1,0:T(8,128)(2,1)S(1)}, bf16[16,1280]{1,0:T(8,128)(2,1)S(1)}, u32[]{:S(2)}, u32[]{:S(2)}) %collective-permute-start) | collective-permute-done | bytes 40992 | tf_op jit(solution)/shard_map/ppermute | solution.py:21
  146.1 2.0 collective-permute-start.5
  148.1 1.2 collective-permute-done.1
  149.3 0.2 collective-permute-start.6
  149.6 3.8 collective-permute-done.3
  153.4 2.8 collective-permute-start.9
  156.2 0.9 collective-permute-start.8
  157.1 0.9 collective-permute-start.7
  157.9 9.6 %collective-permute-done.9 = bf16[8,16,1280]{2,1,0:T(8,128)(2,1)S(1)} collective-permute-done((bf16[8,16,1280]{2,1,0:T(8,128)(2,1)S(1)}, bf16[8,16,1280]{2,1,0:T(8,128)(2,1)S(1)}, u32[]{:S(2)}, u32[]{:S(2)}) %collective-permute-start.9) | collective-permute-done | bytes 327712 | tf_op jit(solution)/shard_map/ppermute | solution.py:21
  167.8 3.4 collective-permute-done.7
  171.2 0.2 fusion.53
  171.4 0.5 collective-permute-start.12
  171.9 2.7 collective-permute-start.11
  174.6 2.0 collective-permute-start.10
  176.6 25.5 %collective-permute-done.12 = bf16[4,8,16,1280]{3,2,1,0:T(8,128)(2,1)S(1)} collective-permute-done((bf16[4,8,16,1280]{3,2,1,0:T(8,128)(2,1)S(1)}, bf16[4,8,16,1280]{3,2,1,0:T(8,128)(2,1)S(1)}, u32[]{:S(2)}, u32[]{:S(2)}) %collective-permute-start.12) | collective-permute-done | bytes 1310752 | tf_op jit(solution)/shard_map/ppermute | solution.py:21
  202.1 28.4 %collective-permute-done.11 = bf16[4,8,16,1280]{3,2,1,0:T(8,128)(2,1)S(1)} collective-permute-done((bf16[4,8,16,1280]{3,2,1,0:T(8,128)(2,1)S(1)}, bf16[4,8,16,1280]{3,2,1,0:T(8,128)(2,1)S(1)}, u32[]{:S(2)}, u32[]{:S(2)}) %collective-permute-start.11) | collective-permute-done | bytes 1310752 | tf_op jit(solution)/shard_map/ppermute | solution.py:21
  230.5 0.7 collective-permute-done.10
  231.2 2.6 pad_maximum_fusion
  233.8 4.5 %constant_dynamic-slice_fusion = (bf16[1,1280,2,384]{3,2,1,0:T(2,128)(2,1)S(1)}, bf16[1,1280,2,384]{3,2,1,0:T(2,128)(2,1)S(1)}) fusion(bf16[1,2560,2,384]{3,2,1,0:T(2,128)(2,1)} %param.18, s32[]{:T(128)S(6)} %select_n.77, s32[]{:T(128)S(6)} %select_n.76), kind=kLoop, calls=%fused_computation.89 | loop fusion | bytes 7864328 | tf_op jit(solution)/shard_map/dynamic_slice | solution.py:54
  238.3 6.2 %fusion.18 = f32[2048,2,384]{2,0,1:T(8,128)S(1)} fusion(bf16[2048,1280,1]{1,0,2:T(8,128)(2,1)} %bitcast.22, bf16[1,1280,2,384]{3,2,1,0:T(2,128)(2,1)S(1)} %get-tuple-element.14), kind=kOutput, calls=%fused_computation.31 | convolution fusion | flops 4026531840 | bytes 13500416 | tf_op jit(solution)/shard_map/rd,dgf->rgf/dot_general | solution.py:57
  244.6 6.3 %fusion.2 = f32[2048,2,384]{2,0,1:T(8,128)S(1)} fusion(f32[2048,2,384]{2,0,1:T(8,128)S(1)} %fusion.18, bf16[2048,1280]{1,0:T(8,128)(2,1)} %collective-permute-done.13, bf16[1,1280,2,384]{3,2,1,0:T(2,128)(2,1)S(1)} %get-tuple-element.13), kind=kOutput, calls=%fused_computation.16 | convolution fusion | flops 4028104704 | bytes 19791872 | tf_op jit(solution)/shard_map/rd,dgf->rgf/dot_general | solution.py:59
  250.9 0.9 fusion.5
  251.8 3.1 convolution_convert_fusion
  255.0 0.6 collective-permute-start.14
  255.5 8.3 %collective-permute-done.14 = bf16[2048,1280]{1,0:T(8,128)(2,1)S(1)} collective-permute-done((bf16[2048,1280]{1,0:T(8,128)(2,1)S(1)}, bf16[2048,1280]{1,0:T(8,128)(2,1)S(1)}, u32[]{:S(2)}, u32[]{:S(2)}) %collective-permute-start.14) | collective-permute-done | bytes 5242912 | tf_op jit(solution)/shard_map/ppermute | solution.py:45
  263.8 4.5 %add_convert_fusion = bf16[2048,1280]{1,0:T(8,128)(2,1)} fusion(bf16[2048,1280]{1,0:T(8,128)(2,1)S(1)} %collective-permute-done.14, bf16[2048,1,384]{2,0,1:T(8,128)(2,1)S(1)} %fusion.5, bf16[1,384,2560]{2,1,0:T(8,128)(2,1)S(1)} %copy-done, s32[]{:T(128)S(6)} %select_n.76), kind=kOutput, calls=%fused_computation.1 | convolution fusion | flops 2026373120 | bytes 13041668 | tf_op jit(solution)/shard_map/dot_general | solution.py:68
  268.3 11.1 %all-to-all-start.1 = ((bf16[128,16,1280]{2,1,0:T(8,128)(2,1)}), bf16[128,16,1280]{2,1,0:T(8,128)(2,1)}, u32[]{:S(2)}, u32[]{:S(2)}) async-start(bf16[128,16,1280]{2,1,0:T(8,128)(2,1)} %bitcast.76), calls=%async_computation.1 | async-start | bytes 10485760 | tf_op jit(solution)/shard_map/all_to_all | solution.py:160
  280.0 1.2 gather_fusion
  281.4 0.7 broadcast_compare_fusion
  282.1 3.5 select_reduce_fusion
  285.6 2.9 fusion.24
  288.4 5.3 %all-reduce.1 = bf16[128,128,8]{0,2,1:T(8,128)(2,1)} all-reduce(f32[128,128,8]{0,2,1:T(8,128)S(1)} %fusion.24), channel_id=1, replica_groups=mesh['kv'=2,'px'=4,'pz'=8,'py'=4] {'kv'}, use_global_device_ids=true, to_apply=%region_7.8 | all-reduce | flops 131072 | bytes 786432 | tf_op jit(solution)/shard_map/psum | solution.py:182
  293.8 3.3 fusion.12
  297.0 102.8 %all-to-all-done.1 = bf16[128,16,1280]{2,1,0:T(8,128)(2,1)} async-done(((bf16[128,16,1280]{2,1,0:T(8,128)(2,1)}), bf16[128,16,1280]{2,1,0:T(8,128)(2,1)}, u32[]{:S(2)}, u32[]{:S(2)}) %all-to-all-start.1) | async-done | bytes 5242912 | tf_op jit(solution)/shard_map/all_to_all | solution.py:160
  399.8 3.8 fusion.36
  403.7 4.2 %fusion.15 = bf16[128,1280]{1,0:T(8,128)(2,1)} fusion(f32[128,1280]{1,0:T(8,128)S(1)} %copy-done.3, f32[128,1280]{1,0:T(8,128)S(1)} %fusion.36, bf16[2048,1280]{1,0:T(8,128)(2,1)} %bitcast.30, f32[128,2048]{1,0:T(8,128)S(1)} %copy-done.2, f32[128,2048]{1,0:T(8,128)S(1)} %get-tuple-element.9), kind=kOutput, calls=%fused_computation.27 | convolution fusion | flops 672890880 | bytes 8978432 | tf_op jit(solution)/shard_map/dot_general | solution.py:112
  (59 shorter events, 1.3 us)
Async XLA Ops:
  0.0 251.8 %copy-start = (bf16[1,384,2560]{2,1,0:T(8,128)(2,1)S(1)}, bf16[1,384,2560]{2,1,0:T(8,128)(2,1)}, u32[]{:S(2)}) copy-start(bf16[1,384,2560]{2,1,0:T(8,128)(2,1)} %param.19) | copy-start | bytes 5898244
  0.0 5.3 %copy-start.5 = (s32[128,6]{0,1:T(8,128)S(1)}, s32[128,6]{0,1:T(8,128)}, u32[]{:S(2)}) copy-start(s32[128,6]{0,1:T(8,128)} %param.13) | copy-start | bytes 9220
  0.0 8.0 %copy-start.7 = (f32[2560]{0:T(1024)S(1)}, f32[2560]{0:T(1024)}, u32[]{:S(2)}) copy-start(f32[2560]{0:T(1024)} %param.12) | copy-start | bytes 30724
  13.4 16.1 %copy-start.6 = (bf16[1,2560,8]{1,2,0:T(8,128)(2,1)S(1)}, bf16[1,2560,8]{1,2,0:T(8,128)(2,1)}, u32[]{:S(2)}) copy-start(bf16[1,2560,8]{1,2,0:T(8,128)(2,1)} %param.20) | copy-start | bytes 122884
  13.4 16.1 %copy-start.4 = (bf16[1,8,1280]{2,1,0:T(8,128)(2,1)S(1)}, bf16[1,8,1280]{2,1,0:T(8,128)(2,1)}, u32[]{:S(2)}) copy-start(bf16[1,8,1280]{2,1,0:T(8,128)(2,1)} %param.21) | copy-start | bytes 61444
  13.4 220.4 %all-to-all-start = ((bf16[128,16,1280]{2,1,0:T(8,128)(2,1)}), bf16[128,16,1280]{2,1,0:T(8,128)(2,1)}, u32[]{:S(2)}, u32[]{:S(2)}) async-start(bf16[128,16,1280]{2,1,0:T(8,128)(2,1)} %bitcast.73), calls=%async_computation | async-start | bytes 10485760 | tf_op jit(solution)/shard_map/all_to_all | solution.py:151
  29.5 116.6 %collective-permute-start = (bf16[16,1280]{1,0:T(8,128)(2,1)S(1)}, bf16[16,1280]{1,0:T(8,128)(2,1)S(1)}, u32[]{:S(2)}, u32[]{:S(2)}) collective-permute-start(bf16[16,1280]{1,0:T(8,128)(2,1)S(1)} %pad_maximum_fusion.2), channel_id=1, source_target_pairs={{0,4},{4,8},{8,12},{12,16},{16,20},{20,24},{24,28},{28,0},{1,5},{5... | collective-permute-start | bytes 122888 | tf_op jit(solution)/shard_map/ppermute | solution.py:21
  31.1 118.2 %collective-permute-start.1 = (bf16[16,1280]{1,0:T(8,128)(2,1)S(1)}, bf16[16,1280]{1,0:T(8,128)(2,1)S(1)}, u32[]{:S(2)}, u32[]{:S(2)}) collective-permute-start(bf16[16,1280]{1,0:T(8,128)(2,1)S(1)} %pad_maximum_fusion.2), channel_id=1, source_target_pairs={{0,8},{4,12},{8,16},{12,20},{16,24},{20,28},{24,0},{28,4},{1,9},{5... | collective-permute-start | bytes 122888 | tf_op jit(solution)/shard_map/ppermute | solution.py:21
  33.5 116.1 %collective-permute-start.2 = (bf16[16,1280]{1,0:T(8,128)(2,1)S(1)}, bf16[16,1280]{1,0:T(8,128)(2,1)S(1)}, u32[]{:S(2)}, u32[]{:S(2)}) collective-permute-start(bf16[16,1280]{1,0:T(8,128)(2,1)S(1)} %pad_maximum_fusion.2), channel_id=1, source_target_pairs={{0,12},{4,16},{8,20},{12,24},{16,28},{20,0},{24,4},{28,8},{1,13},{... | collective-permute-start | bytes 122888 | tf_op jit(solution)/shard_map/ppermute | solution.py:21
  36.3 117.1 %collective-permute-start.3 = (bf16[16,1280]{1,0:T(8,128)(2,1)S(1)}, bf16[16,1280]{1,0:T(8,128)(2,1)S(1)}, u32[]{:S(2)}, u32[]{:S(2)}) collective-permute-start(bf16[16,1280]{1,0:T(8,128)(2,1)S(1)} %pad_maximum_fusion.2), channel_id=1, source_target_pairs={{0,16},{4,20},{8,24},{12,28},{16,0},{20,4},{24,8},{28,12},{1,17},{... | collective-permute-start | bytes 122888 | tf_op jit(solution)/shard_map/ppermute | solution.py:21
  38.5 114.9 %collective-permute-start.4 = (bf16[16,1280]{1,0:T(8,128)(2,1)S(1)}, bf16[16,1280]{1,0:T(8,128)(2,1)S(1)}, u32[]{:S(2)}, u32[]{:S(2)}) collective-permute-start(bf16[16,1280]{1,0:T(8,128)(2,1)S(1)} %pad_maximum_fusion.2), channel_id=1, source_target_pairs={{0,20},{4,24},{8,28},{12,0},{16,4},{20,8},{24,12},{28,16},{1,21},{... | collective-permute-start | bytes 122888 | tf_op jit(solution)/shard_map/ppermute | solution.py:21
  146.1 7.3 %collective-permute-start.5 = (bf16[16,1280]{1,0:T(8,128)(2,1)S(1)}, bf16[16,1280]{1,0:T(8,128)(2,1)S(1)}, u32[]{:S(2)}, u32[]{:S(2)}) collective-permute-start(bf16[16,1280]{1,0:T(8,128)(2,1)S(1)} %pad_maximum_fusion.2), channel_id=1, source_target_pairs={{0,24},{4,28},{8,0},{12,4},{16,8},{20,12},{24,16},{28,20},{1,25},{... | collective-permute-start | bytes 122888 | tf_op jit(solution)/shard_map/ppermute | solution.py:21
  149.3 4.1 %collective-permute-start.6 = (bf16[16,1280]{1,0:T(8,128)(2,1)S(1)}, bf16[16,1280]{1,0:T(8,128)(2,1)S(1)}, u32[]{:S(2)}, u32[]{:S(2)}) collective-permute-start(bf16[16,1280]{1,0:T(8,128)(2,1)S(1)} %pad_maximum_fusion.2), channel_id=1, source_target_pairs={{0,28},{4,0},{8,4},{12,8},{16,12},{20,16},{24,20},{28,24},{1,29},{... | collective-permute-start | bytes 122888 | tf_op jit(solution)/shard_map/ppermute | solution.py:21
  153.4 14.1 %collective-permute-start.9 = (bf16[8,16,1280]{2,1,0:T(8,128)(2,1)S(1)}, bf16[8,16,1280]{2,1,0:T(8,128)(2,1)S(1)}, u32[]{:S(2)}, u32[]{:S(2)}) collective-permute-start(bf16[8,16,1280]{2,1,0:T(8,128)(2,1)S(1)} %bitcast_dynamic-update-slice_fusion), channel_id=1, source_target_pairs={{0,3},{1,0},{2,1},{3,2},{4,7},{5,4},{6,5},{7,6},{8,11},{9,8},{10,9... | collective-permute-start | bytes 983048 | tf_op jit(solution)/shard_map/ppermute | solution.py:21
  156.2 11.6 %collective-permute-start.8 = (bf16[8,16,1280]{2,1,0:T(8,128)(2,1)S(1)}, bf16[8,16,1280]{2,1,0:T(8,128)(2,1)S(1)}, u32[]{:S(2)}, u32[]{:S(2)}) collective-permute-start(bf16[8,16,1280]{2,1,0:T(8,128)(2,1)S(1)} %bitcast_dynamic-update-slice_fusion), channel_id=1, source_target_pairs={{0,2},{1,3},{2,0},{3,1},{4,6},{5,7},{6,4},{7,5},{8,10},{9,11},{10,... | collective-permute-start | bytes 983048 | tf_op jit(solution)/shard_map/ppermute | solution.py:21
  157.1 14.1 %collective-permute-start.7 = (bf16[8,16,1280]{2,1,0:T(8,128)(2,1)S(1)}, bf16[8,16,1280]{2,1,0:T(8,128)(2,1)S(1)}, u32[]{:S(2)}, u32[]{:S(2)}) collective-permute-start(bf16[8,16,1280]{2,1,0:T(8,128)(2,1)S(1)} %bitcast_dynamic-update-slice_fusion), channel_id=1, source_target_pairs={{0,1},{1,2},{2,3},{3,0},{4,5},{5,6},{6,7},{7,4},{8,9},{9,10},{10,1... | collective-permute-start | bytes 983048 | tf_op jit(solution)/shard_map/ppermute | solution.py:21
  171.4 30.7 %collective-permute-start.12 = (bf16[4,8,16,1280]{3,2,1,0:T(8,128)(2,1)S(1)}, bf16[4,8,16,1280]{3,2,1,0:T(8,128)(2,1)S(1)}, u32[]{:S(2)}, u32[]{:S(2)}) collective-permute-start(bf16[4,8,16,1280]{3,2,1,0:T(8,128)(2,1)S(1)} %get-tuple-element.16), channel_id=1, source_target_pairs={{0,96},{32,0},{64,32},{96,64},{1,97},{33,1},{65,33},{97,65},{2,98}... | collective-permute-start | bytes 3932168 | tf_op jit(solution)/shard_map/ppermute | solution.py:21
  171.9 58.6 %collective-permute-start.11 = (bf16[4,8,16,1280]{3,2,1,0:T(8,128)(2,1)S(1)}, bf16[4,8,16,1280]{3,2,1,0:T(8,128)(2,1)S(1)}, u32[]{:S(2)}, u32[]{:S(2)}) collective-permute-start(bf16[4,8,16,1280]{3,2,1,0:T(8,128)(2,1)S(1)} %get-tuple-element.16), channel_id=1, source_target_pairs={{0,64},{32,96},{64,0},{96,32},{1,65},{33,97},{65,1},{97,33},{2,66}... | collective-permute-start | bytes 3932168 | tf_op jit(solution)/shard_map/ppermute | solution.py:21
  174.6 56.6 %collective-permute-start.10 = (bf16[4,8,16,1280]{3,2,1,0:T(8,128)(2,1)S(1)}, bf16[4,8,16,1280]{3,2,1,0:T(8,128)(2,1)S(1)}, u32[]{:S(2)}, u32[]{:S(2)}) collective-permute-start(bf16[4,8,16,1280]{3,2,1,0:T(8,128)(2,1)S(1)} %get-tuple-element.16), channel_id=1, source_target_pairs={{0,32},{32,64},{64,96},{96,0},{1,33},{33,65},{65,97},{97,1},{2,34}... | collective-permute-start | bytes 3932168 | tf_op jit(solution)/shard_map/ppermute | solution.py:21
  233.8 10.8 %collective-permute-start.13 = (bf16[2048,1280]{1,0:T(8,128)(2,1)}, bf16[2048,1280]{1,0:T(8,128)(2,1)}, u32[]{:S(2)}, u32[]{:S(2)}) collective-permute-start(bf16[2048,1280]{1,0:T(8,128)(2,1)} %bitcast.21), channel_id=1, source_target_pairs={{0,128},{128,0},{1,129},{129,1},{2,130},{130,2},{3,131},{131,3},{4... | collective-permute-start | bytes 15728648 | tf_op jit(solution)/shard_map/ppermute | solution.py:45
  255.0 8.9 %collective-permute-start.14 = (bf16[2048,1280]{1,0:T(8,128)(2,1)S(1)}, bf16[2048,1280]{1,0:T(8,128)(2,1)S(1)}, u32[]{:S(2)}, u32[]{:S(2)}) collective-permute-start(bf16[2048,1280]{1,0:T(8,128)(2,1)S(1)} %convolution_convert_fusion), channel_id=1, source_target_pairs={{0,128},{128,0},{1,129},{129,1},{2,130},{130,2},{3,131},{131,3},{4... | collective-permute-start | bytes 15728648 | tf_op jit(solution)/shard_map/ppermute | solution.py:45
  268.3 11.7 %copy-start.1 = (s32[128]{0:T(128)S(1)}, s32[128]{0:T(128)}, u32[]{:S(2)}) copy-start(s32[128]{0:T(128)} %param.17) | copy-start | bytes 1540
  268.3 12.9 %copy-start.9 = (s32[256]{0:T(256)S(1)}, s32[256]{0:T(256)}, u32[]{:S(2)}) copy-start(s32[256]{0:T(256)} %param.16) | copy-start | bytes 3076
  268.3 12.9 %copy-start.10 = (s32[128]{0:T(128)S(1)}, s32[128]{0:T(128)}, u32[]{:S(2)}) copy-start(s32[128]{0:T(128)} %param.15) | copy-start | bytes 1540
  268.3 13.8 %copy-start.8 = (f32[128,6]{0,1:T(8,128)S(1)}, f32[128,6]{0,1:T(8,128)}, u32[]{:S(2)}) copy-start(f32[128,6]{0,1:T(8,128)} %param.14) | copy-start | bytes 9220
  268.3 131.5 %all-to-all-start.1 = ((bf16[128,16,1280]{2,1,0:T(8,128)(2,1)}), bf16[128,16,1280]{2,1,0:T(8,128)(2,1)}, u32[]{:S(2)}, u32[]{:S(2)}) async-start(bf16[128,16,1280]{2,1,0:T(8,128)(2,1)} %bitcast.76), calls=%async_computation.1 | async-start | bytes 10485760 | tf_op jit(solution)/shard_map/all_to_all | solution.py:160
  399.8 3.8 copy-start.2
  399.8 3.8 copy-start.3

commit v7 on v4

--- a/solution.py
+++ b/solution.py
@@ -17,22 +17,13 @@
     return lax.ppermute(values, "kv", perm=[(0, 1), (1, 0)])
 
 
-def expert_half(own_rows, expert_gate_up_weight, expert_down_weight):
-    kv_index = lax.axis_index("kv")
-    half_width = own_rows.shape[1]
+def expert_half(own_rows, weights):
+    own_weight, other_weight, own_cols, other_cols = weights
     other_rows = swap_kv(own_rows)
-    gate_up_weight = expert_gate_up_weight[0]
-    own_weight = lax.dynamic_slice_in_dim(gate_up_weight, kv_index * half_width, half_width, 0)
-    other_weight = lax.dynamic_slice_in_dim(
-        gate_up_weight, (1 - kv_index) * half_width, half_width, 0
-    )
     gate_up = jnp.einsum(
         "rd,dgf->rgf", own_rows, own_weight, preferred_element_type=jnp.float32
     ) + jnp.einsum("rd,dgf->rgf", other_rows, other_weight, preferred_element_type=jnp.float32)
     hidden = (jax.nn.silu(gate_up[:, 0]) * gate_up[:, 1]).astype(jnp.bfloat16)
-    down_weight = expert_down_weight[0]
-    other_cols = lax.dynamic_slice_in_dim(down_weight, (1 - kv_index) * half_width, half_width, 1)
-    own_cols = lax.dynamic_slice_in_dim(down_weight, kv_index * half_width, half_width, 1)
     sent_quarter = jnp.dot(hidden, other_cols, preferred_element_type=jnp.float32).astype(
         jnp.bfloat16
     )
@@ -40,9 +31,23 @@
     own_quarter = jnp.dot(hidden, own_cols, preferred_element_type=jnp.float32).astype(
         jnp.bfloat16
     )
+    own_quarter, received_quarter = lax.optimization_barrier((own_quarter, received_quarter))
     return (own_quarter.astype(jnp.float32) + received_quarter.astype(jnp.float32)).astype(
         jnp.bfloat16
     )
+
+
+def split_weights(expert_gate_up_weight, expert_down_weight, half_width):
+    kv_index = lax.axis_index("kv")
+    gate_up_weight = expert_gate_up_weight[0]
+    own_weight = lax.dynamic_slice_in_dim(gate_up_weight, kv_index * half_width, half_width, 0)
+    other_weight = lax.dynamic_slice_in_dim(
+        gate_up_weight, (1 - kv_index) * half_width, half_width, 0
+    )
+    down_weight = expert_down_weight[0]
+    own_cols = lax.dynamic_slice_in_dim(down_weight, kv_index * half_width, half_width, 1)
+    other_cols = lax.dynamic_slice_in_dim(down_weight, (1 - kv_index) * half_width, half_width, 1)
+    return own_weight, other_weight, own_cols, other_cols
 
 
 def rank_in_expert(flat_ids, expert_count):
@@ -122,7 +127,9 @@
     )
     inbox_half = lax.all_to_all(outbox, PG_AXES, split_axis=0, concat_axis=0, tiled=True)
     packed_all = lax.all_gather(packed, PG_AXES, axis=0, tiled=False)
-    half_out = expert_half(inbox_half.reshape(pg_size * slot_cap, half_width), expert_gate_up_weight, expert_down_weight)
+    weights = split_weights(expert_gate_up_weight, expert_down_weight, half_width)
+    inbox_half, packed_all, weights = lax.optimization_barrier((inbox_half, packed_all, weights))
+    half_out = expert_half(inbox_half.reshape(pg_size * slot_cap, half_width), weights)
     results = lax.all_to_all(
         half_out.reshape(pg_size, slot_cap, half_width),
         PG_AXES,

time: 362 us -> 351 us (0.970)
  blocking collectives: 140 us -> 5.59 us
  waiting for transfers between devices: 140 us -> 243 us
  starting transfers between devices: 8.71 us -> 29.1 us
  matrix products: 39.4 us -> 35 us
  local copies, waits for them, and re-layouts: 6.44 us -> 10.3 us
    all_to_all x1 -> x0, blocking collectives: 135 us -> none  [on_device(): lax.all_to_all(outbox, PG_AXES, split_axis=0, concat_axis=0, tiled=True)]
    all_to_all x1, waiting for transfers between devices: 0.01 us -> 106 us  [on_device(): lax.all_to_all(half_out.reshape(pg_size, slot_cap, half_width), PG_AXES,...]
    all_to_all x0 -> x1, starting transfers between devices: none -> 16.1 us  [on_device(): lax.all_to_all(outbox, PG_AXES, split_axis=0, concat_axis=0, tiled=True)]
    all_to_all x1, starting transfers between devices: 8.21 us -> 12.7 us  [on_device(): lax.all_to_all(half_out.reshape(pg_size, slot_cap, half_width), PG_AXES,...]
    convert_element_type x0 -> x1, other arithmetic: none -> 3.95 us  [expert_half(): (own_quarter.astype(jnp.float32) + received_quarter.astype(jnp.float32))....]
  transfers between devices with their start and end apart: 4 -> 5, of which waited for: 2 -> 4; matrix products, arithmetic and copies ran while one was open for 8% -> 10% of each run, Pallas kernels for 0% -> 0%
where the time goes in v7:
time: 351 us
  waiting for transfers between devices  243 us (69%)
  matrix products  35 us (10%)
  starting transfers between devices  29.1 us (8%)
  other arithmetic  13.9 us (4%)
  between operations  13.6 us (4%)
  local copies, waits for them, and re-layouts  10.3 us (3%)
  blocking collectives  5.59 us (2%)
    all_gather x1, waiting for transfers between devices, on_device(): packed_all = lax.all_gather(packed, PG_AXES, axis=0, tiled=False)  130 us
    all_to_all x1, waiting for transfers between devices, on_device(): lax.all_to_all(half_out.reshape(pg_size, slot_cap, half_width), PG_AXES,...  106 us
    all_to_all x1, starting transfers between devices, on_device(): lax.all_to_all(outbox, PG_AXES, split_axis=0, concat_axis=0, tiled=True)  16.1 us
    all_to_all x1, starting transfers between devices, on_device(): lax.all_to_all(half_out.reshape(pg_size, slot_cap, half_width), PG_AXES,...  12.7 us
    ppermute x2, waiting for transfers between devices, swap_kv(): return lax.ppermute(values, 'kv', perm=[(0, 1), (1, 0)])  7.5 us
  transfers between devices with their start and end apart: 5, of which 4 were waited for; matrix products, arithmetic and copies ran while one was open for 10% of the time, Pallas kernels for 0%

profile of v7, /device:TPU:2, one launch (start us, length us, event | category | flops | bytes accessed | tf_op | source)
XLA Modules:
  0.0 350.5 jit_solution(8967705044014713759)
XLA Ops:
  6.5 0.0 copy-start
  6.5 0.0 all-gather.3.cloned.1.call-start
  6.5 0.8 copy-done
  7.3 1.3 pad_maximum_fusion
  8.7 0.0 all-gather.3.cloned.1.call-update
  8.7 1.2 convert_element_type.73
  9.9 1.3 multiply_reduce_fusion
  11.2 0.8 copy.37
  12.0 0.1 eq.98
  12.1 0.4 fusion.22
  12.5 0.1 convert_element_type.68
  12.7 0.1 copy.38
  12.7 0.7 broadcast_add_fusion
  13.5 0.8 dynamic-slice.5
  14.2 1.7 convert_reduce_fusion
  15.9 4.0 %convolution_convert_fusion.2 = bf16[2048,1280]{1,0:T(8,128)(2,1)} fusion(f32[2048,128]{1,0:T(8,128)S(1)} %get-tuple-element.30, f32[2048,128]{1,0:T(8,128)S(1)} %get-tuple-element.29, f32[128,2560]{1,0:T(8,128)S(1)} %convert_element_type.73, s32[]{:T(128)S(6)} %select_n.27, f32[1280]{0:T(1024)S(1)} %dynamic-slice.5, f32[128]{0:T(128)S(1)} %add_rsqrt_fusion), kind=kOutput, calls=%fused_computation.3 | convolution fusion | flops 674725888 | bytes 8004100 | tf_op jit(solution)/shard_map/dot_general | solution.py:73
  19.9 16.1 %all-to-all-start = ((bf16[128,16,1280]{2,1,0:T(8,128)(2,1)}), bf16[128,16,1280]{2,1,0:T(8,128)(2,1)}, u32[]{:S(2)}, u32[]{:S(2)}) async-start(bf16[128,16,1280]{2,1,0:T(8,128)(2,1)} %bitcast.53), calls=%async_computation | async-start | bytes 10485760 | tf_op jit(solution)/shard_map/all_to_all | solution.py:128
  36.0 0.0 copy-done.3
  36.0 0.0 copy-start.2
  36.0 1.4 dynamic-slice_bitcast_fusion
  37.4 1.4 copy-done.2
  38.8 2.8 constant_dynamic-slice_fusion
  41.6 1.8 copy_bitcast_fusion
  43.4 129.9 %all-gather.3.cloned.1.call-done = bf16[2048,1280]{1,0:T(8,128)(2,1)} async-done(((bf16[16,1280]{1,0:T(8,128)(2,1)}), bf16[2048,1280]{1,0:T(8,128)(2,1)}) %all-gather.3.cloned.1.call-update) | async-done | bytes 5242896 | tf_op jit(solution)/shard_map/all_gather | solution.py:129
  173.3 0.0 all-to-all-done
  173.3 0.1 collective-permute-start
  173.4 6.8 %fusion.34 = f32[2048,2,384]{2,0,1:T(8,128)S(1)} fusion(bf16[2048,1280,1]{1,0,2:T(8,128)(2,1)} %bitcast.10, bf16[1280,2,384]{2,0,1:T(8,128)(2,1)} %get-tuple-element.14), kind=kOutput, calls=%fused_computation.64 | convolution fusion | flops 4026531840 | bytes 13500416 | tf_op jit(solution)/shard_map/rd,dgf->rgf/dot_general | solution.py:23
  180.1 2.0 collective-permute-done
  182.2 4.3 %fusion.2 = f32[2048,2,384]{2,0,1:T(8,128)S(1)} fusion(f32[2048,2,384]{2,0,1:T(8,128)S(1)} %fusion.34, bf16[1280,2,384]{2,0,1:T(8,128)(2,1)S(1)} %get-tuple-element.15, bf16[2048,1280]{1,0:T(8,128)(2,1)S(1)} %collective-permute-done), kind=kOutput, calls=%fused_computation.14 | convolution fusion | flops 4028104704 | bytes 19791872 | tf_op jit(solution)/shard_map/rd,dgf->rgf/dot_general | solution.py:25
  186.5 0.9 fusion.6
  187.5 0.3 copy-done.5
  187.7 3.1 convolution_convert_fusion
  190.8 0.2 collective-permute-start.1
  191.0 3.0 convolution_convert_fusion.1
  194.1 5.5 %collective-permute-done.1 = bf16[2048,1280]{1,0:T(8,128)(2,1)S(1)} collective-permute-done((bf16[2048,1280]{1,0:T(8,128)(2,1)S(1)}, bf16[2048,1280]{1,0:T(8,128)(2,1)S(1)}, u32[]{:S(2)}, u32[]{:S(2)}) %collective-permute-start.1) | collective-permute-done | bytes 5242912 | tf_op jit(solution)/shard_map/ppermute | solution.py:17
  199.5 4.0 %add_convert_fusion = bf16[2048,1280]{1,0:T(8,128)(2,1)} fusion(bf16[2048,1280]{1,0:T(8,128)(2,1)S(1)} %collective-permute-done.1, bf16[2048,1280]{1,0:T(8,128)(2,1)S(1)} %convolution_convert_fusion.1), kind=kLoop, calls=%fused_computation | loop fusion | flops 10485760 | bytes 15728640 | tf_op jit(solution)/shard_map/convert_element_type | solution.py:35
  203.5 12.7 %all-to-all-start.1 = ((bf16[128,16,1280]{2,1,0:T(8,128)(2,1)}), bf16[128,16,1280]{2,1,0:T(8,128)(2,1)}, u32[]{:S(2)}, u32[]{:S(2)}) async-start(bf16[128,16,1280]{2,1,0:T(8,128)(2,1)} %bitcast.54), calls=%async_computation.1 | async-start | bytes 10485760 | tf_op jit(solution)/shard_map/all_to_all | solution.py:133
  216.2 0.2 select_reduce_fusion.2
  216.4 0.0 copy-done.8
  216.4 0.1 broadcast_compare_fusion
  216.5 2.5 select_reduce_fusion
  219.0 3.5 fusion.18
  222.5 5.6 %all-reduce.1 = bf16[128,128,8]{0,2,1:T(8,128)(2,1)S(1)} all-reduce(f32[128,128,8]{0,2,1:T(8,128)} %fusion.18), channel_id=1, replica_groups=mesh['kv'=2,'px'=4,'pz'=8,'py'=4] {'kv'}, use_global_device_ids=true, to_apply=%region_7.8 | all-reduce | flops 131072 | bytes 786432 | tf_op jit(solution)/shard_map/psum | solution.py:155
  228.1 2.3 fusion.13
  230.4 105.6 %all-to-all-done.1 = bf16[128,16,1280]{2,1,0:T(8,128)(2,1)} async-done(((bf16[128,16,1280]{2,1,0:T(8,128)(2,1)}), bf16[128,16,1280]{2,1,0:T(8,128)(2,1)}, u32[]{:S(2)}, u32[]{:S(2)}) %all-to-all-start.1) | async-done | bytes 5242912 | tf_op jit(solution)/shard_map/all_to_all | solution.py:133
  336.0 3.4 fusion.26
  339.5 4.2 %fusion.16 = bf16[128,1280]{1,0:T(8,128)(2,1)} fusion(f32[128,1280]{1,0:T(8,128)S(1)} %fusion.13, f32[128,1280]{1,0:T(8,128)S(1)} %fusion.26, bf16[2048,1280]{1,0:T(8,128)(2,1)} %bitcast.15, f32[128,2048]{1,0:T(8,128)S(1)} %get-tuple-element.22, f32[128,2048]{1,0:T(8,128)S(1)} %get-tuple-element.21), kind=kOutput, calls=%fused_computation.27 | convolution fusion | flops 672890880 | bytes 8978432 | tf_op jit(solution)/shard_map/dot_general | solution.py:89
  343.7 0.0 copy-done.1
  (15 shorter events, 0.0 us)
Async XLA Ops:
  6.5 0.8 copy-start
  6.5 166.8 %all-gather.3.cloned.1.call-start = ((), (), s32[]{:S(2)}) async-start(), calls=%async_computation.2 | async-start | bytes 5283840 | tf_op jit(solution)/shard_map/all_gather | solution.py:129
  19.9 16.1 %copy-start.3 = (bf16[1,384,2560]{2,1,0:T(8,128)(2,1)S(1)}, bf16[1,384,2560]{2,1,0:T(8,128)(2,1)}, u32[]{:S(2)}) copy-start(bf16[1,384,2560]{2,1,0:T(8,128)(2,1)} %param.19) | copy-start | bytes 5898244
  19.9 153.4 %all-to-all-start = ((bf16[128,16,1280]{2,1,0:T(8,128)(2,1)}), bf16[128,16,1280]{2,1,0:T(8,128)(2,1)}, u32[]{:S(2)}, u32[]{:S(2)}) async-start(bf16[128,16,1280]{2,1,0:T(8,128)(2,1)} %bitcast.53), calls=%async_computation | async-start | bytes 10485760 | tf_op jit(solution)/shard_map/all_to_all | solution.py:128
  36.0 2.8 copy-start.2
  173.3 8.9 %collective-permute-start = (bf16[2048,1280]{1,0:T(8,128)(2,1)}, bf16[2048,1280]{1,0:T(8,128)(2,1)S(1)}, u32[]{:S(2)}, u32[]{:S(2)}) collective-permute-start(bf16[2048,1280]{1,0:T(8,128)(2,1)} %bitcast.9), channel_id=1, source_target_pairs={{0,128},{128,0},{1,129},{129,1},{2,130},{130,2},{3,131},{131,3},{4... | collective-permute-start | bytes 15728648 | tf_op jit(solution)/shard_map/ppermute | solution.py:17
  186.5 1.2 copy-start.5
  187.7 3.3 copy-start.4
  190.8 8.7 %collective-permute-start.1 = (bf16[2048,1280]{1,0:T(8,128)(2,1)S(1)}, bf16[2048,1280]{1,0:T(8,128)(2,1)S(1)}, u32[]{:S(2)}, u32[]{:S(2)}) collective-permute-start(bf16[2048,1280]{1,0:T(8,128)(2,1)S(1)} %convolution_convert_fusion), channel_id=1, source_target_pairs={{0,128},{128,0},{1,129},{129,1},{2,130},{130,2},{3,131},{131,3},{4... | collective-permute-start | bytes 15728648 | tf_op jit(solution)/shard_map/ppermute | solution.py:17
  203.5 12.7 %copy-start.7 = (s32[256]{0:T(256)S(1)}, s32[256]{0:T(256)}, u32[]{:S(2)}) copy-start(s32[256]{0:T(256)} %param.16) | copy-start | bytes 3076
  203.5 12.7 %copy-start.9 = (s32[128]{0:T(128)S(1)}, s32[128]{0:T(128)}, u32[]{:S(2)}) copy-start(s32[128]{0:T(128)} %param.15) | copy-start | bytes 1540
  203.5 12.9 %copy-start.8 = (s32[128]{0:T(128)S(1)}, s32[128]{0:T(128)}, u32[]{:S(2)}) copy-start(s32[128]{0:T(128)} %param.17) | copy-start | bytes 1540
  203.5 13.0 %copy-start.6 = (f32[128,6]{0,1:T(8,128)S(1)}, f32[128,6]{0,1:T(8,128)}, u32[]{:S(2)}) copy-start(f32[128,6]{0,1:T(8,128)} %param.14) | copy-start | bytes 9220
  203.5 132.5 %all-to-all-start.1 = ((bf16[128,16,1280]{2,1,0:T(8,128)(2,1)}), bf16[128,16,1280]{2,1,0:T(8,128)(2,1)}, u32[]{:S(2)}, u32[]{:S(2)}) async-start(bf16[128,16,1280]{2,1,0:T(8,128)(2,1)} %bitcast.54), calls=%async_computation.1 | async-start | bytes 10485760 | tf_op jit(solution)/shard_map/all_to_all | solution.py:133
  336.0 7.6 %copy-start.1 = (bf16[1,2560,8]{1,2,0:T(8,128)(2,1)S(1)}, bf16[1,2560,8]{1,2,0:T(8,128)(2,1)}, u32[]{:S(2)}) copy-start(bf16[1,2560,8]{1,2,0:T(8,128)(2,1)} %param.20) | copy-start | bytes 122884
Sparse Core Ops, SparseCore 0:
  10.8 162.4 all-gather.2

commit v8 on v7

--- a/solution.py
+++ b/solution.py
@@ -126,7 +126,9 @@
         pg_size, slot_cap, half_width
     )
     inbox_half = lax.all_to_all(outbox, PG_AXES, split_axis=0, concat_axis=0, tiled=True)
-    packed_all = lax.all_gather(packed, PG_AXES, axis=0, tiled=False)
+    packed_all = lax.all_gather(packed, PG_AXES[1:], axis=0, tiled=False)
+    packed_all = lax.all_gather(packed_all, PG_AXES[0], axis=0, tiled=False)
+    packed_all = packed_all.reshape((pg_size,) + packed.shape)
     weights = split_weights(expert_gate_up_weight, expert_down_weight, half_width)
     inbox_half, packed_all, weights = lax.optimization_barrier((inbox_half, packed_all, weights))
     half_out = expert_half(inbox_half.reshape(pg_size * slot_cap, half_width), weights)

time: 351 us -> 359 us (1.023)
  waiting for transfers between devices: 243 us -> 249 us
    all_to_all x1, waiting for transfers between devices: 0.01 us -> 49.9 us  [on_device(): lax.all_to_all(outbox, PG_AXES, split_axis=0, concat_axis=0, tiled=True)]
    all_gather x1 -> x2, waiting for transfers between devices: 130 us -> 86.4 us  [the longest x1 68.7 us: on_device(): packed_all = lax.all_gather(packed, PG_AXES[1:], axis=0, tiled=False)]
  transfers between devices with their start and end apart: 5 -> 6, of which waited for: 4 -> 6; matrix products, arithmetic and copies ran while one was open for 10% -> 10% of each run, Pallas kernels for 0% -> 0%
where the time goes in v8:
time: 359 us; the launch traced here: 358 us
  waiting for transfers between devices  249 us (69%)
  matrix products  35.8 us (10%)
  starting transfers between devices  30.5 us (8%)
  other arithmetic  13.6 us (4%)
  between operations  13.6 us (4%)
  local copies, waits for them, and re-layouts  10.3 us (3%)
  blocking collectives  5.58 us (2%)
    all_to_all x1, waiting for transfers between devices, on_device(): lax.all_to_all(half_out.reshape(pg_size, slot_cap, half_width), PG_AXES,...  105 us
    all_gather x1, waiting for transfers between devices, on_device(): packed_all = lax.all_gather(packed, PG_AXES[1:], axis=0, tiled=False)  68.7 us
    all_to_all x1, waiting for transfers between devices, on_device(): lax.all_to_all(outbox, PG_AXES, split_axis=0, concat_axis=0, tiled=True)  49.9 us
    all_gather x1, waiting for transfers between devices, on_device(): packed_all = lax.all_gather(packed_all, PG_AXES[0], axis=0, tiled=False)  17.7 us
    all_to_all x1, starting transfers between devices, on_device(): lax.all_to_all(outbox, PG_AXES, split_axis=0, concat_axis=0, tiled=True)  16.1 us
    all_to_all x1, starting transfers between devices, on_device(): lax.all_to_all(half_out.reshape(pg_size, slot_cap, half_width), PG_AXES,...  14.2 us
    ppermute x2, waiting for transfers between devices, swap_kv(): return lax.ppermute(values, 'kv', perm=[(0, 1), (1, 0)])  7.56 us
  transfers between devices with their start and end apart: 6, of which 6 were waited for; matrix products, arithmetic and copies ran while one was open for 10% of the time, Pallas kernels for 0%

profile of v8, /device:TPU:2, one launch (start us, length us, event | category | flops | bytes accessed | tf_op | source)
XLA Modules:
  0.0 358.0 jit_solution(10331658684218667976)
XLA Ops:
  6.5 0.0 all-gather.5.cloned.1.call-start
  6.5 0.8 copy-done
  7.3 1.3 pad_maximum_fusion
  8.7 0.0 all-gather.5.cloned.1.call-update
  8.7 1.2 convert_element_type.73
  9.9 1.3 multiply_reduce_fusion
  11.2 0.8 copy.48
  12.0 0.1 eq.98
  12.1 0.4 fusion.22
  12.5 0.1 convert_element_type.68
  12.7 0.1 copy.49
  12.7 0.7 broadcast_add_fusion
  13.5 0.8 dynamic-slice.5
  14.2 1.7 convert_reduce_fusion
  15.9 4.0 %convolution_convert_fusion.2 = bf16[2048,1280]{1,0:T(8,128)(2,1)} fusion(f32[2048,128]{1,0:T(8,128)S(1)} %get-tuple-element.30, f32[2048,128]{1,0:T(8,128)S(1)} %get-tuple-element.29, f32[128,2560]{1,0:T(8,128)S(1)} %convert_element_type.73, s32[]{:T(128)S(6)} %select_n.27, f32[1280]{0:T(1024)S(1)} %dynamic-slice.5, f32[128]{0:T(128)S(1)} %add_rsqrt_fusion), kind=kOutput, calls=%fused_computation.3 | convolution fusion | flops 674725888 | bytes 8004100 | tf_op jit(solution)/shard_map/dot_general | solution.py:73
  19.9 16.1 %all-to-all-start = ((bf16[128,16,1280]{2,1,0:T(8,128)(2,1)}), bf16[128,16,1280]{2,1,0:T(8,128)(2,1)}, u32[]{:S(2)}, u32[]{:S(2)}) async-start(bf16[128,16,1280]{2,1,0:T(8,128)(2,1)} %bitcast.53), calls=%async_computation | async-start | bytes 10485760 | tf_op jit(solution)/shard_map/all_to_all | solution.py:128
  36.0 0.0 all-gather.7.cloned.1.call-start
  36.0 68.7 %all-gather.5.cloned.1.call-done = bf16[512,1280]{1,0:T(8,128)(2,1)} async-done(((bf16[16,1280]{1,0:T(8,128)(2,1)}), bf16[512,1280]{1,0:T(8,128)(2,1)}) %all-gather.5.cloned.1.call-update) | async-done | bytes 1310736 | tf_op jit(solution)/shard_map/all_gather | solution.py:129
  104.7 0.0 all-gather.7.cloned.1.call-update
  104.7 0.0 copy-done.3
  104.7 0.0 copy-start.2
  104.7 1.4 dynamic-slice_bitcast_fusion
  106.1 1.4 copy-done.2
  107.6 2.8 constant_dynamic-slice_fusion
  110.3 1.8 copy_bitcast_fusion
  112.1 49.9 %all-to-all-done = bf16[128,16,1280]{2,1,0:T(8,128)(2,1)} async-done(((bf16[128,16,1280]{2,1,0:T(8,128)(2,1)}), bf16[128,16,1280]{2,1,0:T(8,128)(2,1)}, u32[]{:S(2)}, u32[]{:S(2)}) %all-to-all-start) | async-done | bytes 5242912 | tf_op jit(solution)/shard_map/all_to_all | solution.py:128
  162.0 17.7 %all-gather.7.cloned.1.call-done = bf16[128,16,1280]{2,1,0:T(8,128)(2,1)} async-done(((bf16[32,16,1280]{2,1,0:T(8,128)(2,1)}), bf16[128,16,1280]{2,1,0:T(8,128)(2,1)}) %all-gather.7.cloned.1.call-update) | async-done | bytes 5242896 | tf_op jit(solution)/shard_map/all_gather | solution.py:130
  179.7 0.0 collective-permute-start
  179.7 6.8 %fusion.34 = f32[2048,2,384]{2,0,1:T(8,128)S(1)} fusion(bf16[2048,1280,1]{1,0,2:T(8,128)(2,1)} %bitcast.10, bf16[1280,2,384]{2,0,1:T(8,128)(2,1)} %get-tuple-element.14), kind=kOutput, calls=%fused_computation.64 | convolution fusion | flops 4026531840 | bytes 13500416 | tf_op jit(solution)/shard_map/rd,dgf->rgf/dot_general | solution.py:23
  186.5 2.1 collective-permute-done
  188.6 4.3 %fusion.2 = f32[2048,2,384]{2,0,1:T(8,128)S(1)} fusion(f32[2048,2,384]{2,0,1:T(8,128)S(1)} %fusion.34, bf16[1280,2,384]{2,0,1:T(8,128)(2,1)S(1)} %get-tuple-element.15, bf16[2048,1280]{1,0:T(8,128)(2,1)S(1)} %collective-permute-done), kind=kOutput, calls=%fused_computation.14 | convolution fusion | flops 4028104704 | bytes 19791872 | tf_op jit(solution)/shard_map/rd,dgf->rgf/dot_general | solution.py:25
  192.9 0.9 fusion.6
  193.8 0.3 copy-done.5
  194.1 3.1 convolution_convert_fusion
  197.2 0.2 collective-permute-start.1
  197.4 3.0 convolution_convert_fusion.1
  200.4 5.5 %collective-permute-done.1 = bf16[2048,1280]{1,0:T(8,128)(2,1)S(1)} collective-permute-done((bf16[2048,1280]{1,0:T(8,128)(2,1)S(1)}, bf16[2048,1280]{1,0:T(8,128)(2,1)S(1)}, u32[]{:S(2)}, u32[]{:S(2)}) %collective-permute-start.1) | collective-permute-done | bytes 5242912 | tf_op jit(solution)/shard_map/ppermute | solution.py:17
  205.9 3.7 %add_convert_fusion = bf16[2048,1280]{1,0:T(8,128)(2,1)} fusion(bf16[2048,1280]{1,0:T(8,128)(2,1)S(1)} %collective-permute-done.1, bf16[2048,1280]{1,0:T(8,128)(2,1)S(1)} %convolution_convert_fusion.1), kind=kLoop, calls=%fused_computation | loop fusion | flops 10485760 | bytes 15728640 | tf_op jit(solution)/shard_map/convert_element_type | solution.py:35
  209.6 14.2 %all-to-all-start.1 = ((bf16[128,16,1280]{2,1,0:T(8,128)(2,1)}), bf16[128,16,1280]{2,1,0:T(8,128)(2,1)}, u32[]{:S(2)}, u32[]{:S(2)}) async-start(bf16[128,16,1280]{2,1,0:T(8,128)(2,1)} %bitcast.54), calls=%async_computation.1 | async-start | bytes 10485760 | tf_op jit(solution)/shard_map/all_to_all | solution.py:135
  223.8 0.2 select_reduce_fusion.2
  224.0 0.1 broadcast_compare_fusion
  224.1 2.5 select_reduce_fusion
  226.5 3.4 fusion.18
  230.0 5.6 %all-reduce.1 = bf16[128,128,8]{0,2,1:T(8,128)(2,1)S(1)} all-reduce(f32[128,128,8]{0,2,1:T(8,128)} %fusion.18), channel_id=1, replica_groups=mesh['kv'=2,'px'=4,'pz'=8,'py'=4] {'kv'}, use_global_device_ids=true, to_apply=%region_7.8 | all-reduce | flops 131072 | bytes 786432 | tf_op jit(solution)/shard_map/psum | solution.py:157
  235.6 3.2 fusion.13
  238.8 104.8 %all-to-all-done.1 = bf16[128,16,1280]{2,1,0:T(8,128)(2,1)} async-done(((bf16[128,16,1280]{2,1,0:T(8,128)(2,1)}), bf16[128,16,1280]{2,1,0:T(8,128)(2,1)}, u32[]{:S(2)}, u32[]{:S(2)}) %all-to-all-start.1) | async-done | bytes 5242912 | tf_op jit(solution)/shard_map/all_to_all | solution.py:135
  343.6 3.4 fusion.26
  347.0 4.2 %fusion.16 = bf16[128,1280]{1,0:T(8,128)(2,1)} fusion(f32[128,1280]{1,0:T(8,128)S(1)} %copy-done.6, f32[128,1280]{1,0:T(8,128)S(1)} %fusion.26, bf16[2048,1280]{1,0:T(8,128)(2,1)} %bitcast.15, f32[128,2048]{1,0:T(8,128)S(1)} %get-tuple-element.22, f32[128,2048]{1,0:T(8,128)S(1)} %get-tuple-element.21), kind=kOutput, calls=%fused_computation.27 | convolution fusion | flops 672890880 | bytes 8978432 | tf_op jit(solution)/shard_map/dot_general | solution.py:89
  (20 shorter events, 0.0 us)
Async XLA Ops:
  6.5 0.8 copy-start
  6.5 98.2 %all-gather.5.cloned.1.call-start = ((), (), s32[]{:S(2)}) async-start(), calls=%async_computation.2 | async-start | bytes 1351680 | tf_op jit(solution)/shard_map/all_gather | solution.py:129
  19.9 84.8 %copy-start.3 = (bf16[1,384,2560]{2,1,0:T(8,128)(2,1)S(1)}, bf16[1,384,2560]{2,1,0:T(8,128)(2,1)}, u32[]{:S(2)}) copy-start(bf16[1,384,2560]{2,1,0:T(8,128)(2,1)} %param.19) | copy-start | bytes 5898244
  19.9 142.1 %all-to-all-start = ((bf16[128,16,1280]{2,1,0:T(8,128)(2,1)}), bf16[128,16,1280]{2,1,0:T(8,128)(2,1)}, u32[]{:S(2)}, u32[]{:S(2)}) async-start(bf16[128,16,1280]{2,1,0:T(8,128)(2,1)} %bitcast.53), calls=%async_computation | async-start | bytes 10485760 | tf_op jit(solution)/shard_map/all_to_all | solution.py:128
  36.0 143.7 %all-gather.7.cloned.1.call-start = ((), (), s32[]{:S(2)}) async-start(), calls=%async_computation.3 | async-start | bytes 6553600 | tf_op jit(solution)/shard_map/all_gather | solution.py:130
  104.7 2.8 copy-start.2
  179.7 8.9 %collective-permute-start = (bf16[2048,1280]{1,0:T(8,128)(2,1)}, bf16[2048,1280]{1,0:T(8,128)(2,1)S(1)}, u32[]{:S(2)}, u32[]{:S(2)}) collective-permute-start(bf16[2048,1280]{1,0:T(8,128)(2,1)} %bitcast.9), channel_id=1, source_target_pairs={{0,128},{128,0},{1,129},{129,1},{2,130},{130,2},{3,131},{131,3},{4... | collective-permute-start | bytes 15728648 | tf_op jit(solution)/shard_map/ppermute | solution.py:17
  192.9 1.2 copy-start.5
  194.1 3.3 copy-start.4
  197.2 8.7 %collective-permute-start.1 = (bf16[2048,1280]{1,0:T(8,128)(2,1)S(1)}, bf16[2048,1280]{1,0:T(8,128)(2,1)S(1)}, u32[]{:S(2)}, u32[]{:S(2)}) collective-permute-start(bf16[2048,1280]{1,0:T(8,128)(2,1)S(1)} %convolution_convert_fusion), channel_id=1, source_target_pairs={{0,128},{128,0},{1,129},{129,1},{2,130},{130,2},{3,131},{131,3},{4... | collective-permute-start | bytes 15728648 | tf_op jit(solution)/shard_map/ppermute | solution.py:17
  209.6 14.2 %copy-start.8 = (s32[256]{0:T(256)S(1)}, s32[256]{0:T(256)}, u32[]{:S(2)}) copy-start(s32[256]{0:T(256)} %param.16) | copy-start | bytes 3076
  209.6 14.2 %copy-start.10 = (s32[128]{0:T(128)S(1)}, s32[128]{0:T(128)}, u32[]{:S(2)}) copy-start(s32[128]{0:T(128)} %param.15) | copy-start | bytes 1540
  209.6 14.4 %copy-start.9 = (s32[128]{0:T(128)S(1)}, s32[128]{0:T(128)}, u32[]{:S(2)}) copy-start(s32[128]{0:T(128)} %param.17) | copy-start | bytes 1540
  209.6 14.5 %copy-start.7 = (f32[128,6]{0,1:T(8,128)S(1)}, f32[128,6]{0,1:T(8,128)}, u32[]{:S(2)}) copy-start(f32[128,6]{0,1:T(8,128)} %param.14) | copy-start | bytes 9220
  209.6 134.0 %all-to-all-start.1 = ((bf16[128,16,1280]{2,1,0:T(8,128)(2,1)}), bf16[128,16,1280]{2,1,0:T(8,128)(2,1)}, u32[]{:S(2)}, u32[]{:S(2)}) async-start(bf16[128,16,1280]{2,1,0:T(8,128)(2,1)} %bitcast.54), calls=%async_computation.1 | async-start | bytes 10485760 | tf_op jit(solution)/shard_map/all_to_all | solution.py:135
  343.6 3.4 copy-start.6
  343.6 7.6 %copy-start.1 = (bf16[1,2560,8]{1,2,0:T(8,128)(2,1)S(1)}, bf16[1,2560,8]{1,2,0:T(8,128)(2,1)}, u32[]{:S(2)}) copy-start(bf16[1,2560,8]{1,2,0:T(8,128)(2,1)} %param.20) | copy-start | bytes 122884
Sparse Core Ops, SparseCore 0:
  9.9 94.7 all-gather.4
  106.5 73.1 all-gather.6

commit v9 on v7

--- a/solution.py
+++ b/solution.py
@@ -115,7 +115,6 @@
     own_features = lax.dynamic_slice_in_dim(normalized_input, kv_index * half_width, half_width, axis=1)
     down_own = lax.dynamic_slice_in_dim(adapter_down_weight[0], kv_index * half_width, half_width, axis=0)
     rank_half = down_own.shape[1]
-    packed = jnp.concatenate([down_own.T, adapter_up_weight[0]], axis=0)
     flat_ids = expert_choice_index.reshape(-1)
     slot_rank = rank_in_expert(flat_ids, expert_count)
     rank_table = slot_rank.reshape(tok_rows, top_count)
@@ -126,9 +125,11 @@
         pg_size, slot_cap, half_width
     )
     inbox_half = lax.all_to_all(outbox, PG_AXES, split_axis=0, concat_axis=0, tiled=True)
-    packed_all = lax.all_gather(packed, PG_AXES, axis=0, tiled=False)
+    down_gathered = lax.all_gather(down_own.T, PG_AXES, axis=0, tiled=False)
     weights = split_weights(expert_gate_up_weight, expert_down_weight, half_width)
-    inbox_half, packed_all, weights = lax.optimization_barrier((inbox_half, packed_all, weights))
+    inbox_half, down_gathered, weights = lax.optimization_barrier(
+        (inbox_half, down_gathered, weights)
+    )
     half_out = expert_half(inbox_half.reshape(pg_size * slot_cap, half_width), weights)
     results = lax.all_to_all(
         half_out.reshape(pg_size, slot_cap, half_width),
@@ -146,9 +147,10 @@
     request_count = adapter_of_request.shape[0]
     owner_table = request_of_token[:, None] == jnp.arange(request_count, dtype=jnp.int32)[None, :]
     token_adapter = jnp.sum(jnp.where(owner_table, adapter_of_request[None, :], 0), axis=1)
-    slot_count = packed_all.shape[0]
-    down_all = packed_all[:, 0:rank_half, :].reshape(slot_count * rank_half, half_width)
-    up_all = packed_all[:, rank_half:, :].reshape(slot_count * rank_half, half_width)
+    up_gathered = lax.all_gather(adapter_up_weight[0], PG_AXES, axis=0, tiled=False)
+    slot_count = down_gathered.shape[0]
+    down_all = down_gathered.reshape(slot_count * rank_half, half_width)
+    up_all = up_gathered.reshape(slot_count * rank_half, half_width)
     partial_rank = lax.dot_general(
         own_features, down_all, (((1,), (1,)), ((), ())), preferred_element_type=jnp.float32
     )

time: 351 us -> 358 us (1.020)
  waiting for transfers between devices: 243 us -> 253 us
    all_gather x1 -> x2, waiting for transfers between devices: 130 us -> 245 us  [the longest x1 124 us: on_device(): down_gathered = lax.all_gather(down_own.T, PG_AXES, axis=0, tiled=False)]
    all_to_all x1, waiting for transfers between devices: 106 us -> 0.01 us  [on_device(): lax.all_to_all(half_out.reshape(pg_size, slot_cap, half_width), PG_AXES,...]
  transfers between devices with their start and end apart: 5 -> 6, of which waited for: 4 -> 4; matrix products, arithmetic and copies ran while one was open for 10% -> 7% of each run, Pallas kernels for 0% -> 0%
where the time goes in v9:
time: 358 us; the launch traced here: 357 us
  waiting for transfers between devices  253 us (71%)
  matrix products  34.9 us (10%)
  starting transfers between devices  28.4 us (8%)
  between operations  13.7 us (4%)
  other arithmetic  11.8 us (3%)
  local copies, waits for them, and re-layouts  9.47 us (3%)
  blocking collectives  5.59 us (2%)
    all_gather x1, waiting for transfers between devices, on_device(): down_gathered = lax.all_gather(down_own.T, PG_AXES, axis=0, tiled=False)  124 us
    all_gather x1, waiting for transfers between devices, on_device(): lax.all_gather(adapter_up_weight[0], PG_AXES, axis=0, tiled=False)  120 us
    all_to_all x1, starting transfers between devices, on_device(): lax.all_to_all(outbox, PG_AXES, split_axis=0, concat_axis=0, tiled=True)  16.1 us
    all_to_all x1, starting transfers between devices, on_device(): lax.all_to_all(half_out.reshape(pg_size, slot_cap, half_width), PG_AXES,...  12 us
    ppermute x2, waiting for transfers between devices, swap_kv(): return lax.ppermute(values, 'kv', perm=[(0, 1), (1, 0)])  7.55 us
  transfers between devices with their start and end apart: 6, of which 4 were waited for; matrix products, arithmetic and copies ran while one was open for 7% of the time, Pallas kernels for 0%

profile of v9, /device:TPU:2, one launch (start us, length us, event | category | flops | bytes accessed | tf_op | source)
XLA Modules:
  0.0 356.9 jit_solution(16688125799353661403)
XLA Ops:
  6.5 1.2 convert_element_type.73
  7.8 1.3 multiply_reduce_fusion
  9.1 0.8 copy.45
  9.9 0.1 eq.98
  10.0 0.4 fusion.16
  10.4 0.1 convert_element_type.68
  10.6 0.1 copy.46
  10.7 1.7 convert_reduce_fusion
  12.3 0.0 copy-done.7
  12.4 0.1 dynamic-slice.5
  12.4 3.9 %convolution_convert_fusion.2 = bf16[2048,1280]{1,0:T(8,128)(2,1)} fusion(f32[2048,128]{1,0:T(8,128)S(1)} %get-tuple-element.30, f32[2048,128]{1,0:T(8,128)S(1)} %get-tuple-element.29, f32[128,2560]{1,0:T(8,128)S(1)} %convert_element_type.73, s32[]{:T(128)S(6)} %select_n.27, f32[1280]{0:T(1024)S(1)} %dynamic-slice.5, f32[128]{0:T(128)S(1)} %add_rsqrt_fusion), kind=kOutput, calls=%fused_computation.3 | convolution fusion | flops 674725888 | bytes 8004100 | tf_op jit(solution)/shard_map/dot_general | solution.py:73
  16.4 16.1 %all-to-all-start = ((bf16[128,16,1280]{2,1,0:T(8,128)(2,1)}), bf16[128,16,1280]{2,1,0:T(8,128)(2,1)}, u32[]{:S(2)}, u32[]{:S(2)}) async-start(bf16[128,16,1280]{2,1,0:T(8,128)(2,1)} %bitcast.53), calls=%async_computation | async-start | bytes 10485760 | tf_op jit(solution)/shard_map/all_to_all | solution.py:127
  32.4 0.0 all-gather.6.cloned.1.call-start
  32.5 0.6 dynamic-slice_bitcast_fusion.2
  33.1 0.1 all-gather.6.cloned.1.call-update
  33.2 0.0 copy-start.2
  33.2 1.4 dynamic-slice_bitcast_fusion
  34.6 1.4 copy-done.2
  36.0 2.8 constant_dynamic-slice_fusion
  38.8 1.8 copy_bitcast_fusion
  40.6 124.3 %all-gather.6.cloned.1.call-done = bf16[1024,1280]{1,0:T(8,128)(2,1)} async-done(((bf16[8,1280]{1,0:T(8,128)(2,1)}), bf16[1024,1280]{1,0:T(8,128)(2,1)}) %all-gather.6.cloned.1.call-update) | async-done | bytes 2621456 | tf_op jit(solution)/shard_map/all_gather | solution.py:128
  164.9 0.0 all-to-all-done
  164.9 0.0 collective-permute-start
  164.9 6.8 %fusion.28 = f32[2048,2,384]{2,0,1:T(8,128)S(1)} fusion(bf16[2048,1280,1]{1,0,2:T(8,128)(2,1)} %bitcast.9, bf16[1280,2,384]{2,0,1:T(8,128)(2,1)} %get-tuple-element.14), kind=kOutput, calls=%fused_computation.60 | convolution fusion | flops 4026531840 | bytes 13500416 | tf_op jit(solution)/shard_map/rd,dgf->rgf/dot_general | solution.py:23
  171.6 2.1 collective-permute-done
  173.7 4.3 %fusion.2 = f32[2048,2,384]{2,0,1:T(8,128)S(1)} fusion(f32[2048,2,384]{2,0,1:T(8,128)S(1)} %fusion.28, bf16[1280,2,384]{2,0,1:T(8,128)(2,1)S(1)} %get-tuple-element.15, bf16[2048,1280]{1,0:T(8,128)(2,1)S(1)} %collective-permute-done), kind=kOutput, calls=%fused_computation.14 | convolution fusion | flops 4028104704 | bytes 19791872 | tf_op jit(solution)/shard_map/rd,dgf->rgf/dot_general | solution.py:25
  178.1 0.9 fusion.6
  179.0 0.3 copy-done.5
  179.3 3.1 convolution_convert_fusion
  182.3 0.2 collective-permute-start.1
  182.6 3.0 convolution_convert_fusion.1
  185.6 5.5 %collective-permute-done.1 = bf16[2048,1280]{1,0:T(8,128)(2,1)S(1)} collective-permute-done((bf16[2048,1280]{1,0:T(8,128)(2,1)S(1)}, bf16[2048,1280]{1,0:T(8,128)(2,1)S(1)}, u32[]{:S(2)}, u32[]{:S(2)}) %collective-permute-start.1) | collective-permute-done | bytes 5242912 | tf_op jit(solution)/shard_map/ppermute | solution.py:17
  191.1 3.9 %add_convert_fusion = bf16[2048,1280]{1,0:T(8,128)(2,1)} fusion(bf16[2048,1280]{1,0:T(8,128)(2,1)S(1)} %collective-permute-done.1, bf16[2048,1280]{1,0:T(8,128)(2,1)S(1)} %convolution_convert_fusion.1), kind=kLoop, calls=%fused_computation | loop fusion | flops 10485760 | bytes 15728640 | tf_op jit(solution)/shard_map/convert_element_type | solution.py:35
  195.0 12.0 %all-to-all-start.1 = ((bf16[128,16,1280]{2,1,0:T(8,128)(2,1)}), bf16[128,16,1280]{2,1,0:T(8,128)(2,1)}, u32[]{:S(2)}, u32[]{:S(2)}) async-start(bf16[128,16,1280]{2,1,0:T(8,128)(2,1)} %bitcast.54), calls=%async_computation.1 | async-start | bytes 10485760 | tf_op jit(solution)/shard_map/all_to_all | solution.py:134
  207.0 0.0 all-gather.4.cloned.1.call-start
  207.1 0.7 all-gather.4.cloned.1.call-update
  207.8 0.2 select_reduce_fusion.2
  208.0 0.1 broadcast_compare_fusion
  208.1 2.5 select_reduce_fusion
  210.6 3.5 fusion.12
  214.1 5.6 %all-reduce.1 = bf16[128,128,8]{0,2,1:T(8,128)(2,1)S(1)} all-reduce(f32[128,128,8]{0,2,1:T(8,128)} %fusion.12), channel_id=1, replica_groups=mesh['kv'=2,'px'=4,'pz'=8,'py'=4] {'kv'}, use_global_device_ids=true, to_apply=%region_7.8 | all-reduce | flops 131072 | bytes 786432 | tf_op jit(solution)/shard_map/psum | solution.py:157
  219.7 120.4 %all-gather.4.cloned.1.call-done = bf16[128,8,1280]{2,1,0:T(8,128)(2,1)} async-done(((bf16[1,8,1280]{2,1,0:T(8,128)(2,1)}), bf16[128,8,1280]{2,1,0:T(8,128)(2,1)}) %all-gather.4.cloned.1.call-update) | async-done | bytes 2621456 | tf_op jit(solution)/shard_map/all_gather | solution.py:150
  340.0 2.3 convolution_bitcast_fusion
  342.4 0.0 all-to-all-done.1
  342.4 0.0 copy-start.1
  342.4 3.4 fusion.20
  345.8 4.2 %fusion.10 = bf16[128,1280]{1,0:T(8,128)(2,1)} fusion(f32[128,1280]{1,0:T(8,128)S(1)} %convolution_bitcast_fusion, f32[128,1280]{1,0:T(8,128)S(1)} %fusion.20, bf16[2048,1280]{1,0:T(8,128)(2,1)} %bitcast.14, f32[128,2048]{1,0:T(8,128)S(1)} %get-tuple-element.22, f32[128,2048]{1,0:T(8,128)S(1)} %get-tuple-element.21), kind=kOutput, calls=%fused_computation.24 | convolution fusion | flops 672890880 | bytes 8978432 | tf_op jit(solution)/shard_map/dot_general | solution.py:89
  350.0 0.0 copy-done.1
  (21 shorter events, 0.1 us)
Async XLA Ops:
  6.5 26.0 %copy-start = (bf16[1,2560,8]{1,2,0:T(8,128)(2,1)S(1)}, bf16[1,2560,8]{1,2,0:T(8,128)(2,1)}, u32[]{:S(2)}) copy-start(bf16[1,2560,8]{1,2,0:T(8,128)(2,1)} %param.20) | copy-start | bytes 122884
  6.5 4.1 %copy-start.6 = (s32[128,6]{0,1:T(8,128)S(1)}, s32[128,6]{0,1:T(8,128)}, u32[]{:S(2)}) copy-start(s32[128,6]{0,1:T(8,128)} %param.13) | copy-start | bytes 9220
  6.5 5.8 %copy-start.7 = (f32[2560]{0:T(1024)S(1)}, f32[2560]{0:T(1024)}, u32[]{:S(2)}) copy-start(f32[2560]{0:T(1024)} %param.12) | copy-start | bytes 30724
  16.4 16.8 %copy-start.3 = (bf16[1,384,2560]{2,1,0:T(8,128)(2,1)S(1)}, bf16[1,384,2560]{2,1,0:T(8,128)(2,1)}, u32[]{:S(2)}) copy-start(bf16[1,384,2560]{2,1,0:T(8,128)(2,1)} %param.19) | copy-start | bytes 5898244
  16.4 148.5 %all-to-all-start = ((bf16[128,16,1280]{2,1,0:T(8,128)(2,1)}), bf16[128,16,1280]{2,1,0:T(8,128)(2,1)}, u32[]{:S(2)}, u32[]{:S(2)}) async-start(bf16[128,16,1280]{2,1,0:T(8,128)(2,1)} %bitcast.53), calls=%async_computation | async-start | bytes 10485760 | tf_op jit(solution)/shard_map/all_to_all | solution.py:127
  32.4 132.4 %all-gather.6.cloned.1.call-start = ((), (), s32[]{:S(2)}) async-start(), calls=%async_computation.3 | async-start | bytes 2641920 | tf_op jit(solution)/shard_map/all_gather | solution.py:128
  33.2 2.8 copy-start.2
  164.9 8.9 %collective-permute-start = (bf16[2048,1280]{1,0:T(8,128)(2,1)}, bf16[2048,1280]{1,0:T(8,128)(2,1)S(1)}, u32[]{:S(2)}, u32[]{:S(2)}) collective-permute-start(bf16[2048,1280]{1,0:T(8,128)(2,1)} %bitcast.8), channel_id=1, source_target_pairs={{0,128},{128,0},{1,129},{129,1},{2,130},{130,2},{3,131},{131,3},{4... | collective-permute-start | bytes 15728648 | tf_op jit(solution)/shard_map/ppermute | solution.py:17
  178.1 1.2 copy-start.5
  179.3 3.3 copy-start.4
  182.3 8.7 %collective-permute-start.1 = (bf16[2048,1280]{1,0:T(8,128)(2,1)S(1)}, bf16[2048,1280]{1,0:T(8,128)(2,1)S(1)}, u32[]{:S(2)}, u32[]{:S(2)}) collective-permute-start(bf16[2048,1280]{1,0:T(8,128)(2,1)S(1)} %convolution_convert_fusion), channel_id=1, source_target_pairs={{0,128},{128,0},{1,129},{129,1},{2,130},{130,2},{3,131},{131,3},{4... | collective-permute-start | bytes 15728648 | tf_op jit(solution)/shard_map/ppermute | solution.py:17
  195.0 12.8 %copy-start.9 = (s32[256]{0:T(256)S(1)}, s32[256]{0:T(256)}, u32[]{:S(2)}) copy-start(s32[256]{0:T(256)} %param.16) | copy-start | bytes 3076
  195.0 12.8 %copy-start.11 = (s32[128]{0:T(128)S(1)}, s32[128]{0:T(128)}, u32[]{:S(2)}) copy-start(s32[128]{0:T(128)} %param.15) | copy-start | bytes 1540
  195.0 13.0 %copy-start.10 = (s32[128]{0:T(128)S(1)}, s32[128]{0:T(128)}, u32[]{:S(2)}) copy-start(s32[128]{0:T(128)} %param.17) | copy-start | bytes 1540
  195.0 13.1 %copy-start.8 = (f32[128,6]{0,1:T(8,128)S(1)}, f32[128,6]{0,1:T(8,128)}, u32[]{:S(2)}) copy-start(f32[128,6]{0,1:T(8,128)} %param.14) | copy-start | bytes 9220
  195.0 147.4 %all-to-all-start.1 = ((bf16[128,16,1280]{2,1,0:T(8,128)(2,1)}), bf16[128,16,1280]{2,1,0:T(8,128)(2,1)}, u32[]{:S(2)}, u32[]{:S(2)}) async-start(bf16[128,16,1280]{2,1,0:T(8,128)(2,1)} %bitcast.54), calls=%async_computation.1 | async-start | bytes 10485760 | tf_op jit(solution)/shard_map/all_to_all | solution.py:134
  207.0 133.0 %all-gather.4.cloned.1.call-start = ((), (), s32[]{:S(2)}) async-start(), calls=%async_computation.2 | async-start | bytes 2641920 | tf_op jit(solution)/shard_map/all_gather | solution.py:150
  342.4 7.6 %copy-start.1 = (bf16[1,2560,8]{1,2,0:T(8,128)(2,1)S(1)}, bf16[1,2560,8]{1,2,0:T(8,128)(2,1)}, u32[]{:S(2)}) copy-start(bf16[1,2560,8]{1,2,0:T(8,128)(2,1)} %param.20) | copy-start | bytes 122884
Sparse Core Ops, SparseCore 0:
  36.9 127.9 all-gather.5
  211.5 128.4 all-gather.3

commit v10 on v8

--- a/solution.py
+++ b/solution.py
@@ -11,6 +11,29 @@
     values = states.astype(jnp.float32)
     inverse_rms = lax.rsqrt(jnp.mean(values * values, axis=-1, keepdims=True) + 1e-06)
     return (values * inverse_rms * gain_vector).astype(jnp.bfloat16)
+
+
+def shift_gather(block, axis_name):
+    count = lax.axis_size(axis_name)
+    pieces = [block]
+    for shift in range(1, count):
+        pieces.append(
+            lax.ppermute(
+                block, axis_name, perm=[(j, (j + shift) % count) for j in range(count)]
+            )
+        )
+    return jnp.stack(pieces)
+
+
+def gathered_slot_order():
+    x_axis, z_axis, y_axis = PG_AXES
+    y_count = lax.axis_size(y_axis)
+    x_ids = jnp.arange(lax.axis_size(x_axis), dtype=jnp.int32)
+    z_ids = jnp.arange(lax.axis_size(z_axis), dtype=jnp.int32)
+    y_src = (lax.axis_index(y_axis).astype(jnp.int32) - jnp.arange(y_count, dtype=jnp.int32)) % y_count
+    z_count = z_ids.shape[0]
+    slot = (x_ids[:, None, None] * z_count + z_ids[None, :, None]) * y_count + y_src[None, None, :]
+    return slot.reshape(-1)
 
 
 def swap_kv(values):
@@ -125,10 +148,13 @@
     outbox = place_rows((first_slot, second_slot), slot_total, own_features).reshape(
         pg_size, slot_cap, half_width
     )
+    packed_near = shift_gather(packed, PG_AXES[2])
+    outbox, packed_near = lax.optimization_barrier((outbox, packed_near))
     inbox_half = lax.all_to_all(outbox, PG_AXES, split_axis=0, concat_axis=0, tiled=True)
-    packed_all = lax.all_gather(packed, PG_AXES[1:], axis=0, tiled=False)
+    packed_all = lax.all_gather(packed_near, PG_AXES[1], axis=0, tiled=False)
     packed_all = lax.all_gather(packed_all, PG_AXES[0], axis=0, tiled=False)
     packed_all = packed_all.reshape((pg_size,) + packed.shape)
+    adapter_of_position = adapter_of_slot[gathered_slot_order()]
     weights = split_weights(expert_gate_up_weight, expert_down_weight, half_width)
     inbox_half, packed_all, weights = lax.optimization_barrier((inbox_half, packed_all, weights))
     half_out = expert_half(inbox_half.reshape(pg_size * slot_cap, half_width), weights)
@@ -155,7 +181,7 @@
         own_features, down_all, (((1,), (1,)), ((), ())), preferred_element_type=jnp.float32
     )
     rank_projected = lax.psum(partial_rank, "kv").reshape(tok_rows, slot_count, rank_half)
-    matched = adapter_of_slot[None, :, None] == token_adapter[:, None, None]
+    matched = adapter_of_position[None, :, None] == token_adapter[:, None, None]
     rank_projected = jnp.where(matched, rank_projected, 0.0).astype(jnp.bfloat16)
     flat_low = rank_projected.reshape(tok_rows, slot_count * rank_half)
     adapter_total_output = jnp.dot(flat_low, up_all, preferred_element_type=jnp.float32)

time: 359 us -> 363 us (1.011)
    all_gather x1, waiting for transfers between devices: 17.7 us -> 73.5 us  [on_device(): packed_all = lax.all_gather(packed_all, PG_AXES[0], axis=0, tiled=False)]
    all_to_all x1, waiting for transfers between devices: 49.9 us -> 0.01 us  [on_device(): lax.all_to_all(outbox, PG_AXES, split_axis=0, concat_axis=0, tiled=True)]
    all_gather x1, waiting for transfers between devices: 68.7 us -> 62.6 us  [on_device(): packed_all = lax.all_gather(packed_near, PG_AXES[1], axis=0, tiled=False)]
    ppermute x0 -> x3, starting transfers between devices: none -> 4.61 us  [shift_gather(): lax.ppermute(block, axis_name, perm=[(j, (j + shift) % count) for j in ra...]
  transfers between devices with their start and end apart: 6 -> 9, of which waited for: 6 -> 5; matrix products, arithmetic and copies ran while one was open for 10% -> 10% of each run, Pallas kernels for 0% -> 0%
where the time goes in v10:
time: 363 us; the launch traced here: 362 us
  waiting for transfers between devices  248 us (68%)
  matrix products  35.8 us (10%)
  starting transfers between devices  33.9 us (9%)
  other arithmetic  13.9 us (4%)
  between operations  13.7 us (4%)
  local copies, waits for them, and re-layouts  11.7 us (3%)
  blocking collectives  5.58 us (2%)
    all_to_all x1, waiting for transfers between devices, on_device(): lax.all_to_all(half_out.reshape(pg_size, slot_cap, half_width), PG_AXES,...  103 us
    all_gather x1, waiting for transfers between devices, on_device(): packed_all = lax.all_gather(packed_all, PG_AXES[0], axis=0, tiled=False)  73.5 us
    all_gather x1, waiting for transfers between devices, on_device(): packed_all = lax.all_gather(packed_near, PG_AXES[1], axis=0, tiled=False)  62.6 us
    all_to_all x1, starting transfers between devices, on_device(): lax.all_to_all(outbox, PG_AXES, split_axis=0, concat_axis=0, tiled=True)  15.1 us
    all_to_all x1, starting transfers between devices, on_device(): lax.all_to_all(half_out.reshape(pg_size, slot_cap, half_width), PG_AXES,...  13.8 us
    ppermute x2, waiting for transfers between devices, swap_kv(): return lax.ppermute(values, 'kv', perm=[(0, 1), (1, 0)])  7.51 us
  transfers between devices with their start and end apart: 9, of which 5 were waited for; matrix products, arithmetic and copies ran while one was open for 10% of the time, Pallas kernels for 0%

profile of v10, /device:TPU:2, one launch (start us, length us, event | category | flops | bytes accessed | tf_op | source)
XLA Modules:
  0.0 362.0 jit_solution(12727029166916439450)
XLA Ops:
  6.5 0.8 copy-done
  7.3 0.7 fusion.34
  8.1 3.0 collective-permute-start.2
  11.1 0.6 collective-permute-start.1
  11.7 1.0 collective-permute-start
  12.7 1.2 convert_element_type.73
  13.9 1.3 multiply_reduce_fusion
  15.2 0.8 copy.53
  16.0 0.1 eq.100
  16.1 0.4 fusion.22
  16.5 0.1 convert_element_type.68
  16.7 0.7 broadcast_add_fusion.1
  17.4 0.8 dynamic-slice.5
  18.2 1.7 convert_reduce_fusion
  19.9 4.0 %convolution_convert_fusion.2 = bf16[2048,1280]{1,0:T(8,128)(2,1)} fusion(f32[2048,128]{1,0:T(8,128)S(1)} %get-tuple-element.36, f32[2048,128]{1,0:T(8,128)S(1)} %get-tuple-element.35, f32[128,2560]{1,0:T(8,128)S(1)} %convert_element_type.73, s32[]{:T(128)S(6)} %select_n.48, f32[1280]{0:T(1024)S(1)} %dynamic-slice.5, f32[128]{0:T(128)S(1)} %add_rsqrt_fusion), kind=kOutput, calls=%fused_computation.4 | convolution fusion | flops 674725888 | bytes 8004100 | tf_op jit(solution)/shard_map/dot_general | solution.py:96
  23.9 0.7 pad_maximum_fusion
  24.6 15.1 %all-to-all-start = ((bf16[128,16,1280]{2,1,0:T(8,128)(2,1)}), bf16[128,16,1280]{2,1,0:T(8,128)(2,1)}, u32[]{:S(2)}, u32[]{:S(2)}) async-start(bf16[128,16,1280]{2,1,0:T(8,128)(2,1)} %bitcast.61), calls=%async_computation | async-start | bytes 10485760 | tf_op jit(solution)/shard_map/all_to_all | solution.py:153
  39.8 0.7 all-gather.5.cloned.1.call-update
  40.5 62.6 %all-gather.5.cloned.1.call-done = bf16[32,16,1280]{2,1,0:T(8,128)(2,1)} async-done(((bf16[4,16,1280]{2,1,0:T(8,128)(2,1)}), bf16[32,16,1280]{2,1,0:T(8,128)(2,1)}) %all-gather.5.cloned.1.call-update) | async-done | bytes 1310736 | tf_op jit(solution)/shard_map/all_gather | solution.py:154
  103.2 1.4 dynamic-slice_bitcast_fusion
  104.6 1.4 copy-done.3
  106.0 2.8 constant_dynamic-slice_fusion
  108.8 1.8 copy_bitcast_fusion
  110.5 73.5 %all-gather.7.cloned.1.call-done = bf16[32,4,16,1280]{3,2,1,0:T(8,128)(2,1)} async-done(((bf16[8,4,16,1280]{3,2,1,0:T(8,128)(2,1)}), bf16[32,4,16,1280]{3,2,1,0:T(8,128)(2,1)}) %all-gather.7.cloned.1.call-update) | async-done | bytes 5242896 | tf_op jit(solution)/shard_map/all_gather | solution.py:155
  184.1 6.8 %fusion.37 = f32[2048,2,384]{2,0,1:T(8,128)S(1)} fusion(bf16[2048,1280,1]{1,0,2:T(8,128)(2,1)} %bitcast.15, bf16[1280,2,384]{2,0,1:T(8,128)(2,1)} %get-tuple-element.18), kind=kOutput, calls=%fused_computation.77 | convolution fusion | flops 4026531840 | bytes 13500416 | tf_op jit(solution)/shard_map/rd,dgf->rgf/dot_general | solution.py:46
  190.8 2.0 collective-permute-done.3
  192.9 4.3 %fusion.2 = f32[2048,2,384]{2,0,1:T(8,128)S(1)} fusion(f32[2048,2,384]{2,0,1:T(8,128)S(1)} %fusion.37, bf16[1280,2,384]{2,0,1:T(8,128)(2,1)S(1)} %get-tuple-element.19, bf16[2048,1280]{1,0:T(8,128)(2,1)S(1)} %collective-permute-done.3), kind=kOutput, calls=%fused_computation.15 | convolution fusion | flops 4028104704 | bytes 19791872 | tf_op jit(solution)/shard_map/rd,dgf->rgf/dot_general | solution.py:48
  197.2 0.9 fusion.6
  198.1 0.3 copy-done.6
  198.4 3.1 convolution_convert_fusion
  201.5 0.2 collective-permute-start.4
  201.7 3.0 convolution_convert_fusion.1
  204.8 5.5 %collective-permute-done.4 = bf16[2048,1280]{1,0:T(8,128)(2,1)S(1)} collective-permute-done((bf16[2048,1280]{1,0:T(8,128)(2,1)S(1)}, bf16[2048,1280]{1,0:T(8,128)(2,1)S(1)}, u32[]{:S(2)}, u32[]{:S(2)}) %collective-permute-start.4) | collective-permute-done | bytes 5242912 | tf_op jit(solution)/shard_map/ppermute | solution.py:40
  210.2 3.7 %add_convert_fusion = bf16[2048,1280]{1,0:T(8,128)(2,1)} fusion(bf16[2048,1280]{1,0:T(8,128)(2,1)S(1)} %collective-permute-done.4, bf16[2048,1280]{1,0:T(8,128)(2,1)S(1)} %convolution_convert_fusion.1), kind=kLoop, calls=%fused_computation.1 | loop fusion | flops 10485760 | bytes 15728640 | tf_op jit(solution)/shard_map/convert_element_type | solution.py:58
  213.9 13.8 %all-to-all-start.1 = ((bf16[128,16,1280]{2,1,0:T(8,128)(2,1)}), bf16[128,16,1280]{2,1,0:T(8,128)(2,1)}, u32[]{:S(2)}, u32[]{:S(2)}) async-start(bf16[128,16,1280]{2,1,0:T(8,128)(2,1)} %bitcast.62), calls=%async_computation.1 | async-start | bytes 10485760 | tf_op jit(solution)/shard_map/all_to_all | solution.py:161
  227.7 0.1 add_multiply_fusion
  227.8 0.1 broadcast_add_fusion
  227.8 0.1 add.138
  228.0 1.2 gather_fusion
  229.2 0.2 select_reduce_fusion.2
  229.4 0.1 broadcast_compare_fusion
  229.5 2.5 select_reduce_fusion
  232.0 3.5 fusion.18
  235.5 5.6 %all-reduce.1 = bf16[128,128,8]{0,2,1:T(8,128)(2,1)S(1)} all-reduce(f32[128,128,8]{0,2,1:T(8,128)} %fusion.18), channel_id=1, replica_groups=mesh['kv'=2,'px'=4,'pz'=8,'py'=4] {'kv'}, use_global_device_ids=true, to_apply=%region_7.8 | all-reduce | flops 131072 | bytes 786432 | tf_op jit(solution)/shard_map/psum | solution.py:183
  241.1 3.2 fusion.13
  244.3 103.2 %all-to-all-done.1 = bf16[128,16,1280]{2,1,0:T(8,128)(2,1)} async-done(((bf16[128,16,1280]{2,1,0:T(8,128)(2,1)}), bf16[128,16,1280]{2,1,0:T(8,128)(2,1)}, u32[]{:S(2)}, u32[]{:S(2)}) %all-to-all-start.1) | async-done | bytes 5242912 | tf_op jit(solution)/shard_map/all_to_all | solution.py:161
  347.5 3.4 fusion.26
  350.9 4.2 %fusion.16 = bf16[128,1280]{1,0:T(8,128)(2,1)} fusion(f32[128,1280]{1,0:T(8,128)S(1)} %copy-done.7, f32[128,1280]{1,0:T(8,128)S(1)} %fusion.26, bf16[2048,1280]{1,0:T(8,128)(2,1)} %bitcast.20, f32[128,2048]{1,0:T(8,128)S(1)} %get-tuple-element.26, f32[128,2048]{1,0:T(8,128)S(1)} %get-tuple-element.25), kind=kOutput, calls=%fused_computation.28 | convolution fusion | flops 672890880 | bytes 8978432 | tf_op jit(solution)/shard_map/dot_general | solution.py:112
  (35 shorter events, 0.3 us)
Async XLA Ops:
  6.5 0.8 copy-start
  8.1 15.8 %collective-permute-start.2 = (bf16[16,1280]{1,0:T(8,128)(2,1)S(1)}, bf16[16,1280]{1,0:T(8,128)(2,1)S(1)}, u32[]{:S(2)}, u32[]{:S(2)}) collective-permute-start(bf16[16,1280]{1,0:T(8,128)(2,1)S(1)} %get-tuple-element.34), channel_id=1, source_target_pairs={{0,3},{1,0},{2,1},{3,2},{4,7},{5,4},{6,5},{7,6},{8,11},{9,8},{10,9... | collective-permute-start | bytes 122888 | tf_op jit(solution)/shard_map/ppermute | solution.py:21
  11.1 12.8 %collective-permute-start.1 = (bf16[16,1280]{1,0:T(8,128)(2,1)S(1)}, bf16[16,1280]{1,0:T(8,128)(2,1)S(1)}, u32[]{:S(2)}, u32[]{:S(2)}) collective-permute-start(bf16[16,1280]{1,0:T(8,128)(2,1)S(1)} %get-tuple-element.34), channel_id=1, source_target_pairs={{0,2},{1,3},{2,0},{3,1},{4,6},{5,7},{6,4},{7,5},{8,10},{9,11},{10,... | collective-permute-start | bytes 122888 | tf_op jit(solution)/shard_map/ppermute | solution.py:21
  11.7 12.2 %collective-permute-start = (bf16[16,1280]{1,0:T(8,128)(2,1)S(1)}, bf16[16,1280]{1,0:T(8,128)(2,1)S(1)}, u32[]{:S(2)}, u32[]{:S(2)}) collective-permute-start(bf16[16,1280]{1,0:T(8,128)(2,1)S(1)} %get-tuple-element.34), channel_id=1, source_target_pairs={{0,1},{1,2},{2,3},{3,0},{4,5},{5,6},{6,7},{7,4},{8,9},{9,10},{10,1... | collective-permute-start | bytes 122888 | tf_op jit(solution)/shard_map/ppermute | solution.py:21
  24.6 78.6 %copy-start.4 = (bf16[1,384,2560]{2,1,0:T(8,128)(2,1)S(1)}, bf16[1,384,2560]{2,1,0:T(8,128)(2,1)}, u32[]{:S(2)}) copy-start(bf16[1,384,2560]{2,1,0:T(8,128)(2,1)} %param.19) | copy-start | bytes 5898244
  24.6 159.4 %all-to-all-start = ((bf16[128,16,1280]{2,1,0:T(8,128)(2,1)}), bf16[128,16,1280]{2,1,0:T(8,128)(2,1)}, u32[]{:S(2)}, u32[]{:S(2)}) async-start(bf16[128,16,1280]{2,1,0:T(8,128)(2,1)} %bitcast.61), calls=%async_computation | async-start | bytes 10485760 | tf_op jit(solution)/shard_map/all_to_all | solution.py:153
  39.7 63.4 %all-gather.5.cloned.1.call-start = ((), (), s32[]{:S(2)}) async-start(), calls=%async_computation.2 | async-start | bytes 1474560 | tf_op jit(solution)/shard_map/all_gather | solution.py:154
  40.5 143.5 %all-gather.7.cloned.1.call-start = ((), (), s32[]{:S(2)}) async-start(), calls=%async_computation.3 | async-start | bytes 6553600 | tf_op jit(solution)/shard_map/all_gather | solution.py:155
  103.2 2.8 copy-start.3
  184.0 8.9 %collective-permute-start.3 = (bf16[2048,1280]{1,0:T(8,128)(2,1)}, bf16[2048,1280]{1,0:T(8,128)(2,1)S(1)}, u32[]{:S(2)}, u32[]{:S(2)}) collective-permute-start(bf16[2048,1280]{1,0:T(8,128)(2,1)} %bitcast.14), channel_id=1, source_target_pairs={{0,128},{128,0},{1,129},{129,1},{2,130},{130,2},{3,131},{131,3},{4... | collective-permute-start | bytes 15728648 | tf_op jit(solution)/shard_map/ppermute | solution.py:40
  197.2 1.2 copy-start.6
  198.4 3.3 copy-start.5
  201.5 8.7 %collective-permute-start.4 = (bf16[2048,1280]{1,0:T(8,128)(2,1)S(1)}, bf16[2048,1280]{1,0:T(8,128)(2,1)S(1)}, u32[]{:S(2)}, u32[]{:S(2)}) collective-permute-start(bf16[2048,1280]{1,0:T(8,128)(2,1)S(1)} %convolution_convert_fusion), channel_id=1, source_target_pairs={{0,128},{128,0},{1,129},{129,1},{2,130},{130,2},{3,131},{131,3},{4... | collective-permute-start | bytes 15728648 | tf_op jit(solution)/shard_map/ppermute | solution.py:40
  213.9 14.1 %copy-start.2 = (s32[128]{0:T(128)S(1)}, s32[128]{0:T(128)}, u32[]{:S(2)}) copy-start(s32[128]{0:T(128)} %param.17) | copy-start | bytes 1540
  213.9 15.3 %copy-start.9 = (s32[256]{0:T(256)S(1)}, s32[256]{0:T(256)}, u32[]{:S(2)}) copy-start(s32[256]{0:T(256)} %param.16) | copy-start | bytes 3076
  213.9 15.3 %copy-start.10 = (s32[128]{0:T(128)S(1)}, s32[128]{0:T(128)}, u32[]{:S(2)}) copy-start(s32[128]{0:T(128)} %param.15) | copy-start | bytes 1540
  213.9 15.6 %copy-start.8 = (f32[128,6]{0,1:T(8,128)S(1)}, f32[128,6]{0,1:T(8,128)}, u32[]{:S(2)}) copy-start(f32[128,6]{0,1:T(8,128)} %param.14) | copy-start | bytes 9220
  213.9 133.6 %all-to-all-start.1 = ((bf16[128,16,1280]{2,1,0:T(8,128)(2,1)}), bf16[128,16,1280]{2,1,0:T(8,128)(2,1)}, u32[]{:S(2)}, u32[]{:S(2)}) async-start(bf16[128,16,1280]{2,1,0:T(8,128)(2,1)} %bitcast.62), calls=%async_computation.1 | async-start | bytes 10485760 | tf_op jit(solution)/shard_map/all_to_all | solution.py:161
  347.5 3.4 copy-start.7
  347.5 7.6 %copy-start.1 = (bf16[1,2560,8]{1,2,0:T(8,128)(2,1)S(1)}, bf16[1,2560,8]{1,2,0:T(8,128)(2,1)}, u32[]{:S(2)}) copy-start(bf16[1,2560,8]{1,2,0:T(8,128)(2,1)} %param.20) | copy-start | bytes 122884
Sparse Core Ops, SparseCore 0:
  42.3 60.7 all-gather.4
  104.9 79.0 all-gather.6

commit v11 on v7

--- a/solution.py
+++ b/solution.py
@@ -18,21 +18,21 @@
 
 
 def expert_half(own_rows, weights):
-    own_weight, other_weight, own_cols, other_cols = weights
+    own_weight, other_weight, own_units_down, other_units_down = weights
     other_rows = swap_kv(own_rows)
     gate_up = jnp.einsum(
         "rd,dgf->rgf", own_rows, own_weight, preferred_element_type=jnp.float32
     ) + jnp.einsum("rd,dgf->rgf", other_rows, other_weight, preferred_element_type=jnp.float32)
-    hidden = (jax.nn.silu(gate_up[:, 0]) * gate_up[:, 1]).astype(jnp.bfloat16)
-    sent_quarter = jnp.dot(hidden, other_cols, preferred_element_type=jnp.float32).astype(
+    own_hidden = (jax.nn.silu(gate_up[:, 0]) * gate_up[:, 1]).astype(jnp.bfloat16)
+    other_hidden = swap_kv(own_hidden)
+    own_quarter = jnp.dot(own_hidden, own_units_down, preferred_element_type=jnp.float32).astype(
         jnp.bfloat16
     )
-    received_quarter = swap_kv(sent_quarter)
-    own_quarter = jnp.dot(hidden, own_cols, preferred_element_type=jnp.float32).astype(
-        jnp.bfloat16
-    )
-    own_quarter, received_quarter = lax.optimization_barrier((own_quarter, received_quarter))
-    return (own_quarter.astype(jnp.float32) + received_quarter.astype(jnp.float32)).astype(
+    other_quarter = jnp.dot(
+        other_hidden, other_units_down, preferred_element_type=jnp.float32
+    ).astype(jnp.bfloat16)
+    own_quarter, other_quarter = lax.optimization_barrier((own_quarter, other_quarter))
+    return (own_quarter.astype(jnp.float32) + other_quarter.astype(jnp.float32)).astype(
         jnp.bfloat16
     )
 
@@ -45,9 +45,10 @@
         gate_up_weight, (1 - kv_index) * half_width, half_width, 0
     )
     down_weight = expert_down_weight[0]
-    own_cols = lax.dynamic_slice_in_dim(down_weight, kv_index * half_width, half_width, 1)
-    other_cols = lax.dynamic_slice_in_dim(down_weight, (1 - kv_index) * half_width, half_width, 1)
-    return own_weight, other_weight, own_cols, other_cols
+    own_units_down = lax.dynamic_slice_in_dim(down_weight, kv_index * half_width, half_width, 1)
+    lent_down = lax.dynamic_slice_in_dim(down_weight, (1 - kv_index) * half_width, half_width, 1)
+    other_units_down = swap_kv(lent_down)
+    return own_weight, other_weight, own_units_down, other_units_down
 
 
 def rank_in_expert(flat_ids, expert_count):

time: 351 us -> 356 us (1.014)
  waiting for transfers between devices: 243 us -> 247 us
    ppermute x2 -> x3, waiting for transfers between devices: 7.5 us -> 9.01 us  [swap_kv(): return lax.ppermute(values, 'kv', perm=[(0, 1), (1, 0)])]
  transfers between devices with their start and end apart: 5 -> 6, of which waited for: 4 -> 4; matrix products, arithmetic and copies ran while one was open for 10% -> 7% of each run, Pallas kernels for 0% -> 0%
where the time goes in v11:
time: 356 us; the launch traced here: 355 us
  waiting for transfers between devices  247 us (69%)
  matrix products  35.8 us (10%)
  starting transfers between devices  29 us (8%)
  other arithmetic  13.9 us (4%)
  between operations  13.6 us (4%)
  local copies, waits for them, and re-layouts  9.75 us (3%)
  blocking collectives  5.59 us (2%)
    all_gather x1, waiting for transfers between devices, on_device(): packed_all = lax.all_gather(packed, PG_AXES, axis=0, tiled=False)  130 us
    all_to_all x1, waiting for transfers between devices, on_device(): lax.all_to_all(half_out.reshape(pg_size, slot_cap, half_width), PG_AXES,...  108 us
    all_to_all x1, starting transfers between devices, on_device(): lax.all_to_all(outbox, PG_AXES, split_axis=0, concat_axis=0, tiled=True)  16.1 us
    all_to_all x1, starting transfers between devices, on_device(): lax.all_to_all(half_out.reshape(pg_size, slot_cap, half_width), PG_AXES,...  12.7 us
    ppermute x3, waiting for transfers between devices, swap_kv(): return lax.ppermute(values, 'kv', perm=[(0, 1), (1, 0)])  9.01 us
  transfers between devices with their start and end apart: 6, of which 4 were waited for; matrix products, arithmetic and copies ran while one was open for 7% of the time, Pallas kernels for 0%

profile of v11, /device:TPU:2, one launch (start us, length us, event | category | flops | bytes accessed | tf_op | source)
XLA Modules:
  0.0 355.2 jit_solution(14761507038634751660)
XLA Ops:
  6.5 0.0 all-gather.3.cloned.1.call-start
  6.5 0.8 copy-done
  7.3 1.3 pad_maximum_fusion
  8.7 0.0 all-gather.3.cloned.1.call-update
  8.7 1.2 convert_element_type.73
  9.9 1.3 multiply_reduce_fusion
  11.2 0.8 dynamic-slice.5
  12.0 0.8 copy.37
  12.8 0.1 eq.98
  12.9 0.4 fusion.23
  13.3 0.1 convert_element_type.68
  13.5 0.1 copy.38
  13.5 0.7 broadcast_add_fusion
  14.2 1.7 convert_reduce_fusion
  15.9 4.0 %convolution_convert_fusion.2 = bf16[2048,1280]{1,0:T(8,128)(2,1)} fusion(f32[2048,128]{1,0:T(8,128)S(1)} %get-tuple-element.30, f32[2048,128]{1,0:T(8,128)S(1)} %get-tuple-element.29, f32[128,2560]{1,0:T(8,128)S(1)} %convert_element_type.73, s32[]{:T(128)S(6)} %select_n.27, f32[1280]{0:T(1024)S(1)} %dynamic-slice.5, f32[128]{0:T(128)S(1)} %add_rsqrt_fusion), kind=kOutput, calls=%fused_computation.3 | convolution fusion | flops 674725888 | bytes 8004100 | tf_op jit(solution)/shard_map/dot_general | solution.py:74
  19.9 16.1 %all-to-all-start = ((bf16[128,16,1280]{2,1,0:T(8,128)(2,1)}), bf16[128,16,1280]{2,1,0:T(8,128)(2,1)}, u32[]{:S(2)}, u32[]{:S(2)}) async-start(bf16[128,16,1280]{2,1,0:T(8,128)(2,1)} %bitcast.55), calls=%async_computation | async-start | bytes 10485760 | tf_op jit(solution)/shard_map/all_to_all | solution.py:129
  36.0 0.0 copy-start.2
  36.0 1.1 dynamic-slice_bitcast_fusion
  37.1 0.0 collective-permute-start
  37.1 1.3 copy-done.2
  38.5 2.8 constant_dynamic-slice_fusion
  41.2 1.8 copy_bitcast_fusion
  43.0 0.0 collective-permute-done
  43.0 130.3 %all-gather.3.cloned.1.call-done = bf16[2048,1280]{1,0:T(8,128)(2,1)} async-done(((bf16[16,1280]{1,0:T(8,128)(2,1)}), bf16[2048,1280]{1,0:T(8,128)(2,1)}) %all-gather.3.cloned.1.call-update) | async-done | bytes 5242896 | tf_op jit(solution)/shard_map/all_gather | solution.py:130
  173.3 0.0 all-to-all-done
  173.3 0.1 collective-permute-start.1
  173.3 8.8 %collective-permute-done.1 = bf16[2048,1280]{1,0:T(8,128)(2,1)S(1)} collective-permute-done((bf16[2048,1280]{1,0:T(8,128)(2,1)}, bf16[2048,1280]{1,0:T(8,128)(2,1)S(1)}, u32[]{:S(2)}, u32[]{:S(2)}) %collective-permute-start.1) | collective-permute-done | bytes 5242912 | tf_op jit(solution)/shard_map/ppermute | solution.py:17
  182.2 6.1 %fusion = f32[2048,2,384]{2,0,1:T(8,128)S(1)} fusion(bf16[1280,2,384]{2,0,1:T(8,128)(2,1)} %get-tuple-element.15, bf16[2048,1280]{1,0:T(8,128)(2,1)S(1)} %collective-permute-done.1), kind=kOutput, calls=%fused_computation.12 | convolution fusion | flops 4026531840 | bytes 13500416 | tf_op jit(solution)/shard_map/rd,dgf->rgf/dot_general | solution.py:25
  188.2 6.3 %convolution_add_fusion = f32[2048,2,384]{2,0,1:T(8,128)S(1)} fusion(f32[2048,2,384]{2,0,1:T(8,128)S(1)} %fusion, bf16[2048,1280,1]{1,0,2:T(8,128)(2,1)} %bitcast.10, bf16[1280,2,384]{2,0,1:T(8,128)(2,1)S(1)} %get-tuple-element.14), kind=kOutput, calls=%fused_computation.14 | convolution fusion | flops 4028104704 | bytes 19791872 | tf_op jit(solution)/shard_map/rd,dgf->rgf/dot_general | solution.py:23
  194.5 0.0 copy-start.4
  194.6 0.9 fusion.3
  195.5 0.2 collective-permute-start.2
  195.7 0.0 copy-done.4
  195.7 3.0 convolution_convert_fusion.1
  198.8 0.2 collective-permute-done.2
  199.0 4.3 %convolution_convert_fusion = bf16[2048,1280]{1,0:T(8,128)(2,1)S(1)} fusion(bf16[2048,384]{1,0:T(8,128)(2,1)S(1)} %collective-permute-done.2, bf16[384,1280]{1,0:T(8,128)(2,1)} %collective-permute-done), kind=kOutput, calls=%fused_computation.1 | convolution fusion | flops 2015887360 | bytes 7798784 | tf_op jit(solution)/shard_map/dot_general | solution.py:31
  203.3 3.9 %add_convert_fusion = bf16[2048,1280]{1,0:T(8,128)(2,1)} fusion(bf16[2048,1280]{1,0:T(8,128)(2,1)S(1)} %convolution_convert_fusion, bf16[2048,1280]{1,0:T(8,128)(2,1)S(1)} %convolution_convert_fusion.1), kind=kLoop, calls=%fused_computation | loop fusion | flops 10485760 | bytes 15728640 | tf_op jit(solution)/shard_map/convert_element_type | solution.py:35
  207.2 12.7 %all-to-all-start.1 = ((bf16[128,16,1280]{2,1,0:T(8,128)(2,1)}), bf16[128,16,1280]{2,1,0:T(8,128)(2,1)}, u32[]{:S(2)}, u32[]{:S(2)}) async-start(bf16[128,16,1280]{2,1,0:T(8,128)(2,1)} %bitcast.56), calls=%async_computation.1 | async-start | bytes 10485760 | tf_op jit(solution)/shard_map/all_to_all | solution.py:134
  219.9 0.2 select_reduce_fusion.2
  220.1 0.1 broadcast_compare_fusion
  220.2 2.5 select_reduce_fusion
  222.7 3.5 fusion.19
  226.2 5.6 %all-reduce.1 = bf16[128,128,8]{0,2,1:T(8,128)(2,1)S(1)} all-reduce(f32[128,128,8]{0,2,1:T(8,128)} %fusion.19), channel_id=1, replica_groups=mesh['kv'=2,'px'=4,'pz'=8,'py'=4] {'kv'}, use_global_device_ids=true, to_apply=%region_7.8 | all-reduce | flops 131072 | bytes 786432 | tf_op jit(solution)/shard_map/psum | solution.py:156
  231.8 108.1 %all-to-all-done.1 = bf16[128,16,1280]{2,1,0:T(8,128)(2,1)} async-done(((bf16[128,16,1280]{2,1,0:T(8,128)(2,1)}), bf16[128,16,1280]{2,1,0:T(8,128)(2,1)}, u32[]{:S(2)}, u32[]{:S(2)}) %all-to-all-start.1) | async-done | bytes 5242912 | tf_op jit(solution)/shard_map/all_to_all | solution.py:134
  339.9 3.6 %fusion.27 = f32[128,1280]{1,0:T(8,128)S(1)} fusion(bf16[2048,1280]{1,0:T(8,128)(2,1)} %bitcast.15, f32[128,2048]{1,0:T(8,128)S(1)} %get-tuple-element.22, f32[128,2048]{1,0:T(8,128)S(1)} %get-tuple-element.21), kind=kOutput, calls=%fused_computation.46 | convolution fusion | flops 671612928 | bytes 7995392 | tf_op jit(solution)/shard_map/dot_general | solution.py:90
  343.5 0.0 slice-start.1
  343.5 3.5 convolution_add_fusion.1
  347.0 1.3 fusion.15
  (20 shorter events, 0.0 us)
Async XLA Ops:
  6.5 0.8 copy-start
  6.5 166.8 %all-gather.3.cloned.1.call-start = ((), (), s32[]{:S(2)}) async-start(), calls=%async_computation.2 | async-start | bytes 5283840 | tf_op jit(solution)/shard_map/all_gather | solution.py:130
  19.9 16.1 %copy-start.3 = (bf16[1,384,2560]{2,1,0:T(8,128)(2,1)S(1)}, bf16[1,384,2560]{2,1,0:T(8,128)(2,1)}, u32[]{:S(2)}) copy-start(bf16[1,384,2560]{2,1,0:T(8,128)(2,1)} %param.19) | copy-start | bytes 5898244
  19.9 153.4 %all-to-all-start = ((bf16[128,16,1280]{2,1,0:T(8,128)(2,1)}), bf16[128,16,1280]{2,1,0:T(8,128)(2,1)}, u32[]{:S(2)}, u32[]{:S(2)}) async-start(bf16[128,16,1280]{2,1,0:T(8,128)(2,1)} %bitcast.55), calls=%async_computation | async-start | bytes 10485760 | tf_op jit(solution)/shard_map/all_to_all | solution.py:129
  36.0 2.5 copy-start.2
  37.1 5.9 %collective-permute-start = (bf16[384,1280]{1,0:T(8,128)(2,1)S(1)}, bf16[384,1280]{1,0:T(8,128)(2,1)}, u32[]{:S(2)}, u32[]{:S(2)}) collective-permute-start(bf16[384,1280]{1,0:T(8,128)(2,1)S(1)} %get-tuple-element.27), channel_id=1, source_target_pairs={{0,128},{128,0},{1,129},{129,1},{2,130},{130,2},{3,131},{131,3},{4... | collective-permute-start | bytes 2949128 | tf_op jit(solution)/shard_map/ppermute | solution.py:17
  173.3 8.9 %collective-permute-start.1 = (bf16[2048,1280]{1,0:T(8,128)(2,1)}, bf16[2048,1280]{1,0:T(8,128)(2,1)S(1)}, u32[]{:S(2)}, u32[]{:S(2)}) collective-permute-start(bf16[2048,1280]{1,0:T(8,128)(2,1)} %bitcast.9), channel_id=1, source_target_pairs={{0,128},{128,0},{1,129},{129,1},{2,130},{130,2},{3,131},{131,3},{4... | collective-permute-start | bytes 15728648 | tf_op jit(solution)/shard_map/ppermute | solution.py:17
  194.5 1.2 copy-start.4
  195.5 3.5 collective-permute-start.2
  207.2 12.7 %copy-start.6 = (s32[256]{0:T(256)S(1)}, s32[256]{0:T(256)}, u32[]{:S(2)}) copy-start(s32[256]{0:T(256)} %param.16) | copy-start | bytes 3076
  207.2 12.7 %copy-start.8 = (s32[128]{0:T(128)S(1)}, s32[128]{0:T(128)}, u32[]{:S(2)}) copy-start(s32[128]{0:T(128)} %param.15) | copy-start | bytes 1540
  207.2 12.9 %copy-start.7 = (s32[128]{0:T(128)S(1)}, s32[128]{0:T(128)}, u32[]{:S(2)}) copy-start(s32[128]{0:T(128)} %param.17) | copy-start | bytes 1540
  207.2 13.0 %copy-start.5 = (f32[128,6]{0,1:T(8,128)S(1)}, f32[128,6]{0,1:T(8,128)}, u32[]{:S(2)}) copy-start(f32[128,6]{0,1:T(8,128)} %param.14) | copy-start | bytes 9220
  207.2 132.7 %all-to-all-start.1 = ((bf16[128,16,1280]{2,1,0:T(8,128)(2,1)}), bf16[128,16,1280]{2,1,0:T(8,128)(2,1)}, u32[]{:S(2)}, u32[]{:S(2)}) async-start(bf16[128,16,1280]{2,1,0:T(8,128)(2,1)} %bitcast.56), calls=%async_computation.1 | async-start | bytes 10485760 | tf_op jit(solution)/shard_map/all_to_all | solution.py:134
  339.9 7.1 %slice-start = ((s8[5242880]{0:T(1024)(128)(4,1)}), s8[4194304]{0:T(1024)(128)(4,1)S(1)}, s32[]{:S(2)}) async-start(s8[5242880]{0:T(1024)(128)(4,1)} %bitcast.59), calls=%async_computation.3 | async-start | bytes 8388608
  339.9 8.4 %copy-start.1 = (bf16[1,2560,8]{1,2,0:T(8,128)(2,1)S(1)}, bf16[1,2560,8]{1,2,0:T(8,128)(2,1)}, u32[]{:S(2)}) copy-start(bf16[1,2560,8]{1,2,0:T(8,128)(2,1)} %param.20) | copy-start | bytes 122884
  343.5 3.5 slice-start.1
Sparse Core Ops, SparseCore 0:
  10.8 162.3 all-gather.2

commit v12 on v11

--- a/solution.py
+++ b/solution.py
@@ -20,9 +20,13 @@
 def expert_half(own_rows, weights):
     own_weight, other_weight, own_units_down, other_units_down = weights
     other_rows = swap_kv(own_rows)
-    gate_up = jnp.einsum(
+    own_partial = jnp.einsum(
         "rd,dgf->rgf", own_rows, own_weight, preferred_element_type=jnp.float32
-    ) + jnp.einsum("rd,dgf->rgf", other_rows, other_weight, preferred_element_type=jnp.float32)
+    )
+    own_partial, other_rows = lax.optimization_barrier((own_partial, other_rows))
+    gate_up = own_partial + jnp.einsum(
+        "rd,dgf->rgf", other_rows, other_weight, preferred_element_type=jnp.float32
+    )
     own_hidden = (jax.nn.silu(gate_up[:, 0]) * gate_up[:, 1]).astype(jnp.bfloat16)
     other_hidden = swap_kv(own_hidden)
     own_quarter = jnp.dot(own_hidden, own_units_down, preferred_element_type=jnp.float32).astype(

time: 356 us -> 349 us (0.980)
  waiting for transfers between devices: 247 us -> 242 us
    ppermute x3, waiting for transfers between devices: 9.01 us -> 2.63 us  [swap_kv(): return lax.ppermute(values, 'kv', perm=[(0, 1), (1, 0)])]
  transfers between devices with their start and end apart: 6 -> 6, of which waited for: 4 -> 5; matrix products, arithmetic and copies ran while one was open for 7% -> 9% of each run, Pallas kernels for 0% -> 0%
where the time goes in v12:
time: 349 us
  waiting for transfers between devices  242 us (69%)
  matrix products  34.2 us (10%)
  starting transfers between devices  27.8 us (8%)
  other arithmetic  14.9 us (4%)
  between operations  13.7 us (4%)
  local copies, waits for them, and re-layouts  9.83 us (3%)
  blocking collectives  5.59 us (2%)
    all_gather x1, waiting for transfers between devices, on_device(): packed_all = lax.all_gather(packed, PG_AXES, axis=0, tiled=False)  129 us
    all_to_all x1, waiting for transfers between devices, on_device(): lax.all_to_all(half_out.reshape(pg_size, slot_cap, half_width), PG_AXES,...  108 us
    all_to_all x1, starting transfers between devices, on_device(): lax.all_to_all(outbox, PG_AXES, split_axis=0, concat_axis=0, tiled=True)  16.1 us
    all_to_all x1, starting transfers between devices, on_device(): lax.all_to_all(half_out.reshape(pg_size, slot_cap, half_width), PG_AXES,...  11.5 us
  transfers between devices with their start and end apart: 6, of which 5 were waited for; matrix products, arithmetic and copies ran while one was open for 9% of the time, Pallas kernels for 0%

profile of v12, /device:TPU:2, one launch (start us, length us, event | category | flops | bytes accessed | tf_op | source)
XLA Modules:
  0.0 348.5 jit_solution(6375592046751839141)
XLA Ops:
  6.5 0.8 copy-done
  7.3 1.3 pad_maximum_fusion
  8.7 0.0 all-gather.3.cloned.1.call-update
  8.7 1.2 convert_element_type.73
  9.9 0.0 copy-start.3
  9.9 1.8 multiply_reduce_fusion
  11.7 0.8 copy.37
  12.5 0.1 eq.98
  12.6 0.4 fusion.23
  13.0 0.1 convert_element_type.68
  13.2 0.1 copy.38
  13.2 0.7 broadcast_add_fusion
  13.9 0.8 dynamic-slice.5
  14.7 1.7 convert_reduce_fusion
  16.4 4.0 %convolution_convert_fusion.2 = bf16[2048,1280]{1,0:T(8,128)(2,1)} fusion(f32[2048,128]{1,0:T(8,128)S(1)} %get-tuple-element.34, f32[2048,128]{1,0:T(8,128)S(1)} %get-tuple-element.33, f32[128,2560]{1,0:T(8,128)S(1)} %convert_element_type.73, s32[]{:T(128)S(6)} %select_n.27, f32[1280]{0:T(1024)S(1)} %dynamic-slice.5, f32[128]{0:T(128)S(1)} %add_rsqrt_fusion), kind=kOutput, calls=%fused_computation.3 | convolution fusion | flops 674725888 | bytes 8004100 | tf_op jit(solution)/shard_map/dot_general | solution.py:78
  20.4 16.1 %all-to-all-start = ((bf16[128,16,1280]{2,1,0:T(8,128)(2,1)}), bf16[128,16,1280]{2,1,0:T(8,128)(2,1)}, u32[]{:S(2)}, u32[]{:S(2)}) async-start(bf16[128,16,1280]{2,1,0:T(8,128)(2,1)} %bitcast.55), calls=%async_computation | async-start | bytes 10485760 | tf_op jit(solution)/shard_map/all_to_all | solution.py:133
  36.5 0.0 copy-start.2
  36.5 1.1 dynamic-slice_bitcast_fusion
  37.6 0.0 collective-permute-start
  37.6 1.4 copy-done.2
  38.9 2.8 constant_dynamic-slice_fusion
  41.7 1.8 copy_bitcast_fusion
  43.5 0.0 collective-permute-done
  43.5 129.4 %all-gather.3.cloned.1.call-done = bf16[2048,1280]{1,0:T(8,128)(2,1)} async-done(((bf16[16,1280]{1,0:T(8,128)(2,1)}), bf16[2048,1280]{1,0:T(8,128)(2,1)}) %all-gather.3.cloned.1.call-update) | async-done | bytes 5242896 | tf_op jit(solution)/shard_map/all_gather | solution.py:134
  173.0 2.2 all-to-all-done
  175.2 0.0 collective-permute-start.1
  175.2 6.4 %fusion.35 = f32[2048,2,384]{2,0,1:T(8,128)S(1)} fusion(bf16[2048,1280,1]{1,0,2:T(8,128)(2,1)} %bitcast.10, bf16[1280,2,384]{2,0,1:T(8,128)(2,1)S(1)} %get-tuple-element.16), kind=kOutput, calls=%fused_computation.63 | convolution fusion | flops 4026531840 | bytes 13500416 | tf_op jit(solution)/shard_map/rd,dgf->rgf/dot_general | solution.py:23
  181.6 2.5 collective-permute-done.1
  184.1 4.4 %fusion = f32[2048,2,384]{2,0,1:T(8,128)S(1)} fusion(bf16[1280,2,384]{2,0,1:T(8,128)(2,1)S(1)} %copy-done.6, bf16[2048,1280]{1,0:T(8,128)(2,1)S(1)} %collective-permute-done.1), kind=kOutput, calls=%fused_computation.12 | convolution fusion | flops 4026531840 | bytes 13500416 | tf_op jit(solution)/shard_map/rd,dgf->rgf/dot_general | solution.py:27
  188.5 0.6 add.62
  189.1 0.9 fusion.3
  190.0 0.2 collective-permute-start.2
  190.2 0.1 copy-done.7
  190.3 3.0 convolution_convert_fusion.1
  193.3 0.1 collective-permute-done.2
  193.5 4.3 %convolution_convert_fusion = bf16[2048,1280]{1,0:T(8,128)(2,1)S(1)} fusion(bf16[2048,384]{1,0:T(8,128)(2,1)S(1)} %collective-permute-done.2, bf16[384,1280]{1,0:T(8,128)(2,1)} %collective-permute-done), kind=kOutput, calls=%fused_computation.1 | convolution fusion | flops 2015887360 | bytes 7798784 | tf_op jit(solution)/shard_map/dot_general | solution.py:35
  197.7 3.9 %add_convert_fusion = bf16[2048,1280]{1,0:T(8,128)(2,1)} fusion(bf16[2048,1280]{1,0:T(8,128)(2,1)S(1)} %convolution_convert_fusion, bf16[2048,1280]{1,0:T(8,128)(2,1)S(1)} %convolution_convert_fusion.1), kind=kLoop, calls=%fused_computation | loop fusion | flops 10485760 | bytes 15728640 | tf_op jit(solution)/shard_map/convert_element_type | solution.py:39
  201.7 11.5 %all-to-all-start.1 = ((bf16[128,16,1280]{2,1,0:T(8,128)(2,1)}), bf16[128,16,1280]{2,1,0:T(8,128)(2,1)}, u32[]{:S(2)}, u32[]{:S(2)}) async-start(bf16[128,16,1280]{2,1,0:T(8,128)(2,1)} %bitcast.56), calls=%async_computation.1 | async-start | bytes 10485760 | tf_op jit(solution)/shard_map/all_to_all | solution.py:138
  213.2 0.2 select_reduce_fusion.2
  213.4 0.1 broadcast_compare_fusion
  213.5 2.5 select_reduce_fusion
  216.0 3.5 fusion.19
  219.5 5.6 %all-reduce.1 = bf16[128,128,8]{0,2,1:T(8,128)(2,1)S(1)} all-reduce(f32[128,128,8]{0,2,1:T(8,128)} %fusion.19), channel_id=1, replica_groups=mesh['kv'=2,'px'=4,'pz'=8,'py'=4] {'kv'}, use_global_device_ids=true, to_apply=%region_7.8 | all-reduce | flops 131072 | bytes 786432 | tf_op jit(solution)/shard_map/psum | solution.py:160
  225.1 108.1 %all-to-all-done.1 = bf16[128,16,1280]{2,1,0:T(8,128)(2,1)} async-done(((bf16[128,16,1280]{2,1,0:T(8,128)(2,1)}), bf16[128,16,1280]{2,1,0:T(8,128)(2,1)}, u32[]{:S(2)}, u32[]{:S(2)}) %all-to-all-start.1) | async-done | bytes 5242912 | tf_op jit(solution)/shard_map/all_to_all | solution.py:138
  333.2 3.6 %fusion.27 = f32[128,1280]{1,0:T(8,128)S(1)} fusion(bf16[2048,1280]{1,0:T(8,128)(2,1)} %bitcast.15, f32[128,2048]{1,0:T(8,128)S(1)} %get-tuple-element.26, f32[128,2048]{1,0:T(8,128)S(1)} %get-tuple-element.25), kind=kOutput, calls=%fused_computation.45 | convolution fusion | flops 671612928 | bytes 7995392 | tf_op jit(solution)/shard_map/dot_general | solution.py:94
  336.8 0.0 slice-start.1
  336.8 3.5 %convolution_add_fusion = f32[128,1280]{1,0:T(8,128)S(1)} fusion(f32[128,1280]{1,0:T(8,128)S(1)} %fusion.27, bf16[2048,1280]{1,0:T(8,128)(2,1)} %bitcast.15, f32[128,2048]{1,0:T(8,128)S(1)} %get-tuple-element.26, f32[128,2048]{1,0:T(8,128)S(1)} %get-tuple-element.25), kind=kOutput, calls=%fused_computation.23 | convolution fusion | flops 672563200 | bytes 8650752 | tf_op jit(solution)/shard_map/dot_general | solution.py:94
  340.4 1.3 fusion.15
  (27 shorter events, 0.1 us)
Async XLA Ops:
  6.5 0.8 copy-start
  6.5 166.4 %all-gather.3.cloned.1.call-start = ((), (), s32[]{:S(2)}) async-start(), calls=%async_computation.2 | async-start | bytes 5283840 | tf_op jit(solution)/shard_map/all_gather | solution.py:134
  9.9 10.5 %copy-start.3 = (f32[128,2560]{1,0:T(8,128)}, f32[128,2560]{1,0:T(8,128)S(1)}, u32[]{:S(2)}) copy-start(f32[128,2560]{1,0:T(8,128)S(1)} %convert_element_type.73) | copy-start | bytes 3932164
  20.4 16.1 %copy-start.5 = (bf16[1,384,2560]{2,1,0:T(8,128)(2,1)S(1)}, bf16[1,384,2560]{2,1,0:T(8,128)(2,1)}, u32[]{:S(2)}) copy-start(bf16[1,384,2560]{2,1,0:T(8,128)(2,1)} %param.19) | copy-start | bytes 5898244
  20.4 154.8 %all-to-all-start = ((bf16[128,16,1280]{2,1,0:T(8,128)(2,1)}), bf16[128,16,1280]{2,1,0:T(8,128)(2,1)}, u32[]{:S(2)}, u32[]{:S(2)}) async-start(bf16[128,16,1280]{2,1,0:T(8,128)(2,1)} %bitcast.55), calls=%async_computation | async-start | bytes 10485760 | tf_op jit(solution)/shard_map/all_to_all | solution.py:133
  36.5 2.5 copy-start.2
  37.6 5.9 %collective-permute-start = (bf16[384,1280]{1,0:T(8,128)(2,1)S(1)}, bf16[384,1280]{1,0:T(8,128)(2,1)}, u32[]{:S(2)}, u32[]{:S(2)}) collective-permute-start(bf16[384,1280]{1,0:T(8,128)(2,1)S(1)} %get-tuple-element.31), channel_id=1, source_target_pairs={{0,128},{128,0},{1,129},{129,1},{2,130},{130,2},{3,131},{131,3},{4... | collective-permute-start | bytes 2949128 | tf_op jit(solution)/shard_map/ppermute | solution.py:17
  175.2 8.9 %collective-permute-start.1 = (bf16[2048,1280]{1,0:T(8,128)(2,1)}, bf16[2048,1280]{1,0:T(8,128)(2,1)S(1)}, u32[]{:S(2)}, u32[]{:S(2)}) collective-permute-start(bf16[2048,1280]{1,0:T(8,128)(2,1)} %bitcast.9), channel_id=1, source_target_pairs={{0,128},{128,0},{1,129},{129,1},{2,130},{130,2},{3,131},{131,3},{4... | collective-permute-start | bytes 15728648 | tf_op jit(solution)/shard_map/ppermute | solution.py:17
  175.2 8.9 %copy-start.6 = (bf16[1280,2,384]{2,0,1:T(8,128)(2,1)S(1)}, bf16[1280,2,384]{2,0,1:T(8,128)(2,1)}, u32[]{:S(2)}) copy-start(bf16[1280,2,384]{2,0,1:T(8,128)(2,1)} %get-tuple-element.19) | copy-start | bytes 5898244
  189.1 1.2 copy-start.7
  190.0 3.5 %collective-permute-start.2 = (bf16[2048,384]{1,0:T(8,128)(2,1)S(1)}, bf16[2048,384]{1,0:T(8,128)(2,1)S(1)}, u32[]{:S(2)}, u32[]{:S(2)}) collective-permute-start(bf16[2048,384]{1,0:T(8,128)(2,1)S(1)} %fusion.3), channel_id=1, source_target_pairs={{0,128},{128,0},{1,129},{129,1},{2,130},{130,2},{3,131},{131,3},{4... | collective-permute-start | bytes 4718600 | tf_op jit(solution)/shard_map/ppermute | solution.py:17
  201.7 11.5 %copy-start.9 = (s32[256]{0:T(256)S(1)}, s32[256]{0:T(256)}, u32[]{:S(2)}) copy-start(s32[256]{0:T(256)} %param.16) | copy-start | bytes 3076
  201.7 11.5 %copy-start.11 = (s32[128]{0:T(128)S(1)}, s32[128]{0:T(128)}, u32[]{:S(2)}) copy-start(s32[128]{0:T(128)} %param.15) | copy-start | bytes 1540
  201.7 11.7 %copy-start.10 = (s32[128]{0:T(128)S(1)}, s32[128]{0:T(128)}, u32[]{:S(2)}) copy-start(s32[128]{0:T(128)} %param.17) | copy-start | bytes 1540
  201.7 11.8 %copy-start.8 = (f32[128,6]{0,1:T(8,128)S(1)}, f32[128,6]{0,1:T(8,128)}, u32[]{:S(2)}) copy-start(f32[128,6]{0,1:T(8,128)} %param.14) | copy-start | bytes 9220
  201.7 14.3 %copy-start.4 = (f32[128,2560]{1,0:T(8,128)S(1)}, f32[128,2560]{1,0:T(8,128)}, u32[]{:S(2)}) copy-start(f32[128,2560]{1,0:T(8,128)} %copy-done.3) | copy-start | bytes 3932164
  201.7 131.5 %all-to-all-start.1 = ((bf16[128,16,1280]{2,1,0:T(8,128)(2,1)}), bf16[128,16,1280]{2,1,0:T(8,128)(2,1)}, u32[]{:S(2)}, u32[]{:S(2)}) async-start(bf16[128,16,1280]{2,1,0:T(8,128)(2,1)} %bitcast.56), calls=%async_computation.1 | async-start | bytes 10485760 | tf_op jit(solution)/shard_map/all_to_all | solution.py:138
  333.2 7.1 %slice-start = ((s8[5242880]{0:T(1024)(128)(4,1)}), s8[4194304]{0:T(1024)(128)(4,1)S(1)}, s32[]{:S(2)}) async-start(s8[5242880]{0:T(1024)(128)(4,1)} %bitcast.59), calls=%async_computation.3 | async-start | bytes 8388608
  333.2 8.4 %copy-start.1 = (bf16[1,2560,8]{1,2,0:T(8,128)(2,1)S(1)}, bf16[1,2560,8]{1,2,0:T(8,128)(2,1)}, u32[]{:S(2)}) copy-start(bf16[1,2560,8]{1,2,0:T(8,128)(2,1)} %param.20) | copy-start | bytes 122884
  336.8 3.5 %slice-start.1 = ((s8[5242880]{0:T(1024)(128)(4,1)}), s8[1048576]{0:T(1024)(128)(4,1)S(1)}, s32[]{:S(2)}) async-start(s8[5242880]{0:T(1024)(128)(4,1)} %bitcast.59), calls=%async_computation.4 | async-start | bytes 2097152
Sparse Core Ops, SparseCore 0:
  10.8 162.0 all-gather.2

commit v13 on v12

--- a/solution.py
+++ b/solution.py
@@ -69,16 +69,17 @@
 
 
 def place_rows(slot_table, slot_total, normalized_input):
-    slot_ids = jnp.arange(slot_total, dtype=jnp.int32)
-    hits = jnp.zeros((slot_total, slot_table[0].shape[0]), jnp.float32)
+    token_count, width = normalized_input.shape
+    token_ids = jnp.broadcast_to(
+        jnp.arange(token_count, dtype=jnp.int32)[:, None], slot_table[0].shape
+    ).reshape(-1)
+    slot_token = jnp.full((slot_total,), token_count, jnp.int32)
     for table in slot_table:
-        hits = hits + jnp.sum(
-            (table[None, :, :] == slot_ids[:, None, None]).astype(jnp.float32), axis=2
-        )
-    placed = jnp.dot(
-        hits.astype(jnp.bfloat16), normalized_input, preferred_element_type=jnp.float32
+        slot_token = slot_token.at[table.reshape(-1)].set(token_ids)
+    padded = jnp.concatenate(
+        [normalized_input, jnp.zeros((1, width), normalized_input.dtype)], axis=0
     )
-    return placed.astype(jnp.bfloat16)
+    return jnp.take(padded, slot_token, axis=0)
 
 
 def collect_rows(slot_table, slot_total, weights, gathered):

time: 349 us -> 364 us (1.043)
  local copies, waits for them, and re-layouts: 9.83 us -> 26.7 us
  matrix products: 34.2 us -> 29.4 us
  waiting for transfers between devices: 242 us -> 246 us
    all_to_all x1, waiting for transfers between devices: 2.23 us -> 14.8 us  [on_device(): lax.all_to_all(outbox, PG_AXES, split_axis=0, concat_axis=0, tiled=True)]
    all_gather x1, waiting for transfers between devices: 129 us -> 119 us  [on_device(): packed_all = lax.all_gather(packed, PG_AXES, axis=0, tiled=False)]
    gather x0 -> x1, local copies, waits for them, and re-layouts: none -> 9.99 us  [place_rows(): return jnp.take(padded, slot_token, axis=0)]
    scatter x0 -> x2, local copies, waits for them, and re-layouts: none -> 6.78 us  [place_rows(): slot_token = slot_token.at[table.reshape(-1)].set(token_ids)]
    select_n x0 -> x3, other arithmetic: none -> 5.44 us  [the longest x1 5.41 us: place_rows(): return jnp.take(padded, slot_token, axis=0)]
    dot_general x1 -> x0, matrix products: 3.96 us -> none  [place_rows(): jnp.dot(hits.astype(jnp.bfloat16), normalized_input, preferred_element_ty...]
  transfers between devices with their start and end apart: 6 -> 6, of which waited for: 5 -> 5; matrix products, arithmetic and copies ran while one was open for 9% -> 13% of each run, Pallas kernels for 0% -> 0%
where the time goes in v13:
time: 364 us
  waiting for transfers between devices  246 us (68%)
  matrix products  29.4 us (8%)
  local copies, waits for them, and re-layouts  26.7 us (7%)
  starting transfers between devices  24.6 us (7%)
  other arithmetic  18.3 us (5%)
  between operations  13.8 us (4%)
  blocking collectives  4.83 us (1%)
    all_gather x1, waiting for transfers between devices, on_device(): packed_all = lax.all_gather(packed, PG_AXES, axis=0, tiled=False)  119 us
    all_to_all x1, waiting for transfers between devices, on_device(): lax.all_to_all(half_out.reshape(pg_size, slot_cap, half_width), PG_AXES,...  110 us
    all_to_all x1, starting transfers between devices, on_device(): lax.all_to_all(outbox, PG_AXES, split_axis=0, concat_axis=0, tiled=True)  16.1 us
    all_to_all x1, waiting for transfers between devices, on_device(): lax.all_to_all(outbox, PG_AXES, split_axis=0, concat_axis=0, tiled=True)  14.8 us
    gather x1, local copies, waits for them, and re-layouts, place_rows(): return jnp.take(padded, slot_token, axis=0)  9.99 us
    all_to_all x1, starting transfers between devices, on_device(): lax.all_to_all(half_out.reshape(pg_size, slot_cap, half_width), PG_AXES,...  8.28 us
  transfers between devices with their start and end apart: 6, of which 5 were waited for; matrix products, arithmetic and copies ran while one was open for 13% of the time, Pallas kernels for 0%

profile of v13, /device:TPU:2, one launch (start us, length us, event | category | flops | bytes accessed | tf_op | source)
XLA Modules:
  0.0 363.5 jit_solution(547992450567902647)
XLA Ops:
  6.5 0.8 copy-done
  7.3 1.3 pad_maximum_fusion
  8.7 1.2 convert_element_type.58
  9.9 1.3 multiply_reduce_fusion
  11.2 0.8 copy.33
  12.0 0.1 eq.72
  12.2 0.4 fusion.23
  12.6 0.1 convert_element_type.56
  12.8 0.7 broadcast_add_fusion
  13.5 0.1 copy.35
  13.6 0.1 reshape.153
  13.8 0.1 reshape.181
  13.9 0.1 copy.36
  14.0 0.1 reshape.155
  14.2 3.4 scatter_custom_fusion
  17.6 3.4 scatter_fusion
  21.1 0.1 broadcast_in_dim.88
  21.2 0.1 fusion.25
  21.4 10.0 %gather_fusion = bf16[2048,1280]{1,0:T(8,128)(2,1)} fusion(bf16[129,1280]{1,0:T(8,128)(2,1)S(1)} %concatenate.6, s32[2048]{0:T(1024)S(1)} %fusion.32), kind=kCustom, calls=%fused_computation | custom fusion | bytes 10493952 | tf_op jit(solution)/shard_map/jit(_take)/gather | solution.py:82
  31.4 5.4 %broadcast_select_fusion = bf16[128,16,1280]{2,1,0:T(8,128)(2,1)} fusion(bf16[128,16,1280]{2,1,0:T(8,128)(2,1)} %bitcast.56, pred[128,16]{1,0:T(8,128)(4,1)S(1)} %broadcast_in_dim.88), kind=kLoop, calls=%fused_computation.12 | loop fusion | flops 2621440 | bytes 10487808 | tf_op jit(solution)/shard_map/jit(_take)/select_n | solution.py:82
  36.8 16.1 %all-to-all-start = ((bf16[128,16,1280]{2,1,0:T(8,128)(2,1)}), bf16[128,16,1280]{2,1,0:T(8,128)(2,1)}, u32[]{:S(2)}, u32[]{:S(2)}) async-start(bf16[128,16,1280]{2,1,0:T(8,128)(2,1)} %broadcast_select_fusion), calls=%async_computation | async-start | bytes 10485760 | tf_op jit(solution)/shard_map/all_to_all | solution.py:134
  52.9 1.1 dynamic-slice_bitcast_fusion
  54.0 1.3 copy-done.2
  55.3 2.8 constant_dynamic-slice_fusion
  58.1 1.8 copy_bitcast_fusion
  59.9 118.6 %all-gather.3.cloned.1.call-done = bf16[2048,1280]{1,0:T(8,128)(2,1)} async-done(((bf16[16,1280]{1,0:T(8,128)(2,1)}), bf16[2048,1280]{1,0:T(8,128)(2,1)}) %all-gather.3.cloned.1.call-update) | async-done | bytes 5242896 | tf_op jit(solution)/shard_map/all_gather | solution.py:135
  178.4 14.8 %all-to-all-done = bf16[128,16,1280]{2,1,0:T(8,128)(2,1)} async-done(((bf16[128,16,1280]{2,1,0:T(8,128)(2,1)}), bf16[128,16,1280]{2,1,0:T(8,128)(2,1)}, u32[]{:S(2)}, u32[]{:S(2)}) %all-to-all-start) | async-done | bytes 5242912 | tf_op jit(solution)/shard_map/all_to_all | solution.py:134
  193.3 6.4 %fusion.38 = f32[2048,2,384]{2,0,1:T(8,128)S(1)} fusion(bf16[2048,1280,1]{1,0,2:T(8,128)(2,1)} %bitcast.10, bf16[1280,2,384]{2,0,1:T(8,128)(2,1)S(1)} %get-tuple-element.16), kind=kOutput, calls=%fused_computation.70 | convolution fusion | flops 4026531840 | bytes 13500416 | tf_op jit(solution)/shard_map/rd,dgf->rgf/dot_general | solution.py:23
  199.6 2.5 collective-permute-done.1
  202.1 4.4 %fusion = f32[2048,2,384]{2,0,1:T(8,128)S(1)} fusion(bf16[1280,2,384]{2,0,1:T(8,128)(2,1)S(1)} %copy-done.4, bf16[2048,1280]{1,0:T(8,128)(2,1)S(1)} %collective-permute-done.1), kind=kOutput, calls=%fused_computation.10 | convolution fusion | flops 4026531840 | bytes 13500416 | tf_op jit(solution)/shard_map/rd,dgf->rgf/dot_general | solution.py:27
  206.5 0.6 add.92
  207.2 0.9 fusion.3
  208.0 0.2 collective-permute-start.2
  208.2 0.1 copy-done.5
  208.3 3.0 convolution_convert_fusion.1
  211.4 0.1 collective-permute-done.2
  211.5 4.3 %convolution_convert_fusion = bf16[2048,1280]{1,0:T(8,128)(2,1)S(1)} fusion(bf16[2048,384]{1,0:T(8,128)(2,1)S(1)} %collective-permute-done.2, bf16[384,1280]{1,0:T(8,128)(2,1)} %collective-permute-done), kind=kOutput, calls=%fused_computation.4 | convolution fusion | flops 2015887360 | bytes 7798784 | tf_op jit(solution)/shard_map/dot_general | solution.py:35
  215.8 4.0 %add_convert_fusion = bf16[2048,1280]{1,0:T(8,128)(2,1)} fusion(bf16[2048,1280]{1,0:T(8,128)(2,1)S(1)} %convolution_convert_fusion, bf16[2048,1280]{1,0:T(8,128)(2,1)S(1)} %convolution_convert_fusion.1), kind=kLoop, calls=%fused_computation.3 | loop fusion | flops 10485760 | bytes 15728640 | tf_op jit(solution)/shard_map/convert_element_type | solution.py:39
  219.8 8.3 %all-to-all-start.1 = ((bf16[128,16,1280]{2,1,0:T(8,128)(2,1)}), bf16[128,16,1280]{2,1,0:T(8,128)(2,1)}, u32[]{:S(2)}, u32[]{:S(2)}) async-start(bf16[128,16,1280]{2,1,0:T(8,128)(2,1)} %bitcast.57), calls=%async_computation.1 | async-start | bytes 10485760 | tf_op jit(solution)/shard_map/all_to_all | solution.py:139
  228.1 0.2 select_reduce_fusion.2
  228.3 0.1 broadcast_compare_fusion
  228.4 2.5 select_reduce_fusion
  230.9 2.6 fusion.19
  233.4 4.8 %all-reduce.2 = bf16[128,128,8]{0,2,1:T(8,128)(2,1)S(1)} all-reduce(f32[128,128,8]{0,2,1:T(8,128)S(1)} %fusion.19), channel_id=1, replica_groups=mesh['kv'=2,'px'=4,'pz'=8,'py'=4] {'kv'}, use_global_device_ids=true, to_apply=%region_7.8 | all-reduce | flops 131072 | bytes 786432 | tf_op jit(solution)/shard_map/psum | solution.py:161
  238.3 110.0 %all-to-all-done.1 = bf16[128,16,1280]{2,1,0:T(8,128)(2,1)} async-done(((bf16[128,16,1280]{2,1,0:T(8,128)(2,1)}), bf16[128,16,1280]{2,1,0:T(8,128)(2,1)}, u32[]{:S(2)}, u32[]{:S(2)}) %all-to-all-start.1) | async-done | bytes 5242912 | tf_op jit(solution)/shard_map/all_to_all | solution.py:139
  348.3 3.6 fusion.27
  351.8 3.5 convolution_add_fusion
  355.4 1.3 fusion.15
  (40 shorter events, 0.3 us)
Async XLA Ops:
  6.5 0.8 copy-start
  6.5 171.9 %all-gather.3.cloned.1.call-start = ((), (), s32[]{:S(2)}) async-start(), calls=%async_computation.2 | async-start | bytes 5283840 | tf_op jit(solution)/shard_map/all_gather | solution.py:135
  9.9 11.1 %copy-start.6 = (f32[2560]{0:T(1024)S(1)}, f32[2560]{0:T(1024)}, u32[]{:S(2)}) copy-start(f32[2560]{0:T(1024)} %param.12) | copy-start | bytes 30724
  36.8 16.1 %copy-start.3 = (bf16[1,384,2560]{2,1,0:T(8,128)(2,1)S(1)}, bf16[1,384,2560]{2,1,0:T(8,128)(2,1)}, u32[]{:S(2)}) copy-start(bf16[1,384,2560]{2,1,0:T(8,128)(2,1)} %param.19) | copy-start | bytes 5898244
  36.8 156.5 %all-to-all-start = ((bf16[128,16,1280]{2,1,0:T(8,128)(2,1)}), bf16[128,16,1280]{2,1,0:T(8,128)(2,1)}, u32[]{:S(2)}, u32[]{:S(2)}) async-start(bf16[128,16,1280]{2,1,0:T(8,128)(2,1)} %broadcast_select_fusion), calls=%async_computation | async-start | bytes 10485760 | tf_op jit(solution)/shard_map/all_to_all | solution.py:134
  52.8 2.5 copy-start.2
  54.0 5.9 %collective-permute-start = (bf16[384,1280]{1,0:T(8,128)(2,1)S(1)}, bf16[384,1280]{1,0:T(8,128)(2,1)}, u32[]{:S(2)}, u32[]{:S(2)}) collective-permute-start(bf16[384,1280]{1,0:T(8,128)(2,1)S(1)} %get-tuple-element.31), channel_id=1, source_target_pairs={{0,128},{128,0},{1,129},{129,1},{2,130},{130,2},{3,131},{131,3},{4... | collective-permute-start | bytes 2949128 | tf_op jit(solution)/shard_map/ppermute | solution.py:17
  193.2 8.9 %collective-permute-start.1 = (bf16[2048,1280]{1,0:T(8,128)(2,1)}, bf16[2048,1280]{1,0:T(8,128)(2,1)S(1)}, u32[]{:S(2)}, u32[]{:S(2)}) collective-permute-start(bf16[2048,1280]{1,0:T(8,128)(2,1)} %bitcast.9), channel_id=1, source_target_pairs={{0,128},{128,0},{1,129},{129,1},{2,130},{130,2},{3,131},{131,3},{4... | collective-permute-start | bytes 15728648 | tf_op jit(solution)/shard_map/ppermute | solution.py:17
  193.3 8.9 %copy-start.4 = (bf16[1280,2,384]{2,0,1:T(8,128)(2,1)S(1)}, bf16[1280,2,384]{2,0,1:T(8,128)(2,1)}, u32[]{:S(2)}) copy-start(bf16[1280,2,384]{2,0,1:T(8,128)(2,1)} %get-tuple-element.19) | copy-start | bytes 5898244
  207.1 1.2 copy-start.5
  208.0 3.5 collective-permute-start.2
  219.8 8.3 %copy-start.8 = (s32[256]{0:T(256)S(1)}, s32[256]{0:T(256)}, u32[]{:S(2)}) copy-start(s32[256]{0:T(256)} %param.16) | copy-start | bytes 3076
  219.8 8.3 %copy-start.10 = (s32[128]{0:T(128)S(1)}, s32[128]{0:T(128)}, u32[]{:S(2)}) copy-start(s32[128]{0:T(128)} %param.15) | copy-start | bytes 1540
  219.8 8.5 %copy-start.9 = (s32[128]{0:T(128)S(1)}, s32[128]{0:T(128)}, u32[]{:S(2)}) copy-start(s32[128]{0:T(128)} %param.17) | copy-start | bytes 1540
  219.8 8.6 %copy-start.7 = (f32[128,6]{0,1:T(8,128)S(1)}, f32[128,6]{0,1:T(8,128)}, u32[]{:S(2)}) copy-start(f32[128,6]{0,1:T(8,128)} %param.14) | copy-start | bytes 9220
  219.8 128.5 %all-to-all-start.1 = ((bf16[128,16,1280]{2,1,0:T(8,128)(2,1)}), bf16[128,16,1280]{2,1,0:T(8,128)(2,1)}, u32[]{:S(2)}, u32[]{:S(2)}) async-start(bf16[128,16,1280]{2,1,0:T(8,128)(2,1)} %bitcast.57), calls=%async_computation.1 | async-start | bytes 10485760 | tf_op jit(solution)/shard_map/all_to_all | solution.py:139
  348.3 7.1 %slice-start = ((s8[5242880]{0:T(1024)(128)(4,1)}), s8[4194304]{0:T(1024)(128)(4,1)S(1)}, s32[]{:S(2)}) async-start(s8[5242880]{0:T(1024)(128)(4,1)} %bitcast.60), calls=%async_computation.3 | async-start | bytes 8388608
  348.3 8.4 %copy-start.1 = (bf16[1,2560,8]{1,2,0:T(8,128)(2,1)S(1)}, bf16[1,2560,8]{1,2,0:T(8,128)(2,1)}, u32[]{:S(2)}) copy-start(bf16[1,2560,8]{1,2,0:T(8,128)(2,1)} %param.20) | copy-start | bytes 122884
  351.8 3.5 slice-start.1
Sparse Core Ops, SparseCore 0:
  10.8 167.5 all-gather.2

commit v14 on v12

--- a/solution.py
+++ b/solution.py
@@ -32,10 +32,10 @@
     own_quarter = jnp.dot(own_hidden, own_units_down, preferred_element_type=jnp.float32).astype(
         jnp.bfloat16
     )
+    own_quarter, other_hidden = lax.optimization_barrier((own_quarter, other_hidden))
     other_quarter = jnp.dot(
         other_hidden, other_units_down, preferred_element_type=jnp.float32
     ).astype(jnp.bfloat16)
-    own_quarter, other_quarter = lax.optimization_barrier((own_quarter, other_quarter))
     return (own_quarter.astype(jnp.float32) + other_quarter.astype(jnp.float32)).astype(
         jnp.bfloat16
     )

time: 349 us -> 348 us (level)
  other arithmetic: 14.9 us -> 10.3 us
    convert_element_type x1 -> x0, other arithmetic: 3.94 us -> none  [expert_half(): (own_quarter.astype(jnp.float32) + other_quarter.astype(jnp.float32)).ast...]
  transfers between devices with their start and end apart: 6 -> 6, of which waited for: 5 -> 4; matrix products, arithmetic and copies ran while one was open for 9% -> 9% of each run, Pallas kernels for 0% -> 0%
where the time goes in v14:
time: 348 us; the launch traced here: 347 us
  waiting for transfers between devices  242 us (70%)
  matrix products  35.8 us (10%)
  starting transfers between devices  30.8 us (9%)
  between operations  13.7 us (4%)
  other arithmetic  10.3 us (3%)
  local copies, waits for them, and re-layouts  9.13 us (3%)
  blocking collectives  5.59 us (2%)
    all_gather x1, waiting for transfers between devices, on_device(): packed_all = lax.all_gather(packed, PG_AXES, axis=0, tiled=False)  131 us
    all_to_all x1, waiting for transfers between devices, on_device(): lax.all_to_all(half_out.reshape(pg_size, slot_cap, half_width), PG_AXES,...  108 us
    all_to_all x1, starting transfers between devices, on_device(): lax.all_to_all(outbox, PG_AXES, split_axis=0, concat_axis=0, tiled=True)  16.1 us
    all_to_all x1, starting transfers between devices, on_device(): lax.all_to_all(half_out.reshape(pg_size, slot_cap, half_width), PG_AXES,...  14.5 us
  transfers between devices with their start and end apart: 6, of which 4 were waited for; matrix products, arithmetic and copies ran while one was open for 9% of the time, Pallas kernels for 0%

profile of v14, /device:TPU:2, one launch (start us, length us, event | category | flops | bytes accessed | tf_op | source)
XLA Modules:
  0.0 346.9 jit_solution(657053111146424882)
XLA Ops:
  6.6 0.8 copy-done
  7.3 1.3 pad_maximum_fusion
  8.7 0.0 all-gather.3.cloned.1.call-update
  8.7 1.2 convert_element_type.73
  9.9 1.8 multiply_reduce_fusion
  11.7 0.8 copy.37
  12.5 0.1 eq.98
  12.6 0.4 fusion.23
  13.0 0.1 convert_element_type.68
  13.2 0.1 copy.38
  13.2 0.0 copy-done.9
  13.3 0.1 dynamic-slice.5
  13.3 1.7 convert_reduce_fusion
  15.0 4.0 %convolution_convert_fusion.2 = bf16[2048,1280]{1,0:T(8,128)(2,1)} fusion(f32[2048,128]{1,0:T(8,128)S(1)} %get-tuple-element.34, f32[2048,128]{1,0:T(8,128)S(1)} %get-tuple-element.33, f32[128,2560]{1,0:T(8,128)S(1)} %convert_element_type.73, s32[]{:T(128)S(6)} %select_n.27, f32[1280]{0:T(1024)S(1)} %dynamic-slice.5, f32[128]{0:T(128)S(1)} %add_rsqrt_fusion), kind=kOutput, calls=%fused_computation.3 | convolution fusion | flops 674725888 | bytes 8004100 | tf_op jit(solution)/shard_map/dot_general | solution.py:78
  19.0 16.1 %all-to-all-start = ((bf16[128,16,1280]{2,1,0:T(8,128)(2,1)}), bf16[128,16,1280]{2,1,0:T(8,128)(2,1)}, u32[]{:S(2)}, u32[]{:S(2)}) async-start(bf16[128,16,1280]{2,1,0:T(8,128)(2,1)} %bitcast.55), calls=%async_computation | async-start | bytes 10485760 | tf_op jit(solution)/shard_map/all_to_all | solution.py:133
  35.1 0.0 copy-done.5
  35.1 0.0 copy-start.2
  35.1 1.1 dynamic-slice_bitcast_fusion
  36.2 0.0 collective-permute-start
  36.2 1.3 copy-done.2
  37.6 2.8 constant_dynamic-slice_fusion
  40.3 1.8 copy_bitcast_fusion
  42.1 0.0 collective-permute-done
  42.1 130.9 %all-gather.3.cloned.1.call-done = bf16[2048,1280]{1,0:T(8,128)(2,1)} async-done(((bf16[16,1280]{1,0:T(8,128)(2,1)}), bf16[2048,1280]{1,0:T(8,128)(2,1)}) %all-gather.3.cloned.1.call-update) | async-done | bytes 5242896 | tf_op jit(solution)/shard_map/all_gather | solution.py:134
  173.0 0.0 all-to-all-done
  173.0 0.0 collective-permute-start.1
  173.0 6.4 %fusion.35 = f32[2048,2,384]{2,0,1:T(8,128)S(1)} fusion(bf16[2048,1280,1]{1,0,2:T(8,128)(2,1)} %bitcast.10, bf16[1280,2,384]{2,0,1:T(8,128)(2,1)S(1)} %get-tuple-element.16), kind=kOutput, calls=%fused_computation.63 | convolution fusion | flops 4026531840 | bytes 13500416 | tf_op jit(solution)/shard_map/rd,dgf->rgf/dot_general | solution.py:23
  179.4 2.5 collective-permute-done.1
  181.9 4.4 %fusion = f32[2048,2,384]{2,0,1:T(8,128)S(1)} fusion(bf16[1280,2,384]{2,0,1:T(8,128)(2,1)S(1)} %copy-done.6, bf16[2048,1280]{1,0:T(8,128)(2,1)S(1)} %collective-permute-done.1), kind=kOutput, calls=%fused_computation.12 | convolution fusion | flops 4026531840 | bytes 13500416 | tf_op jit(solution)/shard_map/rd,dgf->rgf/dot_general | solution.py:27
  186.3 0.6 add.62
  186.9 0.9 fusion.3
  187.8 0.2 collective-permute-start.2
  188.0 0.1 copy-done.7
  188.1 3.0 convolution_convert_fusion.1
  191.2 0.1 collective-permute-done.2
  191.3 5.8 %add_convert_fusion = bf16[2048,1280]{1,0:T(8,128)(2,1)} fusion(bf16[2048,1280]{1,0:T(8,128)(2,1)S(1)} %convolution_convert_fusion.1, bf16[2048,384]{1,0:T(8,128)(2,1)S(1)} %collective-permute-done.2, bf16[384,1280]{1,0:T(8,128)(2,1)} %collective-permute-done), kind=kOutput, calls=%fused_computation | convolution fusion | flops 2026373120 | bytes 13041664 | tf_op jit(solution)/shard_map/dot_general | solution.py:36
  197.1 14.5 %all-to-all-start.1 = ((bf16[128,16,1280]{2,1,0:T(8,128)(2,1)}), bf16[128,16,1280]{2,1,0:T(8,128)(2,1)}, u32[]{:S(2)}, u32[]{:S(2)}) async-start(bf16[128,16,1280]{2,1,0:T(8,128)(2,1)} %bitcast.56), calls=%async_computation.1 | async-start | bytes 10485760 | tf_op jit(solution)/shard_map/all_to_all | solution.py:138
  211.6 0.2 select_reduce_fusion.2
  211.8 0.1 broadcast_compare_fusion
  211.9 2.5 select_reduce_fusion
  214.4 3.5 %fusion.19 = f32[128,128,8]{0,2,1:T(8,128)} fusion(bf16[128,16,1280]{2,1,0:T(8,128)(2,1)} %bitcast.58, f32[128,2560]{1,0:T(8,128)S(1)} %copy-done.4, s32[]{:T(128)S(6)} %select_n.27, f32[1280]{0:T(1024)S(1)} %dynamic-slice.5, f32[128]{0:T(128)S(1)} %add_rsqrt_fusion), kind=kOutput, calls=%fused_computation.32 | convolution fusion | flops 336035840 | bytes 3809796 | tf_op jit(solution)/shard_map/dot_general | solution.py:157
  217.9 5.6 %all-reduce.1 = bf16[128,128,8]{0,2,1:T(8,128)(2,1)S(1)} all-reduce(f32[128,128,8]{0,2,1:T(8,128)} %fusion.19), channel_id=1, replica_groups=mesh['kv'=2,'px'=4,'pz'=8,'py'=4] {'kv'}, use_global_device_ids=true, to_apply=%region_7.8 | all-reduce | flops 131072 | bytes 786432 | tf_op jit(solution)/shard_map/psum | solution.py:160
  223.5 108.1 %all-to-all-done.1 = bf16[128,16,1280]{2,1,0:T(8,128)(2,1)} async-done(((bf16[128,16,1280]{2,1,0:T(8,128)(2,1)}), bf16[128,16,1280]{2,1,0:T(8,128)(2,1)}, u32[]{:S(2)}, u32[]{:S(2)}) %all-to-all-start.1) | async-done | bytes 5242912 | tf_op jit(solution)/shard_map/all_to_all | solution.py:138
  331.6 3.6 %fusion.27 = f32[128,1280]{1,0:T(8,128)S(1)} fusion(bf16[2048,1280]{1,0:T(8,128)(2,1)} %bitcast.15, f32[128,2048]{1,0:T(8,128)S(1)} %get-tuple-element.26, f32[128,2048]{1,0:T(8,128)S(1)} %get-tuple-element.25), kind=kOutput, calls=%fused_computation.45 | convolution fusion | flops 671612928 | bytes 7995392 | tf_op jit(solution)/shard_map/dot_general | solution.py:94
  335.2 0.0 slice-start.1
  335.2 0.0 copy-start.1
  335.2 3.5 %convolution_add_fusion = f32[128,1280]{1,0:T(8,128)S(1)} fusion(f32[128,1280]{1,0:T(8,128)S(1)} %fusion.27, bf16[2048,1280]{1,0:T(8,128)(2,1)} %bitcast.15, f32[128,2048]{1,0:T(8,128)S(1)} %get-tuple-element.26, f32[128,2048]{1,0:T(8,128)S(1)} %get-tuple-element.25), kind=kOutput, calls=%fused_computation.23 | convolution fusion | flops 672563200 | bytes 8650752 | tf_op jit(solution)/shard_map/dot_general | solution.py:94
  338.8 1.3 fusion.15
  (30 shorter events, 0.1 us)
Async XLA Ops:
  6.5 0.8 copy-start
  6.5 6.7 %copy-start.8 = (s32[128,6]{0,1:T(8,128)S(1)}, s32[128,6]{0,1:T(8,128)}, u32[]{:S(2)}) copy-start(s32[128,6]{0,1:T(8,128)} %param.13) | copy-start | bytes 9220
  6.5 6.7 %copy-start.9 = (f32[2560]{0:T(1024)S(1)}, f32[2560]{0:T(1024)}, u32[]{:S(2)}) copy-start(f32[2560]{0:T(1024)} %param.12) | copy-start | bytes 30724
  6.5 166.5 %all-gather.3.cloned.1.call-start = ((), (), s32[]{:S(2)}) async-start(), calls=%async_computation.2 | async-start | bytes 5283840 | tf_op jit(solution)/shard_map/all_gather | solution.py:134
  9.9 9.1 %copy-start.3 = (f32[128,2560]{1,0:T(8,128)}, f32[128,2560]{1,0:T(8,128)S(1)}, u32[]{:S(2)}) copy-start(f32[128,2560]{1,0:T(8,128)S(1)} %convert_element_type.73) | copy-start | bytes 3932164
  19.0 16.1 %copy-start.5 = (bf16[1,384,2560]{2,1,0:T(8,128)(2,1)S(1)}, bf16[1,384,2560]{2,1,0:T(8,128)(2,1)}, u32[]{:S(2)}) copy-start(bf16[1,384,2560]{2,1,0:T(8,128)(2,1)} %param.19) | copy-start | bytes 5898244
  19.0 154.0 %all-to-all-start = ((bf16[128,16,1280]{2,1,0:T(8,128)(2,1)}), bf16[128,16,1280]{2,1,0:T(8,128)(2,1)}, u32[]{:S(2)}, u32[]{:S(2)}) async-start(bf16[128,16,1280]{2,1,0:T(8,128)(2,1)} %bitcast.55), calls=%async_computation | async-start | bytes 10485760 | tf_op jit(solution)/shard_map/all_to_all | solution.py:133
  35.1 2.5 copy-start.2
  36.2 5.9 %collective-permute-start = (bf16[384,1280]{1,0:T(8,128)(2,1)S(1)}, bf16[384,1280]{1,0:T(8,128)(2,1)}, u32[]{:S(2)}, u32[]{:S(2)}) collective-permute-start(bf16[384,1280]{1,0:T(8,128)(2,1)S(1)} %get-tuple-element.31), channel_id=1, source_target_pairs={{0,128},{128,0},{1,129},{129,1},{2,130},{130,2},{3,131},{131,3},{4... | collective-permute-start | bytes 2949128 | tf_op jit(solution)/shard_map/ppermute | solution.py:17
  173.0 8.9 %collective-permute-start.1 = (bf16[2048,1280]{1,0:T(8,128)(2,1)}, bf16[2048,1280]{1,0:T(8,128)(2,1)S(1)}, u32[]{:S(2)}, u32[]{:S(2)}) collective-permute-start(bf16[2048,1280]{1,0:T(8,128)(2,1)} %bitcast.9), channel_id=1, source_target_pairs={{0,128},{128,0},{1,129},{129,1},{2,130},{130,2},{3,131},{131,3},{4... | collective-permute-start | bytes 15728648 | tf_op jit(solution)/shard_map/ppermute | solution.py:17
  173.0 8.9 %copy-start.6 = (bf16[1280,2,384]{2,0,1:T(8,128)(2,1)S(1)}, bf16[1280,2,384]{2,0,1:T(8,128)(2,1)}, u32[]{:S(2)}) copy-start(bf16[1280,2,384]{2,0,1:T(8,128)(2,1)} %get-tuple-element.19) | copy-start | bytes 5898244
  186.9 1.2 copy-start.7
  187.8 3.5 %collective-permute-start.2 = (bf16[2048,384]{1,0:T(8,128)(2,1)S(1)}, bf16[2048,384]{1,0:T(8,128)(2,1)S(1)}, u32[]{:S(2)}, u32[]{:S(2)}) collective-permute-start(bf16[2048,384]{1,0:T(8,128)(2,1)S(1)} %fusion.3), channel_id=1, source_target_pairs={{0,128},{128,0},{1,129},{129,1},{2,130},{130,2},{3,131},{131,3},{4... | collective-permute-start | bytes 4718600 | tf_op jit(solution)/shard_map/ppermute | solution.py:17
  197.1 14.5 %copy-start.11 = (s32[256]{0:T(256)S(1)}, s32[256]{0:T(256)}, u32[]{:S(2)}) copy-start(s32[256]{0:T(256)} %param.16) | copy-start | bytes 3076
  197.1 14.5 %copy-start.13 = (s32[128]{0:T(128)S(1)}, s32[128]{0:T(128)}, u32[]{:S(2)}) copy-start(s32[128]{0:T(128)} %param.15) | copy-start | bytes 1540
  197.1 14.7 %copy-start.12 = (s32[128]{0:T(128)S(1)}, s32[128]{0:T(128)}, u32[]{:S(2)}) copy-start(s32[128]{0:T(128)} %param.17) | copy-start | bytes 1540
  197.1 14.8 %copy-start.10 = (f32[128,6]{0,1:T(8,128)S(1)}, f32[128,6]{0,1:T(8,128)}, u32[]{:S(2)}) copy-start(f32[128,6]{0,1:T(8,128)} %param.14) | copy-start | bytes 9220
  197.1 17.3 %copy-start.4 = (f32[128,2560]{1,0:T(8,128)S(1)}, f32[128,2560]{1,0:T(8,128)}, u32[]{:S(2)}) copy-start(f32[128,2560]{1,0:T(8,128)} %copy-done.3) | copy-start | bytes 3932164
  197.1 134.5 %all-to-all-start.1 = ((bf16[128,16,1280]{2,1,0:T(8,128)(2,1)}), bf16[128,16,1280]{2,1,0:T(8,128)(2,1)}, u32[]{:S(2)}, u32[]{:S(2)}) async-start(bf16[128,16,1280]{2,1,0:T(8,128)(2,1)} %bitcast.56), calls=%async_computation.1 | async-start | bytes 10485760 | tf_op jit(solution)/shard_map/all_to_all | solution.py:138
  331.6 7.1 %slice-start = ((s8[5242880]{0:T(1024)(128)(4,1)}), s8[4194304]{0:T(1024)(128)(4,1)S(1)}, s32[]{:S(2)}) async-start(s8[5242880]{0:T(1024)(128)(4,1)} %bitcast.59), calls=%async_computation.3 | async-start | bytes 8388608
  335.2 3.6 %slice-start.1 = ((s8[5242880]{0:T(1024)(128)(4,1)}), s8[1048576]{0:T(1024)(128)(4,1)S(1)}, s32[]{:S(2)}) async-start(s8[5242880]{0:T(1024)(128)(4,1)} %bitcast.59), calls=%async_computation.4 | async-start | bytes 2097152
  335.2 4.9 %copy-start.1 = (bf16[1,2560,8]{1,2,0:T(8,128)(2,1)S(1)}, bf16[1,2560,8]{1,2,0:T(8,128)(2,1)}, u32[]{:S(2)}) copy-start(bf16[1,2560,8]{1,2,0:T(8,128)(2,1)} %param.20) | copy-start | bytes 122884
Sparse Core Ops, SparseCore 0:
  10.8 162.1 all-gather.2

commit v15 on v12

--- a/solution.py
+++ b/solution.py
@@ -91,9 +91,13 @@
         )
     upper_part = combine.astype(jnp.bfloat16)
     lower_part = (combine - upper_part.astype(jnp.float32)).astype(jnp.bfloat16)
-    return jnp.dot(upper_part, gathered, preferred_element_type=jnp.float32) + jnp.dot(
-        lower_part, gathered, preferred_element_type=jnp.float32
+    token_count = weights.shape[0]
+    both = jnp.dot(
+        jnp.concatenate([upper_part, lower_part], axis=0),
+        gathered,
+        preferred_element_type=jnp.float32,
     )
+    return both[:token_count] + both[token_count:]
 
 
 def on_device(

time: 349 us -> 347 us (level)
    dot_general x2 -> x1, matrix products: 7.08 us -> 4.03 us  [collect_rows(): jnp.dot(jnp.concatenate([upper_part, lower_part], axis=0), gathered, pref...]
  transfers between devices with their start and end apart: 6 -> 6, of which waited for: 5 -> 4; matrix products, arithmetic and copies ran while one was open for 9% -> 9% of each run, Pallas kernels for 0% -> 0%
where the time goes in v15:
time: 347 us
  waiting for transfers between devices  243 us (70%)
  matrix products  32.1 us (9%)
  starting transfers between devices  29.9 us (9%)
  other arithmetic  14.4 us (4%)
  between operations  13.7 us (4%)
  local copies, waits for them, and re-layouts  9.13 us (3%)
  blocking collectives  4.83 us (1%)
    all_gather x1, waiting for transfers between devices, on_device(): packed_all = lax.all_gather(packed, PG_AXES, axis=0, tiled=False)  130 us
    all_to_all x1, waiting for transfers between devices, on_device(): lax.all_to_all(half_out.reshape(pg_size, slot_cap, half_width), PG_AXES,...  109 us
    all_to_all x1, starting transfers between devices, on_device(): lax.all_to_all(outbox, PG_AXES, split_axis=0, concat_axis=0, tiled=True)  16.1 us
    all_to_all x1, starting transfers between devices, on_device(): lax.all_to_all(half_out.reshape(pg_size, slot_cap, half_width), PG_AXES,...  13.6 us
  transfers between devices with their start and end apart: 6, of which 4 were waited for; matrix products, arithmetic and copies ran while one was open for 9% of the time, Pallas kernels for 0%

profile of v15, /device:TPU:2, one launch (start us, length us, event | category | flops | bytes accessed | tf_op | source)
XLA Modules:
  0.0 346.6 jit_solution(17309336993688214220)
XLA Ops:
  6.6 0.8 copy-done
  7.3 1.3 pad_maximum_fusion
  8.7 0.0 all-gather.3.cloned.1.call-update
  8.7 1.2 convert_element_type.75
  9.9 1.8 multiply_reduce_fusion
  11.7 0.8 copy.37
  12.5 0.1 eq.98
  12.6 0.4 fusion.23
  13.0 0.1 convert_element_type.68
  13.2 0.1 copy.38
  13.2 0.0 copy-done.9
  13.3 0.1 dynamic-slice.5
  13.3 1.7 convert_reduce_fusion
  15.0 4.0 %convolution_convert_fusion.2 = bf16[2048,1280]{1,0:T(8,128)(2,1)} fusion(f32[2048,128]{1,0:T(8,128)S(1)} %get-tuple-element.36, f32[2048,128]{1,0:T(8,128)S(1)} %get-tuple-element.35, f32[128,2560]{1,0:T(8,128)S(1)} %convert_element_type.75, s32[]{:T(128)S(6)} %select_n.27, f32[1280]{0:T(1024)S(1)} %dynamic-slice.5, f32[128]{0:T(128)S(1)} %add_rsqrt_fusion), kind=kOutput, calls=%fused_computation.3 | convolution fusion | flops 674725888 | bytes 8004100 | tf_op jit(solution)/shard_map/dot_general | solution.py:78
  19.0 0.0 copy-done.3
  19.0 16.1 %all-to-all-start = ((bf16[128,16,1280]{2,1,0:T(8,128)(2,1)}), bf16[128,16,1280]{2,1,0:T(8,128)(2,1)}, u32[]{:S(2)}, u32[]{:S(2)}) async-start(bf16[128,16,1280]{2,1,0:T(8,128)(2,1)} %bitcast.54), calls=%async_computation | async-start | bytes 10485760 | tf_op jit(solution)/shard_map/all_to_all | solution.py:137
  35.1 0.0 copy-start.2
  35.1 1.1 dynamic-slice_bitcast_fusion
  36.2 0.0 collective-permute-start
  36.2 1.4 copy-done.2
  37.6 2.8 constant_dynamic-slice_fusion
  40.3 1.8 copy_bitcast_fusion
  42.1 0.0 collective-permute-done
  42.1 130.4 %all-gather.3.cloned.1.call-done = bf16[2048,1280]{1,0:T(8,128)(2,1)} async-done(((bf16[16,1280]{1,0:T(8,128)(2,1)}), bf16[2048,1280]{1,0:T(8,128)(2,1)}) %all-gather.3.cloned.1.call-update) | async-done | bytes 5242896 | tf_op jit(solution)/shard_map/all_gather | solution.py:138
  172.6 0.0 all-to-all-done
  172.6 0.0 collective-permute-start.1
  172.6 6.4 %fusion.38 = f32[2048,2,384]{2,0,1:T(8,128)S(1)} fusion(bf16[2048,1280,1]{1,0,2:T(8,128)(2,1)} %bitcast.10, bf16[1280,2,384]{2,0,1:T(8,128)(2,1)S(1)} %get-tuple-element.16), kind=kOutput, calls=%fused_computation.66 | convolution fusion | flops 4026531840 | bytes 13500416 | tf_op jit(solution)/shard_map/rd,dgf->rgf/dot_general | solution.py:23
  178.9 2.5 collective-permute-done.1
  181.4 4.4 %fusion = f32[2048,2,384]{2,0,1:T(8,128)S(1)} fusion(bf16[1280,2,384]{2,0,1:T(8,128)(2,1)S(1)} %copy-done.6, bf16[2048,1280]{1,0:T(8,128)(2,1)S(1)} %collective-permute-done.1), kind=kOutput, calls=%fused_computation.12 | convolution fusion | flops 4026531840 | bytes 13500416 | tf_op jit(solution)/shard_map/rd,dgf->rgf/dot_general | solution.py:27
  185.8 0.6 add.62
  186.5 0.0 copy-start.7
  186.5 0.9 fusion.3
  187.3 0.2 collective-permute-start.2
  187.6 0.1 copy-done.7
  187.7 3.0 convolution_convert_fusion.1
  190.7 0.1 collective-permute-done.2
  190.8 4.3 %convolution_convert_fusion = bf16[2048,1280]{1,0:T(8,128)(2,1)S(1)} fusion(bf16[2048,384]{1,0:T(8,128)(2,1)S(1)} %collective-permute-done.2, bf16[384,1280]{1,0:T(8,128)(2,1)} %collective-permute-done), kind=kOutput, calls=%fused_computation.1 | convolution fusion | flops 2015887360 | bytes 7798784 | tf_op jit(solution)/shard_map/dot_general | solution.py:35
  195.1 3.9 %add_convert_fusion = bf16[2048,1280]{1,0:T(8,128)(2,1)} fusion(bf16[2048,1280]{1,0:T(8,128)(2,1)S(1)} %convolution_convert_fusion, bf16[2048,1280]{1,0:T(8,128)(2,1)S(1)} %convolution_convert_fusion.1), kind=kLoop, calls=%fused_computation | loop fusion | flops 10485760 | bytes 15728640 | tf_op jit(solution)/shard_map/convert_element_type | solution.py:39
  199.1 13.6 %all-to-all-start.1 = ((bf16[128,16,1280]{2,1,0:T(8,128)(2,1)}), bf16[128,16,1280]{2,1,0:T(8,128)(2,1)}, u32[]{:S(2)}, u32[]{:S(2)}) async-start(bf16[128,16,1280]{2,1,0:T(8,128)(2,1)} %bitcast.55), calls=%async_computation.1 | async-start | bytes 10485760 | tf_op jit(solution)/shard_map/all_to_all | solution.py:142
  212.7 0.2 select_reduce_fusion.2
  212.9 0.1 broadcast_compare_fusion
  213.0 2.5 select_reduce_fusion
  215.5 0.2 add_convert_fusion.3
  215.7 2.7 fusion.19
  218.4 4.8 %all-reduce.1 = bf16[128,128,8]{0,2,1:T(8,128)(2,1)S(1)} all-reduce(f32[128,128,8]{0,2,1:T(8,128)S(1)} %fusion.19), channel_id=1, replica_groups=mesh['kv'=2,'px'=4,'pz'=8,'py'=4] {'kv'}, use_global_device_ids=true, to_apply=%region_7.8 | all-reduce | flops 131072 | bytes 786432 | tf_op jit(solution)/shard_map/psum | solution.py:164
  223.2 109.5 %all-to-all-done.1 = bf16[128,16,1280]{2,1,0:T(8,128)(2,1)} async-done(((bf16[128,16,1280]{2,1,0:T(8,128)(2,1)}), bf16[128,16,1280]{2,1,0:T(8,128)(2,1)}, u32[]{:S(2)}, u32[]{:S(2)}) %all-to-all-start.1) | async-done | bytes 5242912 | tf_op jit(solution)/shard_map/all_to_all | solution.py:142
  332.7 4.0 %fusion.24 = f32[256,1280]{1,0:T(8,128)S(1)} fusion(bf16[2048,1280]{1,0:T(8,128)(2,1)} %bitcast.15, bf16[128,2048]{1,0:T(8,128)(2,1)S(1)} %get-tuple-element.32, bf16[128,2048]{1,0:T(8,128)(2,1)S(1)} %get-tuple-element.31), kind=kOutput, calls=%fused_computation.34 | convolution fusion | flops 1344274432 | bytes 7602176 | tf_op jit(solution)/shard_map/dot_general | solution.py:95
  336.7 3.0 fusion.15
  (26 shorter events, 0.1 us)
Async XLA Ops:
  6.5 0.8 copy-start
  6.5 6.7 %copy-start.8 = (s32[128,6]{0,1:T(8,128)S(1)}, s32[128,6]{0,1:T(8,128)}, u32[]{:S(2)}) copy-start(s32[128,6]{0,1:T(8,128)} %param.13) | copy-start | bytes 9220
  6.5 6.7 %copy-start.9 = (f32[2560]{0:T(1024)S(1)}, f32[2560]{0:T(1024)}, u32[]{:S(2)}) copy-start(f32[2560]{0:T(1024)} %param.12) | copy-start | bytes 30724
  6.5 166.0 %all-gather.3.cloned.1.call-start = ((), (), s32[]{:S(2)}) async-start(), calls=%async_computation.2 | async-start | bytes 5283840 | tf_op jit(solution)/shard_map/all_gather | solution.py:138
  9.9 9.1 %copy-start.3 = (f32[128,2560]{1,0:T(8,128)}, f32[128,2560]{1,0:T(8,128)S(1)}, u32[]{:S(2)}) copy-start(f32[128,2560]{1,0:T(8,128)S(1)} %convert_element_type.75) | copy-start | bytes 3932164
  19.0 16.1 %copy-start.5 = (bf16[1,384,2560]{2,1,0:T(8,128)(2,1)S(1)}, bf16[1,384,2560]{2,1,0:T(8,128)(2,1)}, u32[]{:S(2)}) copy-start(bf16[1,384,2560]{2,1,0:T(8,128)(2,1)} %param.19) | copy-start | bytes 5898244
  19.0 153.6 %all-to-all-start = ((bf16[128,16,1280]{2,1,0:T(8,128)(2,1)}), bf16[128,16,1280]{2,1,0:T(8,128)(2,1)}, u32[]{:S(2)}, u32[]{:S(2)}) async-start(bf16[128,16,1280]{2,1,0:T(8,128)(2,1)} %bitcast.54), calls=%async_computation | async-start | bytes 10485760 | tf_op jit(solution)/shard_map/all_to_all | solution.py:137
  35.1 2.5 copy-start.2
  36.2 5.9 %collective-permute-start = (bf16[384,1280]{1,0:T(8,128)(2,1)S(1)}, bf16[384,1280]{1,0:T(8,128)(2,1)}, u32[]{:S(2)}, u32[]{:S(2)}) collective-permute-start(bf16[384,1280]{1,0:T(8,128)(2,1)S(1)} %get-tuple-element.33), channel_id=1, source_target_pairs={{0,128},{128,0},{1,129},{129,1},{2,130},{130,2},{3,131},{131,3},{4... | collective-permute-start | bytes 2949128 | tf_op jit(solution)/shard_map/ppermute | solution.py:17
  172.6 8.9 %collective-permute-start.1 = (bf16[2048,1280]{1,0:T(8,128)(2,1)}, bf16[2048,1280]{1,0:T(8,128)(2,1)S(1)}, u32[]{:S(2)}, u32[]{:S(2)}) collective-permute-start(bf16[2048,1280]{1,0:T(8,128)(2,1)} %bitcast.9), channel_id=1, source_target_pairs={{0,128},{128,0},{1,129},{129,1},{2,130},{130,2},{3,131},{131,3},{4... | collective-permute-start | bytes 15728648 | tf_op jit(solution)/shard_map/ppermute | solution.py:17
  172.6 8.9 %copy-start.6 = (bf16[1280,2,384]{2,0,1:T(8,128)(2,1)S(1)}, bf16[1280,2,384]{2,0,1:T(8,128)(2,1)}, u32[]{:S(2)}) copy-start(bf16[1280,2,384]{2,0,1:T(8,128)(2,1)} %get-tuple-element.19) | copy-start | bytes 5898244
  186.5 1.2 copy-start.7
  187.3 3.5 %collective-permute-start.2 = (bf16[2048,384]{1,0:T(8,128)(2,1)S(1)}, bf16[2048,384]{1,0:T(8,128)(2,1)S(1)}, u32[]{:S(2)}, u32[]{:S(2)}) collective-permute-start(bf16[2048,384]{1,0:T(8,128)(2,1)S(1)} %fusion.3), channel_id=1, source_target_pairs={{0,128},{128,0},{1,129},{129,1},{2,130},{130,2},{3,131},{131,3},{4... | collective-permute-start | bytes 4718600 | tf_op jit(solution)/shard_map/ppermute | solution.py:17
  199.1 13.6 %copy-start.11 = (s32[256]{0:T(256)S(1)}, s32[256]{0:T(256)}, u32[]{:S(2)}) copy-start(s32[256]{0:T(256)} %param.16) | copy-start | bytes 3076
  199.1 13.6 %copy-start.13 = (s32[128]{0:T(128)S(1)}, s32[128]{0:T(128)}, u32[]{:S(2)}) copy-start(s32[128]{0:T(128)} %param.15) | copy-start | bytes 1540
  199.1 13.8 %copy-start.12 = (s32[128]{0:T(128)S(1)}, s32[128]{0:T(128)}, u32[]{:S(2)}) copy-start(s32[128]{0:T(128)} %param.17) | copy-start | bytes 1540
  199.1 13.9 %copy-start.10 = (f32[128,6]{0,1:T(8,128)S(1)}, f32[128,6]{0,1:T(8,128)}, u32[]{:S(2)}) copy-start(f32[128,6]{0,1:T(8,128)} %param.14) | copy-start | bytes 9220
  199.1 133.6 %all-to-all-start.1 = ((bf16[128,16,1280]{2,1,0:T(8,128)(2,1)}), bf16[128,16,1280]{2,1,0:T(8,128)(2,1)}, u32[]{:S(2)}, u32[]{:S(2)}) async-start(bf16[128,16,1280]{2,1,0:T(8,128)(2,1)} %bitcast.55), calls=%async_computation.1 | async-start | bytes 10485760 | tf_op jit(solution)/shard_map/all_to_all | solution.py:142
  212.7 3.0 copy-start.4
  332.7 7.1 %copy-start.1 = (bf16[1,2560,8]{1,2,0:T(8,128)(2,1)S(1)}, bf16[1,2560,8]{1,2,0:T(8,128)(2,1)}, u32[]{:S(2)}) copy-start(bf16[1,2560,8]{1,2,0:T(8,128)(2,1)} %param.20) | copy-start | bytes 122884
Sparse Core Ops, SparseCore 0:
  10.8 161.6 all-gather.2
